TPU v7x, 32 devices: a whole 2x2x4 slice. The times are simulated.
32 devices in a mesh: clips: 2 (over y), tm: 4 (over z), height: 4 (over x, core).
Axes of the slice: x: 2, y: 2, z: 4, core: 2. Of those that a mesh axis runs over, the one named last changes fastest.
Arguments:
- clip_frames: bfloat16 [32, 32, 16, 192], P(('clips', 'tm'), 'height'), parts along dimension 0, may hold values from -6 to 6
- w_first: bfloat16 [3, 3, 3, 192, 192], replicated, may hold values from -0.078125 to 0.078125
- b_first: float32 [192], replicated, may hold values from -3 to 3
- w_second: bfloat16 [3, 3, 3, 192, 192], replicated, may hold values from -0.078125 to 0.078125
- b_second: float32 [192], replicated, may hold values from -3 to 3
Outputs:
- block_out: bfloat16 [32, 32, 16, 192], P(('clips', 'tm'), 'height'), parts along dimension 0
There are 2 independent parts, one for each index of `clips`. A program takes and returns all parts, laid end to end along the dimension named above; an argument that names none is the same for every part. Nothing has to cross between parts.
All inputs are finite; a program needn't handle non-finite values.
Results may differ from a plain program's by a relative error of at most 0.003.
Values may be sent and summed in bfloat16 or wider, within the bound.
No kernel may reach another device: no remote copies, remote signals or barrier semaphores. Data moves between devices by JAX's collectives and lax.ppermute only.
A program may use at most 64 MiB of HBM per device.

v0:
```python
import jax
import jax.numpy as jnp
from jax import lax
from jax.sharding import PartitionSpec as P


def shifted(value, axis, steps):
    count = lax.axis_size(axis)
    leading, last = (max(0, -steps), min(count, count - steps))
    return lax.ppermute(value, axis, [(source, source + steps) for source in range(leading, last)])


def with_halo(value, sides, width):
    for axis, dim in sides:
        peers, length = (lax.axis_size(axis), value.shape[dim])
        up = [(i, (i + 1) % peers) for i in range(peers - 1)]
        down = [(j, i) for i, j in up]
        last = lax.slice_in_dim(value, length - width, length, axis=dim)
        leading = lax.slice_in_dim(value, 0, width, axis=dim)
        before = lax.ppermute(last, axis, up)
        after = lax.ppermute(leading, axis, down)
        value = jnp.concatenate([before, value, after], axis=dim)
    return value


def conv_valid(padded, weight):
    frame_count = padded.shape[0] - 2
    row_count = padded.shape[1] - 2
    col_count = padded.shape[2] - 2
    chans = weight.shape[3]
    summed = jnp.zeros((frame_count * row_count * col_count, weight.shape[4]), jnp.float32)
    for tap_time in range(3):
        stacked = jnp.concatenate(
            [
                padded[
                    tap_time : tap_time + frame_count,
                    tap_row : tap_row + row_count,
                    tap_col : tap_col + col_count,
                ]
                for tap_row in range(3)
                for tap_col in range(3)
            ],
            -1,
        )
        stacked = stacked.reshape(-1, 9 * chans)
        kernel = weight[tap_time].reshape(9 * chans, weight.shape[4])
        summed = summed + jnp.dot(stacked, kernel, preferred_element_type=jnp.float32)
    return summed.reshape(frame_count, row_count, col_count, weight.shape[4])


def pad_columns(field):
    return jnp.pad(field, ((0, 0), (0, 0), (1, 1), (0, 0)))


def context(field):
    last_frames = field[field.shape[0] - 2 :]
    earlier = shifted(last_frames, "tm", 1)
    extended = jnp.concatenate([earlier, field], 0)
    extended = with_halo(extended, (("height", 1),), 1)
    return pad_columns(extended)


def local(clip_frames, w_first, b_first, w_second, b_second):
    activated = jax.nn.silu(clip_frames.astype(jnp.float32)).astype(jnp.bfloat16)
    hidden = conv_valid(context(activated), w_first) + b_first
    gated = jax.nn.silu(hidden).astype(jnp.bfloat16)
    second = conv_valid(context(gated), w_second)
    return (clip_frames.astype(jnp.float32) + second + b_second).astype(jnp.bfloat16)


def solution(mesh):
    return jax.shard_map(
        local,
        mesh=mesh,
        in_specs=(P(("clips", "tm"), "height", None, None), P(), P(), P(), P()),
        out_specs=P(("clips", "tm"), "height", None, None),
        check_vma=False,
    )
```

profile of v0, /device:TPU:1, one launch (start us, length us, event | category | flops | bytes accessed | tf_op | source)
XLA Modules:
  0.0 68.7 jit_solution(13731439555836463821)
XLA Ops:
  1.1 4.0 %collective-permute-start = (bf16[2,8,16,192]{3,2,1,0:T(8,128)(2,1)S(1)}, bf16[2,8,16,192]{3,2,1,0:T(8,128)(2,1)S(1)}, u32[]{:S(2)}, u32[]{:S(2)}) collective-permute-start(bf16[2,8,16,192]{3,2,1,0:T(8,128)(2,1)S(1)} %slice.294), channel_id=1, source_target_pairs={{0,4},{4,8},{8,12},{1,5},{5,9},{9,13},{2,6},{6,10},{10,14},{3,7},{... | collective-permute-start | bytes 294920 | tf_op jit(solution)/shard_map/ppermute | solution.py:10
  5.2 3.2 %fusion.20 = (bf16[1,3,3,192,192]{4,3,2,1,0:T(8,128)(2,1)}, bf16[1,3,3,192,192]{4,3,2,1,0:T(8,128)(2,1)S(1)}, bf16[1,3,3,192,192]{4,3,2,1,0:T(8,128)(2,1)}) fusion(bf16[3,3,3,192,192]{4,3,2,1,0:T(8,128)(2,1)} %param.6), kind=kLoop, calls=%fused_computation.46 | loop fusion | bytes 3981312 | tf_op jit(solution)/shard_map/slice | solution.py:46
  8.4 4.0 %collective-permute-start.1 = (bf16[6,1,16,192]{3,2,1,0:T(8,128)(2,1)S(1)}, bf16[6,1,16,192]{3,2,1,0:T(8,128)(2,1)S(1)}, u32[]{:S(2)}, u32[]{:S(2)}) collective-permute-start(bf16[6,1,16,192]{3,2,1,0:T(8,128)(2,1)S(1)} %get-tuple-element.69), channel_id=1, source_target_pairs={{0,1},{1,2},{2,3},{4,5},{5,6},{6,7},{8,9},{9,10},{10,11},{12,13},{... | collective-permute-start | bytes 110600 | tf_op jit(solution)/shard_map/ppermute | solution.py:20
  12.3 1.9 %collective-permute-start.2 = (bf16[6,1,16,192]{3,2,1,0:T(8,128)(2,1)S(1)}, bf16[6,1,16,192]{3,2,1,0:T(8,128)(2,1)S(1)}, u32[]{:S(2)}, u32[]{:S(2)}) collective-permute-start(bf16[6,1,16,192]{3,2,1,0:T(8,128)(2,1)S(1)} %get-tuple-element.70), channel_id=1, source_target_pairs={{1,0},{2,1},{3,2},{5,4},{6,5},{7,6},{9,8},{10,9},{11,10},{13,12},{... | collective-permute-start | bytes 110600 | tf_op jit(solution)/shard_map/ppermute | solution.py:21
  15.1 2.7 %collective-permute-done.2 = bf16[6,1,16,192]{3,2,1,0:T(8,128)(2,1)S(1)} collective-permute-done((bf16[6,1,16,192]{3,2,1,0:T(8,128)(2,1)S(1)}, bf16[6,1,16,192]{3,2,1,0:T(8,128)(2,1)S(1)}, u32[]{:S(2)}, u32[]{:S(2)}) %collective-permute-start.2) | collective-permute-done | bytes 36896 | tf_op jit(solution)/shard_map/ppermute | solution.py:21
  18.1 2.2 %fusion.22 = (bf16[4,8,16,192]{3,2,1,0:T(8,128)(2,1)}, bf16[4,8,16,192]{3,2,1,0:T(8,128)(2,1)}, bf16[4,8,16,192]{3,2,1,0:T(8,128)(2,1)}, bf16[4,8,16,192]{3,2,1,...) fusion(bf16[6,10,18,192]{3,2,1,0:T(8,128)(2,1)S(1)} %fusion.8), kind=kLoop, calls=%fused_computation.48 | loop fusion | bytes 7077888 | tf_op jit(solution)/shard_map/slice | solution.py:35
  20.6 1.2 %fusion.25 = (bf16[4,8,16,192]{3,2,1,0:T(8,128)(2,1)}, bf16[4,8,16,192]{3,2,1,0:T(8,128)(2,1)}, bf16[4,8,16,192]{3,2,1,0:T(8,128)(2,1)}, bf16[4,8,16,192]{3,2,1,...) fusion(bf16[6,9,16,192]{3,2,1,0:T(8,128)(2,1)S(1)} %get-tuple-element.67, ...), kind=kLoop, calls=%fused_computation.51 | loop fusion | bytes 2359296 | tf_op jit(solution)/shard_map/slice | solution.py:35
  21.8 2.8 %concatenate.54 = bf16[4,8,16,1728]{3,2,1,0:T(8,128)(2,1)S(1)} concatenate(bf16[4,8,16,192]{3,2,1,0:T(8,128)(2,1)} %get-tuple-element.46, bf16[4,8,16,192]{3,2,1,0:T(8,128)(2,1)} %get-tuple-element.71, bf16[4,8,16,192]{3,2,1,0:T(8,128)(2,1)} %get-tuple-element.45, bf16[4,8,16,192]{3,2,1,0:T(8,128)(2,1)} %get-tuple-element.44, bf16[4,8,16,192]{3,2,1,0:T(8,128)(2,1)S(1)} %get-tuple-element.66, ...), dimensions={3} | concatenate | bytes 3538944 | tf_op jit(solution)/shard_map/concatenate | solution.py:33
  25.3 2.9 %concatenate.55 = bf16[4,8,16,1728]{3,2,1,0:T(8,128)(2,1)S(1)} concatenate(bf16[4,8,16,192]{3,2,1,0:T(8,128)(2,1)} %get-tuple-element.40, bf16[4,8,16,192]{3,2,1,0:T(8,128)(2,1)} %get-tuple-element.72, bf16[4,8,16,192]{3,2,1,0:T(8,128)(2,1)} %get-tuple-element.39, bf16[4,8,16,192]{3,2,1,0:T(8,128)(2,1)} %get-tuple-element.38, bf16[4,8,16,192]{3,2,1,0:T(8,128)(2,1)} %get-tuple-element.65, ...), dimensions={3} | concatenate | bytes 3538944 | tf_op jit(solution)/shard_map/concatenate | solution.py:33
  28.3 1.5 %convolution_add_fusion.3 = f32[512,192]{0,1:T(8,128)} fusion(f32[512,192]{0,1:T(8,128)S(1)} %fusion.27, bf16[512,1728]{1,0:T(8,128)(2,1)S(1)} %bitcast.28, bf16[1728,192]{1,0:T(8,128)(2,1)S(1)} %bitcast.37), kind=kOutput, calls=%fused_computation.6 | convolution fusion | flops 339836928 | bytes 3219456 | tf_op jit(solution)/shard_map/dot_general | solution.py:47
  29.8 2.9 %concatenate.56 = bf16[4,8,16,1728]{3,2,1,0:T(8,128)(2,1)S(1)} concatenate(bf16[4,8,16,192]{3,2,1,0:T(8,128)(2,1)} %get-tuple-element.34, bf16[4,8,16,192]{3,2,1,0:T(8,128)(2,1)} %get-tuple-element.73, bf16[4,8,16,192]{3,2,1,0:T(8,128)(2,1)} %get-tuple-element.33, bf16[4,8,16,192]{3,2,1,0:T(8,128)(2,1)} %get-tuple-element.32, bf16[4,8,16,192]{3,2,1,0:T(8,128)(2,1)S(1)} %fusion.14, ...), dimensions={3} | concatenate | bytes 3538944 | tf_op jit(solution)/shard_map/concatenate | solution.py:33
  32.7 1.8 %convolution_add_fusion.2 = f32[512,192]{0,1:T(8,128)S(1)} fusion(f32[512,192]{0,1:T(8,128)} %convolution_add_fusion.3, bf16[512,1728]{1,0:T(8,128)(2,1)S(1)} %bitcast.26, bf16[1728,192]{1,0:T(8,128)(2,1)S(1)} %bitcast.35), kind=kOutput, calls=%fused_computation.5 | convolution fusion | flops 339836928 | bytes 3219456 | tf_op jit(solution)/shard_map/dot_general | solution.py:47
  34.9 3.7 %collective-permute-start.3 = (bf16[2,8,16,192]{3,2,1,0:T(8,128)(2,1)S(1)}, bf16[2,8,16,192]{3,2,1,0:T(8,128)(2,1)S(1)}, u32[]{:S(2)}, u32[]{:S(2)}) collective-permute-start(bf16[2,8,16,192]{3,2,1,0:T(8,128)(2,1)S(1)} %slice.321), channel_id=1, source_target_pairs={{0,4},{4,8},{8,12},{1,5},{5,9},{9,13},{2,6},{6,10},{10,14},{3,7},{... | collective-permute-start | bytes 294920 | tf_op jit(solution)/shard_map/ppermute | solution.py:10
  38.5 3.2 %fusion.19 = (bf16[1,3,3,192,192]{4,3,2,1,0:T(8,128)(2,1)}, bf16[1,3,3,192,192]{4,3,2,1,0:T(8,128)(2,1)S(1)}, bf16[1,3,3,192,192]{4,3,2,1,0:T(8,128)(2,1)}) fusion(bf16[3,3,3,192,192]{4,3,2,1,0:T(8,128)(2,1)} %param.8), kind=kLoop, calls=%fused_computation.45 | loop fusion | bytes 3981312 | tf_op jit(solution)/shard_map/slice | solution.py:46
  41.7 2.2 %collective-permute-start.4 = (bf16[6,1,16,192]{3,2,1,0:T(8,128)(2,1)S(1)}, bf16[6,1,16,192]{3,2,1,0:T(8,128)(2,1)S(1)}, u32[]{:S(2)}, u32[]{:S(2)}) collective-permute-start(bf16[6,1,16,192]{3,2,1,0:T(8,128)(2,1)S(1)} %get-tuple-element.63), channel_id=1, source_target_pairs={{0,1},{1,2},{2,3},{4,5},{5,6},{6,7},{8,9},{9,10},{10,11},{12,13},{... | collective-permute-start | bytes 110600 | tf_op jit(solution)/shard_map/ppermute | solution.py:20
  43.9 2.2 %collective-permute-start.5 = (bf16[6,1,16,192]{3,2,1,0:T(8,128)(2,1)S(1)}, bf16[6,1,16,192]{3,2,1,0:T(8,128)(2,1)S(1)}, u32[]{:S(2)}, u32[]{:S(2)}) collective-permute-start(bf16[6,1,16,192]{3,2,1,0:T(8,128)(2,1)S(1)} %get-tuple-element.64), channel_id=1, source_target_pairs={{1,0},{2,1},{3,2},{5,4},{6,5},{7,6},{9,8},{10,9},{11,10},{13,12},{... | collective-permute-start | bytes 110600 | tf_op jit(solution)/shard_map/ppermute | solution.py:21
  46.9 2.5 %collective-permute-done.5 = bf16[6,1,16,192]{3,2,1,0:T(8,128)(2,1)S(1)} collective-permute-done((bf16[6,1,16,192]{3,2,1,0:T(8,128)(2,1)S(1)}, bf16[6,1,16,192]{3,2,1,0:T(8,128)(2,1)S(1)}, u32[]{:S(2)}, u32[]{:S(2)}) %collective-permute-start.5) | collective-permute-done | bytes 36896 | tf_op jit(solution)/shard_map/ppermute | solution.py:21
  51.8 2.2 %fusion.21 = (bf16[4,8,16,192]{3,2,1,0:T(8,128)(2,1)}, bf16[4,8,16,192]{3,2,1,0:T(8,128)(2,1)}, bf16[4,8,16,192]{3,2,1,0:T(8,128)(2,1)}, bf16[4,8,16,192]{3,2,1,...) fusion(bf16[6,10,18,192]{3,2,1,0:T(8,128)(2,1)S(1)} %select_max, ...), kind=kLoop, calls=%fused_computation.47 | loop fusion | bytes 7077888 | tf_op jit(solution)/shard_map/slice | solution.py:35
  54.0 2.8 %concatenate.61 = bf16[4,8,16,1728]{3,2,1,0:T(8,128)(2,1)S(1)} concatenate(bf16[4,8,16,192]{3,2,1,0:T(8,128)(2,1)} %get-tuple-element.28, bf16[4,8,16,192]{3,2,1,0:T(8,128)(2,1)} %get-tuple-element.52, bf16[4,8,16,192]{3,2,1,0:T(8,128)(2,1)} %get-tuple-element.27, bf16[4,8,16,192]{3,2,1,0:T(8,128)(2,1)} %get-tuple-element.26, bf16[4,8,16,192]{3,2,1,0:T(8,128)(2,1)S(1)} %get-tuple-element.60, ...), dimensions={3} | concatenate | bytes 3538944 | tf_op jit(solution)/shard_map/concatenate | solution.py:33
  57.6 2.9 %concatenate.62 = bf16[4,8,16,1728]{3,2,1,0:T(8,128)(2,1)S(1)} concatenate(bf16[4,8,16,192]{3,2,1,0:T(8,128)(2,1)} %get-tuple-element.22, bf16[4,8,16,192]{3,2,1,0:T(8,128)(2,1)} %get-tuple-element.51, bf16[4,8,16,192]{3,2,1,0:T(8,128)(2,1)} %get-tuple-element.21, bf16[4,8,16,192]{3,2,1,0:T(8,128)(2,1)} %get-tuple-element.20, bf16[4,8,16,192]{3,2,1,0:T(8,128)(2,1)} %get-tuple-element.59, ...), dimensions={3} | concatenate | bytes 3538944 | tf_op jit(solution)/shard_map/concatenate | solution.py:33
  60.6 1.5 %convolution_add_fusion.1 = f32[512,192]{0,1:T(8,128)} fusion(f32[512,192]{0,1:T(8,128)S(1)} %fusion.28, bf16[512,1728]{1,0:T(8,128)(2,1)S(1)} %bitcast.29, bf16[1728,192]{1,0:T(8,128)(2,1)S(1)} %bitcast.36), kind=kOutput, calls=%fused_computation.4 | convolution fusion | flops 339836928 | bytes 3219456 | tf_op jit(solution)/shard_map/dot_general | solution.py:47
  62.1 2.9 %concatenate.63 = bf16[4,8,16,1728]{3,2,1,0:T(8,128)(2,1)S(1)} concatenate(bf16[4,8,16,192]{3,2,1,0:T(8,128)(2,1)} %get-tuple-element.16, bf16[4,8,16,192]{3,2,1,0:T(8,128)(2,1)} %get-tuple-element.50, bf16[4,8,16,192]{3,2,1,0:T(8,128)(2,1)} %get-tuple-element.15, bf16[4,8,16,192]{3,2,1,0:T(8,128)(2,1)} %get-tuple-element.14, bf16[4,8,16,192]{3,2,1,0:T(8,128)(2,1)S(1)} %multiply_convert_fusion, ...), dimensions={3} | concatenate | bytes 3538944 | tf_op jit(solution)/shard_map/concatenate | solution.py:33
  65.0 1.8 %convolution_add_fusion = f32[512,192]{0,1:T(8,128)S(1)} fusion(f32[512,192]{0,1:T(8,128)} %convolution_add_fusion.1, bf16[512,1728]{1,0:T(8,128)(2,1)S(1)} %bitcast.27, bf16[1728,192]{1,0:T(8,128)(2,1)S(1)} %bitcast.34), kind=kOutput, calls=%fused_computation.3 | convolution fusion | flops 339836928 | bytes 3219456 | tf_op jit(solution)/shard_map/dot_general | solution.py:47
  66.9 1.7 %fusion.16 = bf16[4,8,16,192]{3,2,1,0:T(8,128)(2,1)} fusion(f32[4,8,16,192]{3,2,1,0:T(8,128)S(1)} %bitcast.39, bf16[4,8,16,192]{3,2,1,0:T(8,128)(2,1)} %param.5, f32[192]{0:T(256)S(1)} %copy-done.5), kind=kLoop, calls=%fused_computation.27 | loop fusion | flops 393216 | bytes 787200 | tf_op jit(solution)/shard_map/convert_element_type | solution.py:68
  (34 shorter events, 7.9 us)
Async XLA Ops:
  1.1 7.2 %collective-permute-start = (bf16[2,8,16,192]{3,2,1,0:T(8,128)(2,1)S(1)}, bf16[2,8,16,192]{3,2,1,0:T(8,128)(2,1)S(1)}, u32[]{:S(2)}, u32[]{:S(2)}) collective-permute-start(bf16[2,8,16,192]{3,2,1,0:T(8,128)(2,1)S(1)} %slice.294), channel_id=1, source_target_pairs={{0,4},{4,8},{8,12},{1,5},{5,9},{9,13},{2,6},{6,10},{10,14},{3,7},{... | collective-permute-start | bytes 294920 | tf_op jit(solution)/shard_map/ppermute | solution.py:10
  8.4 6.7 %collective-permute-start.1 = (bf16[6,1,16,192]{3,2,1,0:T(8,128)(2,1)S(1)}, bf16[6,1,16,192]{3,2,1,0:T(8,128)(2,1)S(1)}, u32[]{:S(2)}, u32[]{:S(2)}) collective-permute-start(bf16[6,1,16,192]{3,2,1,0:T(8,128)(2,1)S(1)} %get-tuple-element.69), channel_id=1, source_target_pairs={{0,1},{1,2},{2,3},{4,5},{5,6},{6,7},{8,9},{9,10},{10,11},{12,13},{... | collective-permute-start | bytes 110600 | tf_op jit(solution)/shard_map/ppermute | solution.py:20
  12.3 5.4 %collective-permute-start.2 = (bf16[6,1,16,192]{3,2,1,0:T(8,128)(2,1)S(1)}, bf16[6,1,16,192]{3,2,1,0:T(8,128)(2,1)S(1)}, u32[]{:S(2)}, u32[]{:S(2)}) collective-permute-start(bf16[6,1,16,192]{3,2,1,0:T(8,128)(2,1)S(1)} %get-tuple-element.70), channel_id=1, source_target_pairs={{1,0},{2,1},{3,2},{5,4},{6,5},{7,6},{9,8},{10,9},{11,10},{13,12},{... | collective-permute-start | bytes 110600 | tf_op jit(solution)/shard_map/ppermute | solution.py:21
  25.3 3.0 %copy-start.3 = (bf16[1,3,3,192,192]{4,3,2,1,0:T(8,128)(2,1)S(1)}, bf16[1,3,3,192,192]{4,3,2,1,0:T(8,128)(2,1)}, u32[]{:S(2)}) copy-start(bf16[1,3,3,192,192]{4,3,2,1,0:T(8,128)(2,1)} %get-tuple-element.10) | copy-start | bytes 1990660
  29.8 2.9 %copy-start.1 = (bf16[1,3,3,192,192]{4,3,2,1,0:T(8,128)(2,1)S(1)}, bf16[1,3,3,192,192]{4,3,2,1,0:T(8,128)(2,1)}, u32[]{:S(2)}) copy-start(bf16[1,3,3,192,192]{4,3,2,1,0:T(8,128)(2,1)} %get-tuple-element.8) | copy-start | bytes 1990660
  32.7 2.0 %copy-start.4 = (f32[192]{0:T(256)S(1)}, f32[192]{0:T(256)}, u32[]{:S(2)}) copy-start(f32[192]{0:T(256)} %param.7) | copy-start | bytes 2308
  34.9 6.8 %collective-permute-start.3 = (bf16[2,8,16,192]{3,2,1,0:T(8,128)(2,1)S(1)}, bf16[2,8,16,192]{3,2,1,0:T(8,128)(2,1)S(1)}, u32[]{:S(2)}, u32[]{:S(2)}) collective-permute-start(bf16[2,8,16,192]{3,2,1,0:T(8,128)(2,1)S(1)} %slice.321), channel_id=1, source_target_pairs={{0,4},{4,8},{8,12},{1,5},{5,9},{9,13},{2,6},{6,10},{10,14},{3,7},{... | collective-permute-start | bytes 294920 | tf_op jit(solution)/shard_map/ppermute | solution.py:10
  41.7 5.1 %collective-permute-start.4 = (bf16[6,1,16,192]{3,2,1,0:T(8,128)(2,1)S(1)}, bf16[6,1,16,192]{3,2,1,0:T(8,128)(2,1)S(1)}, u32[]{:S(2)}, u32[]{:S(2)}) collective-permute-start(bf16[6,1,16,192]{3,2,1,0:T(8,128)(2,1)S(1)} %get-tuple-element.63), channel_id=1, source_target_pairs={{0,1},{1,2},{2,3},{4,5},{5,6},{6,7},{8,9},{9,10},{10,11},{12,13},{... | collective-permute-start | bytes 110600 | tf_op jit(solution)/shard_map/ppermute | solution.py:20
  43.9 5.4 %collective-permute-start.5 = (bf16[6,1,16,192]{3,2,1,0:T(8,128)(2,1)S(1)}, bf16[6,1,16,192]{3,2,1,0:T(8,128)(2,1)S(1)}, u32[]{:S(2)}, u32[]{:S(2)}) collective-permute-start(bf16[6,1,16,192]{3,2,1,0:T(8,128)(2,1)S(1)} %get-tuple-element.64), channel_id=1, source_target_pairs={{1,0},{2,1},{3,2},{5,4},{6,5},{7,6},{9,8},{10,9},{11,10},{13,12},{... | collective-permute-start | bytes 110600 | tf_op jit(solution)/shard_map/ppermute | solution.py:21
  57.6 3.0 %copy-start.2 = (bf16[1,3,3,192,192]{4,3,2,1,0:T(8,128)(2,1)S(1)}, bf16[1,3,3,192,192]{4,3,2,1,0:T(8,128)(2,1)}, u32[]{:S(2)}) copy-start(bf16[1,3,3,192,192]{4,3,2,1,0:T(8,128)(2,1)} %get-tuple-element.7) | copy-start | bytes 1990660
  62.1 2.9 %copy-start = (bf16[1,3,3,192,192]{4,3,2,1,0:T(8,128)(2,1)S(1)}, bf16[1,3,3,192,192]{4,3,2,1,0:T(8,128)(2,1)}, u32[]{:S(2)}) copy-start(bf16[1,3,3,192,192]{4,3,2,1,0:T(8,128)(2,1)} %get-tuple-element.5) | copy-start | bytes 1990660
  65.0 2.0 %copy-start.5 = (f32[192]{0:T(256)S(1)}, f32[192]{0:T(256)}, u32[]{:S(2)}) copy-start(f32[192]{0:T(256)} %param.9) | copy-start | bytes 2308
where the time goes:
time: 69.7 us; the launch traced here: 68.7 us
  local copies, waits for them, and re-layouts  31.6 us (45%)
  starting transfers between devices  17.9 us (26%)
  matrix products  8.06 us (12%)
  other arithmetic  5.74 us (8%)
  waiting for transfers between devices  5.15 us (7%)
    concatenate x6, local copies, waits for them, and re-layouts, conv_valid(): jnp.concatenate([padded[tap_time:tap_time + frame_count, tap_row:tap_row...  17.2 us
    dot_general x6, matrix products, conv_valid(): jnp.dot(stacked, kernel, preferred_element_type=jnp.float32)  8.06 us
    ppermute x2, starting transfers between devices, shifted(): lax.ppermute(value, axis, [(source, source + steps) for source in range(l...  7.7 us
    slice x5, local copies, waits for them, and re-layouts, conv_valid(): padded[tap_time:tap_time + frame_count, tap_row:tap_row + row_count, tap_...  7.59 us
    slice x2, local copies, waits for them, and re-layouts, conv_valid(): kernel = weight[tap_time].reshape(9 * chans, weight.shape[4])  6.35 us
    ppermute x2, starting transfers between devices, with_halo(): before = lax.ppermute(last, axis, up)  6.13 us
    ppermute x2, waiting for transfers between devices, with_halo(): after = lax.ppermute(leading, axis, down)  5.14 us
    ppermute x2, starting transfers between devices, with_halo(): after = lax.ppermute(leading, axis, down)  4.07 us
  transfers between devices with their start and end apart: 6, of which 2 were waited for; matrix products, arithmetic and copies ran while one was open for 12% of the time, Pallas kernels for 0%

commit v1 on v0

v1 whole, which is shorter than its diff:
```python
import jax
import jax.numpy as jnp
from jax import lax
from jax.sharding import PartitionSpec as P


def silu(value):
    value = value.astype(jnp.float32)
    return value / (1 + jnp.exp(-value))


def neighbour(value, shifts):
    axes = tuple(axis for axis, _ in shifts)
    sizes = [lax.axis_size(axis) for axis in axes]
    pairs = []
    total = 1
    for size in sizes:
        total *= size
    for source in range(total):
        coords, rest = [], source
        for size in reversed(sizes):
            coords.append(rest % size)
            rest //= size
        coords = coords[::-1]
        target = [c + step for c, (_, step) in zip(coords, shifts)]
        if all(0 <= t < s for t, s in zip(target, sizes)):
            linear = 0
            for t, s in zip(target, sizes):
                linear = linear * s + t
            pairs.append((source, linear))
    return lax.ppermute(value, axes, pairs)


def conv(field, weight):
    return lax.conv_general_dilated(
        field[None],
        weight,
        window_strides=(1, 1, 1),
        padding=((0, 0), (0, 0), (1, 1)),
        dimension_numbers=("NDHWC", "DHWIO", "NDHWC"),
        preferred_element_type=jnp.float32,
    )[0]


def local(clip_frames, w_first, b_first, w_second, b_second):
    frames, rows = clip_frames.shape[0], clip_frames.shape[1]
    x = clip_frames
    top, bottom = x[:, rows - 2 :], x[:, :2]
    earlier = neighbour(x, (("tm", 1),))
    earlier_top = neighbour(top, (("tm", 1), ("height", 1)))
    earlier_bottom = neighbour(bottom, (("tm", 1), ("height", -1)))
    own_top = neighbour(top, (("height", 1),))
    own_bottom = neighbour(bottom, (("height", -1),))
    extended = jnp.concatenate(
        [
            jnp.concatenate([earlier_top, earlier, earlier_bottom], 1),
            jnp.concatenate([own_top, x, own_bottom], 1),
        ],
        0,
    )
    activated = silu(extended).astype(jnp.bfloat16)
    hidden = conv(activated, w_first) + b_first
    frame = lax.axis_index("tm") * frames - 2 + lax.broadcasted_iota(jnp.int32, (frames + 2, 1, 1, 1), 0)
    row = lax.axis_index("height") * rows - 1 + lax.broadcasted_iota(jnp.int32, (1, rows + 2, 1, 1), 1)
    inside = (frame >= 0) & (row >= 0) & (row < rows * lax.axis_size("height"))
    gated = jnp.where(inside, silu(hidden), 0.0).astype(jnp.bfloat16)
    second = conv(gated, w_second)
    return (x.astype(jnp.float32) + second + b_second).astype(jnp.bfloat16)


def solution(mesh):
    return jax.shard_map(
        local,
        mesh=mesh,
        in_specs=(P(("clips", "tm"), "height", None, None), P(), P(), P(), P()),
        out_specs=P(("clips", "tm"), "height", None, None),
        check_vma=False,
    )
```

time: 69.7 us -> 35.3 us (0.51)
  the two profiles are of different devices: /device:TPU:1 before, /device:TPU:10 now
where the time goes in v1:
time: 35.3 us; the launch traced here: 35 us
  starting transfers between devices  14 us (40%)
  waiting for transfers between devices  7.75 us (22%)
  matrix products  7.03 us (20%)
  local copies, waits for them, and re-layouts  4.55 us (13%)
  other arithmetic  1.53 us (4%)
    ppermute x5, starting transfers between devices, neighbour(): return lax.ppermute(value, axes, pairs)  14 us
    ppermute x5, waiting for transfers between devices, neighbour(): return lax.ppermute(value, axes, pairs)  7.75 us
    conv_general_dilated x2, matrix products, conv(): lax.conv_general_dilated(field[None], weight, window_strides=(1, 1, 1), p...  7.03 us
    unnamed x13, local copies, waits for them, and re-layouts  2.22 us
    convert_element_type x1, local copies, waits for them, and re-layouts, local(): return (x.astype(jnp.float32) + second + b_second).astype(jnp.bfloat16)  0.75 us
  transfers between devices with their start and end apart: 5, of which 1 were waited for; matrix products, arithmetic and copies ran while one was open for 1% of the time, Pallas kernels for 0%

profile of v1, /device:TPU:10, one launch (start us, length us, event | category | flops | bytes accessed | tf_op | source)
XLA Modules:
  0.0 35.0 jit_solution(907991312067158026)
XLA Ops:
  0.0 1.3 %copy.7 = bf16[4,8,16,192]{3,0,2,1:T(4,128)(2,1)S(1)} copy(bf16[4,8,16,192]{3,2,1,0:T(8,128)(2,1)} %param.5) | data formatting | bytes 393216 | tf_op args[0]
  1.3 0.7 %fusion.48 = (bf16[4,2,16,192]{3,0,2,1:T(4,128)(2,1)}, bf16[4,2,16,192]{3,0,2,1:T(4,128)(2,1)S(1)}) fusion(bf16[4,8,16,192]{3,0,2,1:T(4,128)(2,1)S(1)} %copy.7), kind=kLoop, calls=%fused_computation.51 | loop fusion | bytes 196608 | tf_op jit(solution)/shard_map/slice | solution.py:48
  2.0 1.9 %collective-permute-start.3 = (bf16[4,2,16,192]{3,0,2,1:T(4,128)(2,1)}, bf16[4,2,16,192]{3,0,2,1:T(4,128)(2,1)S(1)}, u32[]{:S(2)}, u32[]{:S(2)}) collective-permute-start(bf16[4,2,16,192]{3,0,2,1:T(4,128)(2,1)} %get-tuple-element.7), channel_id=1, source_target_pairs={{0,1},{1,2},{2,3},{4,5},{5,6},{6,7},{8,9},{9,10},{10,11},{12,13},{... | collective-permute-start | bytes 147464 | tf_op jit(solution)/shard_map/ppermute | solution.py:31
  3.9 2.3 %collective-permute-start = (bf16[4,2,16,192]{3,0,2,1:T(4,128)(2,1)}, bf16[4,2,16,192]{3,0,2,1:T(4,128)(2,1)S(1)}, u32[]{:S(2)}, u32[]{:S(2)}) collective-permute-start(bf16[4,2,16,192]{3,0,2,1:T(4,128)(2,1)} %get-tuple-element.7), channel_id=1, source_target_pairs={{0,5},{1,6},{2,7},{4,9},{5,10},{6,11},{8,13},{9,14},{10,15},{16,21... | collective-permute-start | bytes 147464 | tf_op jit(solution)/shard_map/ppermute | solution.py:31
  6.2 4.3 %collective-permute-start.4 = (bf16[4,2,16,192]{3,0,2,1:T(4,128)(2,1)S(1)}, bf16[4,2,16,192]{3,0,2,1:T(4,128)(2,1)S(1)}, u32[]{:S(2)}, u32[]{:S(2)}) collective-permute-start(bf16[4,2,16,192]{3,0,2,1:T(4,128)(2,1)S(1)} %get-tuple-element.8), channel_id=1, source_target_pairs={{1,0},{2,1},{3,2},{5,4},{6,5},{7,6},{9,8},{10,9},{11,10},{13,12},{... | collective-permute-start | bytes 147464 | tf_op jit(solution)/shard_map/ppermute | solution.py:31
  10.5 3.6 %collective-permute-start.2 = (bf16[4,2,16,192]{3,0,2,1:T(4,128)(2,1)S(1)}, bf16[4,2,16,192]{3,0,2,1:T(4,128)(2,1)S(1)}, u32[]{:S(2)}, u32[]{:S(2)}) collective-permute-start(bf16[4,2,16,192]{3,0,2,1:T(4,128)(2,1)S(1)} %get-tuple-element.8), channel_id=1, source_target_pairs={{1,4},{2,5},{3,6},{5,8},{6,9},{7,10},{9,12},{10,13},{11,14},{17,20... | collective-permute-start | bytes 147464 | tf_op jit(solution)/shard_map/ppermute | solution.py:31
  14.1 1.9 %collective-permute-start.1 = (bf16[4,8,16,192]{3,0,2,1:T(4,128)(2,1)S(1)}, bf16[4,8,16,192]{3,0,2,1:T(4,128)(2,1)S(1)}, u32[]{:S(2)}, u32[]{:S(2)}) collective-permute-start(bf16[4,8,16,192]{3,0,2,1:T(4,128)(2,1)S(1)} %copy.7), channel_id=1, source_target_pairs={{0,4},{4,8},{8,12},{1,5},{5,9},{9,13},{2,6},{6,10},{10,14},{3,7},{... | collective-permute-start | bytes 589832 | tf_op jit(solution)/shard_map/ppermute | solution.py:31
  16.1 0.1 and_and_fusion
  16.1 0.3 maximum_bitcast_fusion.1
  16.5 7.7 %collective-permute-done.1 = bf16[4,8,16,192]{3,0,2,1:T(4,128)(2,1)S(1)} collective-permute-done((bf16[4,8,16,192]{3,0,2,1:T(4,128)(2,1)S(1)}, bf16[4,8,16,192]{3,0,2,1:T(4,128)(2,1)S(1)}, u32[]{:S(2)}, u32[]{:S(2)}) %collective-permute-start.1) | collective-permute-done | bytes 196640 | tf_op jit(solution)/shard_map/ppermute | solution.py:31
  24.2 0.3 maximum_bitcast_fusion
  24.5 0.7 %fusion.33 = bf16[8,12,1,16,192]{4,0,3,1,2:T(8,128)(2,1)S(1)} fusion(bf16[1,4,12,16,192]{4,1,3,2,0:T(4,128)(2,1)S(1)} %maximum_bitcast_fusion.1, bf16[1,4,12,16,192]{4,1,3,2,0:T(4,128)(2,1)S(1)} %maximum_bitcast_fusion), kind=kLoop, calls=%fused_computation.30 | loop fusion | flops 2359296 | bytes 1179648 | tf_op jit(solution)/shard_map/convert_element_type | solution.py:61
  25.2 0.2 pad
  25.4 0.0 copy-start.5
  25.4 0.2 copy.12
  25.7 0.2 slice.14
  25.9 0.2 copy-done.4
  26.1 4.6 %fusion.18 = bf16[6,10,1,8,3,192]{5,3,4,1,0,2:T(8,128)(2,1)S(1)} fusion(bf16[3,3,3,192,192]{4,3,2,1,0:T(8,128)(2,1)S(1)} %copy-done, bf16[8,12,1,7,2,192]{5,3,4,1,0,2:T(8,128)(2,1)S(1)} %slice.14, bf16[8,12,1,8,3,192]{5,3,4,1,0,2:T(8,128)(2,1)S(1)} %copy.12, f32[192]{0:T(256)S(1)} %copy-done.4, pred[8,3]{0,1:T(4,128)(4,1)S(1)} %copy-done.5, ...), kind=kOutput, calls=%fused_computation.19 | convolution fusion | flops 2873180160 | bytes 3945300 | tf_op jit(solution)/shard_map/conv_general_dilated | solution.py:35
  30.7 0.1 fusion.47
  30.8 2.4 %fusion.23 = f32[4,8,8,3,192]{4,2,3,1,0:T(8,128)S(1)} fusion(bf16[3,3,3,192,192]{4,3,2,1,0:T(8,128)(2,1)S(1)} %copy-done.3, bf16[6,10,1,7,1,192]{5,3,4,1,0,2:T(8,128)(2,1)S(1)} %get-tuple-element.6, bf16[6,10,1,7,1,192]{5,3,4,1,0,2:T(8,128)(2,1)S(1)} %get-tuple-element.5, bf16[6,10,1,8,3,192]{5,3,4,1,0,2:T(8,128)(2,1)S(1)} %fusion.18), kind=kOutput, calls=%fused_computation.22 | convolution fusion | flops 1533431808 | bytes 3456000 | tf_op jit(solution)/shard_map/conv_general_dilated | solution.py:35
  33.2 0.2 copy.13
  33.5 0.7 %copy-done.1 = bf16[4,8,16,192]{3,2,1,0:T(8,128)(2,1)S(1)} copy-done((bf16[4,8,16,192]{3,2,1,0:T(8,128)(2,1)S(1)}, bf16[4,8,16,192]{3,2,1,0:T(8,128)(2,1)}, u32[]{:S(2)}) %copy-start.1) | copy-done | bytes 196632
  34.2 0.1 fusion.37
  34.3 0.8 %copy.14 = bf16[4,8,16,192]{3,2,1,0:T(8,128)(2,1)} copy(bf16[4,8,16,192]{3,1,2,0:T(8,128)(2,1)S(1)} %fusion.37) | data formatting | bytes 393216 | tf_op jit(solution)/shard_map/convert_element_type | solution.py:68
  (15 shorter events, 0.0 us)
Async XLA Ops:
  0.0 25.9 %copy-start = (bf16[3,3,3,192,192]{4,3,2,1,0:T(8,128)(2,1)S(1)}, bf16[3,3,3,192,192]{4,3,2,1,0:T(8,128)(2,1)}, u32[]{:S(2)}) copy-start(bf16[3,3,3,192,192]{4,3,2,1,0:T(8,128)(2,1)} %param.6) | copy-start | bytes 5971972
  2.0 14.1 %collective-permute-start.3 = (bf16[4,2,16,192]{3,0,2,1:T(4,128)(2,1)}, bf16[4,2,16,192]{3,0,2,1:T(4,128)(2,1)S(1)}, u32[]{:S(2)}, u32[]{:S(2)}) collective-permute-start(bf16[4,2,16,192]{3,0,2,1:T(4,128)(2,1)} %get-tuple-element.7), channel_id=1, source_target_pairs={{0,1},{1,2},{2,3},{4,5},{5,6},{6,7},{8,9},{9,10},{10,11},{12,13},{... | collective-permute-start | bytes 147464 | tf_op jit(solution)/shard_map/ppermute | solution.py:31
  3.9 12.5 %collective-permute-start = (bf16[4,2,16,192]{3,0,2,1:T(4,128)(2,1)}, bf16[4,2,16,192]{3,0,2,1:T(4,128)(2,1)S(1)}, u32[]{:S(2)}, u32[]{:S(2)}) collective-permute-start(bf16[4,2,16,192]{3,0,2,1:T(4,128)(2,1)} %get-tuple-element.7), channel_id=1, source_target_pairs={{0,5},{1,6},{2,7},{4,9},{5,10},{6,11},{8,13},{9,14},{10,15},{16,21... | collective-permute-start | bytes 147464 | tf_op jit(solution)/shard_map/ppermute | solution.py:31
  6.2 9.9 %collective-permute-start.4 = (bf16[4,2,16,192]{3,0,2,1:T(4,128)(2,1)S(1)}, bf16[4,2,16,192]{3,0,2,1:T(4,128)(2,1)S(1)}, u32[]{:S(2)}, u32[]{:S(2)}) collective-permute-start(bf16[4,2,16,192]{3,0,2,1:T(4,128)(2,1)S(1)} %get-tuple-element.8), channel_id=1, source_target_pairs={{1,0},{2,1},{3,2},{5,4},{6,5},{7,6},{9,8},{10,9},{11,10},{13,12},{... | collective-permute-start | bytes 147464 | tf_op jit(solution)/shard_map/ppermute | solution.py:31
  10.5 6.0 %collective-permute-start.2 = (bf16[4,2,16,192]{3,0,2,1:T(4,128)(2,1)S(1)}, bf16[4,2,16,192]{3,0,2,1:T(4,128)(2,1)S(1)}, u32[]{:S(2)}, u32[]{:S(2)}) collective-permute-start(bf16[4,2,16,192]{3,0,2,1:T(4,128)(2,1)S(1)} %get-tuple-element.8), channel_id=1, source_target_pairs={{1,4},{2,5},{3,6},{5,8},{6,9},{7,10},{9,12},{10,13},{11,14},{17,20... | collective-permute-start | bytes 147464 | tf_op jit(solution)/shard_map/ppermute | solution.py:31
  14.1 10.1 %collective-permute-start.1 = (bf16[4,8,16,192]{3,0,2,1:T(4,128)(2,1)S(1)}, bf16[4,8,16,192]{3,0,2,1:T(4,128)(2,1)S(1)}, u32[]{:S(2)}, u32[]{:S(2)}) collective-permute-start(bf16[4,8,16,192]{3,0,2,1:T(4,128)(2,1)S(1)} %copy.7), channel_id=1, source_target_pairs={{0,4},{4,8},{8,12},{1,5},{5,9},{9,13},{2,6},{6,10},{10,14},{3,7},{... | collective-permute-start | bytes 589832 | tf_op jit(solution)/shard_map/ppermute | solution.py:31
  25.4 0.7 %copy-start.4 = (f32[192]{0:T(256)S(1)}, f32[192]{0:T(256)}, u32[]{:S(2)}) copy-start(f32[192]{0:T(256)} %param.7) | copy-start | bytes 2308
  25.4 0.7 %copy-start.5 = (pred[8,3]{0,1:T(4,128)(4,1)S(1)}, pred[8,3]{0,1:T(4,128)(4,1)}, u32[]{:S(2)}) copy-start(pred[8,3]{0,1:T(4,128)(4,1)} %constant.35) | copy-start | bytes 76
  26.1 4.7 %copy-start.3 = (bf16[3,3,3,192,192]{4,3,2,1,0:T(8,128)(2,1)S(1)}, bf16[3,3,3,192,192]{4,3,2,1,0:T(8,128)(2,1)}, u32[]{:S(2)}) copy-start(bf16[3,3,3,192,192]{4,3,2,1,0:T(8,128)(2,1)} %param.8) | copy-start | bytes 5971972
  33.2 1.0 %copy-start.1 = (bf16[4,8,16,192]{3,2,1,0:T(8,128)(2,1)S(1)}, bf16[4,8,16,192]{3,2,1,0:T(8,128)(2,1)}, u32[]{:S(2)}) copy-start(bf16[4,8,16,192]{3,2,1,0:T(8,128)(2,1)} %param.5) | copy-start | bytes 589828
  33.2 0.9 %copy-start.2 = (f32[192]{0:T(256)S(1)}, f32[192]{0:T(256)}, u32[]{:S(2)}) copy-start(f32[192]{0:T(256)} %param.9) | copy-start | bytes 2308

commit v2 on v1

--- a/solution.py
+++ b/solution.py
@@ -31,12 +31,12 @@
     return lax.ppermute(value, axes, pairs)
 
 
-def conv(field, weight):
+def conv(field, weight, frames_before, frames_after):
     return lax.conv_general_dilated(
         field[None],
         weight,
         window_strides=(1, 1, 1),
-        padding=((0, 0), (0, 0), (1, 1)),
+        padding=((frames_before, frames_after), (0, 0), (1, 1)),
         dimension_numbers=("NDHWC", "DHWIO", "NDHWC"),
         preferred_element_type=jnp.float32,
     )[0]
@@ -45,26 +45,28 @@
 def local(clip_frames, w_first, b_first, w_second, b_second):
     frames, rows = clip_frames.shape[0], clip_frames.shape[1]
     x = clip_frames
-    top, bottom = x[:, rows - 2 :], x[:, :2]
     earlier = neighbour(x, (("tm", 1),))
-    earlier_top = neighbour(top, (("tm", 1), ("height", 1)))
-    earlier_bottom = neighbour(bottom, (("tm", 1), ("height", -1)))
-    own_top = neighbour(top, (("height", 1),))
-    own_bottom = neighbour(bottom, (("height", -1),))
-    extended = jnp.concatenate(
+    own = jnp.concatenate(
+        [neighbour(x[:, rows - 2 :], (("height", 1),)), x, neighbour(x[:, :2], (("height", -1),))], 1
+    )
+    own_part = conv(silu(own).astype(jnp.bfloat16), w_first, 2, 0)
+    earlier = jnp.concatenate(
         [
-            jnp.concatenate([earlier_top, earlier, earlier_bottom], 1),
-            jnp.concatenate([own_top, x, own_bottom], 1),
+            neighbour(earlier[:, rows - 2 :], (("height", 1),)),
+            earlier,
+            neighbour(earlier[:, :2], (("height", -1),)),
         ],
-        0,
+        1,
     )
-    activated = silu(extended).astype(jnp.bfloat16)
-    hidden = conv(activated, w_first) + b_first
+    earlier_part = conv(silu(earlier).astype(jnp.bfloat16), w_first, 0, 2)
+    hidden = jnp.concatenate(
+        [earlier_part[:2], earlier_part[2:] + own_part[:2], own_part[2:]], 0
+    ) + b_first
     frame = lax.axis_index("tm") * frames - 2 + lax.broadcasted_iota(jnp.int32, (frames + 2, 1, 1, 1), 0)
     row = lax.axis_index("height") * rows - 1 + lax.broadcasted_iota(jnp.int32, (1, rows + 2, 1, 1), 1)
     inside = (frame >= 0) & (row >= 0) & (row < rows * lax.axis_size("height"))
     gated = jnp.where(inside, silu(hidden), 0.0).astype(jnp.bfloat16)
-    second = conv(gated, w_second)
+    second = conv(gated, w_second, 0, 0)
     return (x.astype(jnp.float32) + second + b_second).astype(jnp.bfloat16)
 
 

time: 35.3 us -> 34.1 us (0.966)
  the two profiles are of different devices: /device:TPU:10 before, /device:TPU:1 now
where the time goes in v2:
time: 34.1 us; the launch traced here: 33.8 us
  starting transfers between devices  14.5 us (43%)
  matrix products  8.25 us (24%)
  local copies, waits for them, and re-layouts  4.56 us (13%)
  waiting for transfers between devices  3.78 us (11%)
  other arithmetic  2.42 us (7%)
    ppermute x5, starting transfers between devices, neighbour(): return lax.ppermute(value, axes, pairs)  14.5 us
    conv_general_dilated x3, matrix products, conv(): lax.conv_general_dilated(field[None], weight, window_strides=(1, 1, 1), p...  8.25 us
    ppermute x5, waiting for transfers between devices, neighbour(): return lax.ppermute(value, axes, pairs)  3.78 us
    unnamed x14, local copies, waits for them, and re-layouts  1.72 us
    convert_element_type x1, other arithmetic, local(): own_part = conv(silu(own).astype(jnp.bfloat16), w_first, 2, 0)  1.2 us
    slice x1, local copies, waits for them, and re-layouts, local(): x[:, rows - 2:]  0.89 us
    convert_element_type x1, local copies, waits for them, and re-layouts, local(): return (x.astype(jnp.float32) + second + b_second).astype(jnp.bfloat16)  0.75 us
  transfers between devices with their start and end apart: 5, of which 2 were waited for; matrix products, arithmetic and copies ran while one was open for 17% of the time, Pallas kernels for 0%

profile of v2, /device:TPU:1, one launch (start us, length us, event | category | flops | bytes accessed | tf_op | source)
XLA Modules:
  0.0 33.8 jit_solution(12917737206268404507)
XLA Ops:
  0.0 4.3 %collective-permute-start = (bf16[4,8,16,192]{3,2,1,0:T(8,128)(2,1)}, bf16[4,8,16,192]{3,2,1,0:T(8,128)(2,1)S(1)}, u32[]{:S(2)}, u32[]{:S(2)}) collective-permute-start(bf16[4,8,16,192]{3,2,1,0:T(8,128)(2,1)} %param.5), channel_id=1, source_target_pairs={{0,4},{4,8},{8,12},{1,5},{5,9},{9,13},{2,6},{6,10},{10,14},{3,7},{... | collective-permute-start | bytes 589832 | tf_op jit(solution)/shard_map/ppermute | solution.py:31
  4.3 0.9 %fusion.56 = (bf16[4,2,16,192]{3,2,1,0:T(8,128)(2,1)S(1)}, bf16[4,2,16,192]{3,2,1,0:T(8,128)(2,1)S(1)}) fusion(bf16[4,8,16,192]{3,2,1,0:T(8,128)(2,1)} %param.5), kind=kLoop, calls=%fused_computation.69 | loop fusion | bytes 196608 | tf_op jit(solution)/shard_map/slice | solution.py:50
  5.2 4.0 %collective-permute-start.3 = (bf16[4,2,16,192]{3,2,1,0:T(8,128)(2,1)S(1)}, bf16[4,2,16,192]{3,2,1,0:T(8,128)(2,1)S(1)}, u32[]{:S(2)}, u32[]{:S(2)}) collective-permute-start(bf16[4,2,16,192]{3,2,1,0:T(8,128)(2,1)S(1)} %get-tuple-element.12), channel_id=1, source_target_pairs={{0,1},{1,2},{2,3},{4,5},{5,6},{6,7},{8,9},{9,10},{10,11},{12,13},{... | collective-permute-start | bytes 147464 | tf_op jit(solution)/shard_map/ppermute | solution.py:31
  9.2 1.9 %collective-permute-start.4 = (bf16[4,2,16,192]{3,2,1,0:T(8,128)(2,1)S(1)}, bf16[4,2,16,192]{3,2,1,0:T(8,128)(2,1)S(1)}, u32[]{:S(2)}, u32[]{:S(2)}) collective-permute-start(bf16[4,2,16,192]{3,2,1,0:T(8,128)(2,1)S(1)} %get-tuple-element.13), channel_id=1, source_target_pairs={{1,0},{2,1},{3,2},{5,4},{6,5},{7,6},{9,8},{10,9},{11,10},{13,12},{... | collective-permute-start | bytes 147464 | tf_op jit(solution)/shard_map/ppermute | solution.py:31
  11.2 3.5 %collective-permute-done.4 = bf16[4,2,16,192]{3,2,1,0:T(8,128)(2,1)S(1)} collective-permute-done((bf16[4,2,16,192]{3,2,1,0:T(8,128)(2,1)S(1)}, bf16[4,2,16,192]{3,2,1,0:T(8,128)(2,1)S(1)}, u32[]{:S(2)}, u32[]{:S(2)}) %collective-permute-start.4) | collective-permute-done | bytes 49184 | tf_op jit(solution)/shard_map/ppermute | solution.py:31
  14.8 1.2 %fusion.39 = bf16[4,12,1,16,192]{4,3,1,0,2:T(8,128)(2,1)S(1)} fusion(bf16[1,4,2,16,192]{4,3,2,1,0:T(8,128)(2,1)S(1)} %bitcast.41, bf16[1,4,8,16,192]{4,3,2,1,0:T(8,128)(2,1)} %bitcast.38, bf16[1,4,2,16,192]{4,3,2,1,0:T(8,128)(2,1)S(1)} %bitcast.40), kind=kLoop, calls=%fused_computation.49 | loop fusion | flops 1032192 | bytes 589824 | tf_op jit(solution)/shard_map/convert_element_type | solution.py:52
  16.0 0.3 copy.16
  16.3 0.3 pad.2.clone
  16.8 1.9 %collective-permute-start.1 = (bf16[4,2,16,192]{3,2,1,0:T(8,128)(2,1)S(1)}, bf16[4,2,16,192]{3,2,1,0:T(8,128)(2,1)S(1)}, u32[]{:S(2)}, u32[]{:S(2)}) collective-permute-start(bf16[4,2,16,192]{3,2,1,0:T(8,128)(2,1)S(1)} %get-tuple-element.10), channel_id=1, source_target_pairs={{0,1},{1,2},{2,3},{4,5},{5,6},{6,7},{8,9},{9,10},{10,11},{12,13},{... | collective-permute-start | bytes 147464 | tf_op jit(solution)/shard_map/ppermute | solution.py:31
  18.7 2.4 %collective-permute-start.2 = (bf16[4,2,16,192]{3,2,1,0:T(8,128)(2,1)S(1)}, bf16[4,2,16,192]{3,2,1,0:T(8,128)(2,1)S(1)}, u32[]{:S(2)}, u32[]{:S(2)}) collective-permute-start(bf16[4,2,16,192]{3,2,1,0:T(8,128)(2,1)S(1)} %get-tuple-element.11), channel_id=1, source_target_pairs={{1,0},{2,1},{3,2},{5,4},{6,5},{7,6},{9,8},{10,9},{11,10},{13,12},{... | collective-permute-start | bytes 147464 | tf_op jit(solution)/shard_map/ppermute | solution.py:31
  21.1 2.9 %convolution_select_fusion = f32[4,10,8,3,192]{4,2,3,1,0:T(8,128)S(1)} fusion(bf16[3,3,3,192,192]{4,3,2,1,0:T(8,128)(2,1)S(1)} %copy-done, bf16[4,12,1,7,2,192]{5,3,4,1,0,2:T(8,128)(2,1)S(1)} %slice.50, bf16[4,12,1,8,3,192]{5,3,4,1,0,2:T(8,128)(2,1)S(1)} %copy.12, pred[8,3]{0,1:T(4,128)(4,1)S(1)} %copy-done.4), kind=kOutput, calls=%fused_computation.9 | convolution fusion | flops 1435668480 | bytes 3428376 | tf_op jit(solution)/shard_map/conv_general_dilated | solution.py:35
  24.1 0.2 collective-permute-done.2
  24.3 0.2 fusion.40
  24.5 0.3 copy.15
  24.9 0.3 pad.clone
  25.3 2.9 %convolution_select_fusion.1 = f32[4,10,8,3,192]{4,2,3,1,0:T(8,128)S(1)} fusion(bf16[3,3,3,192,192]{4,3,2,1,0:T(8,128)(2,1)S(1)} %copy-done, bf16[4,12,1,7,2,192]{5,3,4,1,0,2:T(8,128)(2,1)S(1)} %slice.47, bf16[4,12,1,8,3,192]{5,3,4,1,0,2:T(8,128)(2,1)S(1)} %copy.9, pred[8,3]{0,1:T(4,128)(4,1)S(1)} %copy-done.4), kind=kOutput, calls=%fused_computation.10 | convolution fusion | flops 1435668480 | bytes 3428376 | tf_op jit(solution)/shard_map/conv_general_dilated | solution.py:35
  28.2 0.2 fusion.53
  28.4 0.5 %copy-done.2 = f32[192]{0:T(256)S(1)} copy-done((f32[192]{0:T(256)S(1)}, f32[192]{0:T(256)}, u32[]{:S(2)}) %copy-start.2) | copy-done | bytes 792
  28.9 0.6 %select_bitcast_fusion = bf16[6,10,1,8,3,192]{5,3,4,1,0,2:T(8,128)(2,1)S(1)} fusion(f32[192]{0:T(256)S(1)} %copy-done.2, f32[2,10,8,3,192]{4,2,3,1,0:T(8,128)S(1)} %get-tuple-element.7, f32[2,10,8,3,192]{4,2,3,1,0:T(8,128)S(1)} %get-tuple-element.6, f32[2,10,8,3,192]{4,2,3,1,0:T(8,128)S(1)} %get-tuple-element.5, pred[8,3]{0,1:T(4,128)(4,1)S(1)} %copy-done.4, ...), kind=kLoop, calls=%fused_computation.40 | loop fusion | flops 2488320 | bytes 1659732 | tf_op jit(solution)/shard_map/convert_element_type | solution.py:68
  29.6 0.6 %copy-done.5 = bf16[3,3,3,192,192]{4,3,2,1,0:T(8,128)(2,1)S(1)} copy-done((bf16[3,3,3,192,192]{4,3,2,1,0:T(8,128)(2,1)S(1)}, bf16[3,3,3,192,192]{4,3,2,1,0:T(8,128)(2,1)}, u32[]{:S(2)}) %copy-start.5) | copy-done | bytes 1990680
  30.2 2.5 %fusion.6 = f32[4,8,8,3,192]{4,2,3,1,0:T(8,128)S(1)} fusion(bf16[3,3,3,192,192]{4,3,2,1,0:T(8,128)(2,1)S(1)} %copy-done.5, bf16[6,10,1,7,1,192]{5,3,4,1,0,2:T(8,128)(2,1)S(1)} %get-tuple-element.9, bf16[6,10,1,7,1,192]{5,3,4,1,0,2:T(8,128)(2,1)S(1)} %get-tuple-element.8, bf16[6,10,1,8,3,192]{5,3,4,1,0,2:T(8,128)(2,1)S(1)} %select_bitcast_fusion), kind=kOutput, calls=%fused_computation.13 | convolution fusion | flops 1533431808 | bytes 3456000 | tf_op jit(solution)/shard_map/conv_general_dilated | solution.py:35
  32.6 0.2 copy.13
  32.9 0.1 fusion.36
  33.0 0.8 %copy.14 = bf16[4,8,16,192]{3,2,1,0:T(8,128)(2,1)} copy(bf16[4,8,16,192]{3,1,2,0:T(8,128)(2,1)S(1)} %fusion.36) | data formatting | bytes 393216 | tf_op jit(solution)/shard_map/convert_element_type | solution.py:70
  (22 shorter events, 0.5 us)
Async XLA Ops:
  0.0 21.1 %copy-start = (bf16[3,3,3,192,192]{4,3,2,1,0:T(8,128)(2,1)S(1)}, bf16[3,3,3,192,192]{4,3,2,1,0:T(8,128)(2,1)}, u32[]{:S(2)}) copy-start(bf16[3,3,3,192,192]{4,3,2,1,0:T(8,128)(2,1)} %param.6) | copy-start | bytes 5971972
  0.0 16.7 %collective-permute-start = (bf16[4,8,16,192]{3,2,1,0:T(8,128)(2,1)}, bf16[4,8,16,192]{3,2,1,0:T(8,128)(2,1)S(1)}, u32[]{:S(2)}, u32[]{:S(2)}) collective-permute-start(bf16[4,8,16,192]{3,2,1,0:T(8,128)(2,1)} %param.5), channel_id=1, source_target_pairs={{0,4},{4,8},{8,12},{1,5},{5,9},{9,13},{2,6},{6,10},{10,14},{3,7},{... | collective-permute-start | bytes 589832 | tf_op jit(solution)/shard_map/ppermute | solution.py:31
  5.2 6.0 %collective-permute-start.3 = (bf16[4,2,16,192]{3,2,1,0:T(8,128)(2,1)S(1)}, bf16[4,2,16,192]{3,2,1,0:T(8,128)(2,1)S(1)}, u32[]{:S(2)}, u32[]{:S(2)}) collective-permute-start(bf16[4,2,16,192]{3,2,1,0:T(8,128)(2,1)S(1)} %get-tuple-element.12), channel_id=1, source_target_pairs={{0,1},{1,2},{2,3},{4,5},{5,6},{6,7},{8,9},{9,10},{10,11},{12,13},{... | collective-permute-start | bytes 147464 | tf_op jit(solution)/shard_map/ppermute | solution.py:31
  9.2 5.6 %collective-permute-start.4 = (bf16[4,2,16,192]{3,2,1,0:T(8,128)(2,1)S(1)}, bf16[4,2,16,192]{3,2,1,0:T(8,128)(2,1)S(1)}, u32[]{:S(2)}, u32[]{:S(2)}) collective-permute-start(bf16[4,2,16,192]{3,2,1,0:T(8,128)(2,1)S(1)} %get-tuple-element.13), channel_id=1, source_target_pairs={{1,0},{2,1},{3,2},{5,4},{6,5},{7,6},{9,8},{10,9},{11,10},{13,12},{... | collective-permute-start | bytes 147464 | tf_op jit(solution)/shard_map/ppermute | solution.py:31
  16.0 5.2 %copy-start.4 = (pred[8,3]{0,1:T(4,128)(4,1)S(1)}, pred[8,3]{0,1:T(4,128)(4,1)}, u32[]{:S(2)}) copy-start(pred[8,3]{0,1:T(4,128)(4,1)} %constant.39) | copy-start | bytes 76
  16.8 7.3 %collective-permute-start.1 = (bf16[4,2,16,192]{3,2,1,0:T(8,128)(2,1)S(1)}, bf16[4,2,16,192]{3,2,1,0:T(8,128)(2,1)S(1)}, u32[]{:S(2)}, u32[]{:S(2)}) collective-permute-start(bf16[4,2,16,192]{3,2,1,0:T(8,128)(2,1)S(1)} %get-tuple-element.10), channel_id=1, source_target_pairs={{0,1},{1,2},{2,3},{4,5},{5,6},{6,7},{8,9},{9,10},{10,11},{12,13},{... | collective-permute-start | bytes 147464 | tf_op jit(solution)/shard_map/ppermute | solution.py:31
  18.7 5.6 %collective-permute-start.2 = (bf16[4,2,16,192]{3,2,1,0:T(8,128)(2,1)S(1)}, bf16[4,2,16,192]{3,2,1,0:T(8,128)(2,1)S(1)}, u32[]{:S(2)}, u32[]{:S(2)}) collective-permute-start(bf16[4,2,16,192]{3,2,1,0:T(8,128)(2,1)S(1)} %get-tuple-element.11), channel_id=1, source_target_pairs={{1,0},{2,1},{3,2},{5,4},{6,5},{7,6},{9,8},{10,9},{11,10},{13,12},{... | collective-permute-start | bytes 147464 | tf_op jit(solution)/shard_map/ppermute | solution.py:31
  28.2 0.7 %copy-start.2 = (f32[192]{0:T(256)S(1)}, f32[192]{0:T(256)}, u32[]{:S(2)}) copy-start(f32[192]{0:T(256)} %param.7) | copy-start | bytes 2308
  28.4 1.8 %copy-start.5 = (bf16[3,3,3,192,192]{4,3,2,1,0:T(8,128)(2,1)S(1)}, bf16[3,3,3,192,192]{4,3,2,1,0:T(8,128)(2,1)}, u32[]{:S(2)}) copy-start(bf16[3,3,3,192,192]{4,3,2,1,0:T(8,128)(2,1)} %param.8) | copy-start | bytes 5971972
  30.2 2.7 %copy-start.1 = (bf16[4,8,16,192]{3,2,1,0:T(8,128)(2,1)S(1)}, bf16[4,8,16,192]{3,2,1,0:T(8,128)(2,1)}, u32[]{:S(2)}) copy-start(bf16[4,8,16,192]{3,2,1,0:T(8,128)(2,1)} %param.5) | copy-start | bytes 589828
  30.2 2.7 %copy-start.3 = (f32[192]{0:T(256)S(1)}, f32[192]{0:T(256)}, u32[]{:S(2)}) copy-start(f32[192]{0:T(256)} %param.9) | copy-start | bytes 2308

commit v3 on v2

--- a/solution.py
+++ b/solution.py
@@ -45,23 +45,16 @@
 def local(clip_frames, w_first, b_first, w_second, b_second):
     frames, rows = clip_frames.shape[0], clip_frames.shape[1]
     x = clip_frames
-    earlier = neighbour(x, (("tm", 1),))
-    own = jnp.concatenate(
-        [neighbour(x[:, rows - 2 :], (("height", 1),)), x, neighbour(x[:, :2], (("height", -1),))], 1
-    )
-    own_part = conv(silu(own).astype(jnp.bfloat16), w_first, 2, 0)
-    earlier = jnp.concatenate(
+    extended = jnp.concatenate([neighbour(x, (("tm", 1),)), x], 0)
+    extended = jnp.concatenate(
         [
-            neighbour(earlier[:, rows - 2 :], (("height", 1),)),
-            earlier,
-            neighbour(earlier[:, :2], (("height", -1),)),
+            neighbour(extended[:, rows - 2 :], (("height", 1),)),
+            extended,
+            neighbour(extended[:, :2], (("height", -1),)),
         ],
         1,
     )
-    earlier_part = conv(silu(earlier).astype(jnp.bfloat16), w_first, 0, 2)
-    hidden = jnp.concatenate(
-        [earlier_part[:2], earlier_part[2:] + own_part[:2], own_part[2:]], 0
-    ) + b_first
+    hidden = conv(silu(extended).astype(jnp.bfloat16), w_first, 0, 0) + b_first
     frame = lax.axis_index("tm") * frames - 2 + lax.broadcasted_iota(jnp.int32, (frames + 2, 1, 1, 1), 0)
     row = lax.axis_index("height") * rows - 1 + lax.broadcasted_iota(jnp.int32, (1, rows + 2, 1, 1), 1)
     inside = (frame >= 0) & (row >= 0) & (row < rows * lax.axis_size("height"))

time: 34.1 us -> 32 us (0.938)
  the two profiles are of different devices: /device:TPU:1 before, /device:TPU:17 now
where the time goes in v3:
time: 32 us; the launch traced here: 31.8 us
  waiting for transfers between devices  9.79 us (31%)
  starting transfers between devices  9.68 us (30%)
  matrix products  7.03 us (22%)
  local copies, waits for them, and re-layouts  3.87 us (12%)
  other arithmetic  1.22 us (4%)
    ppermute x3, waiting for transfers between devices, neighbour(): return lax.ppermute(value, axes, pairs)  9.79 us
    ppermute x3, starting transfers between devices, neighbour(): return lax.ppermute(value, axes, pairs)  9.68 us
    conv_general_dilated x2, matrix products, conv(): lax.conv_general_dilated(field[None], weight, window_strides=(1, 1, 1), p...  7.03 us
    unnamed x13, local copies, waits for them, and re-layouts  2.22 us
    convert_element_type x1, local copies, waits for them, and re-layouts, local(): return (x.astype(jnp.float32) + second + b_second).astype(jnp.bfloat16)  0.75 us
    conv_general_dilated x3, local copies, waits for them, and re-layouts, conv(): lax.conv_general_dilated(field[None], weight, window_strides=(1, 1, 1), p...  0.67 us
  transfers between devices with their start and end apart: 3, of which 2 were waited for; matrix products, arithmetic and copies ran while one was open for 1% of the time, Pallas kernels for 0%

profile of v3, /device:TPU:17, one launch (start us, length us, event | category | flops | bytes accessed | tf_op | source)
XLA Modules:
  0.0 31.8 jit_solution(2243752755006393679)
XLA Ops:
  0.0 1.3 %copy.7 = bf16[4,8,16,192]{3,0,2,1:T(4,128)(2,1)S(1)} copy(bf16[4,8,16,192]{3,2,1,0:T(8,128)(2,1)} %param.5) | data formatting | bytes 393216 | tf_op args[0]
  1.3 3.2 %collective-permute-start = (bf16[4,8,16,192]{3,0,2,1:T(4,128)(2,1)S(1)}, bf16[4,8,16,192]{3,0,2,1:T(4,128)(2,1)S(1)}, u32[]{:S(2)}, u32[]{:S(2)}) collective-permute-start(bf16[4,8,16,192]{3,0,2,1:T(4,128)(2,1)S(1)} %copy.7), channel_id=1, source_target_pairs={{0,4},{4,8},{8,12},{1,5},{5,9},{9,13},{2,6},{6,10},{10,14},{3,7},{... | collective-permute-start | bytes 589832 | tf_op jit(solution)/shard_map/ppermute | solution.py:31
  4.6 0.1 and_and_fusion
  4.6 5.7 %collective-permute-done = bf16[4,8,16,192]{3,0,2,1:T(4,128)(2,1)S(1)} collective-permute-done((bf16[4,8,16,192]{3,0,2,1:T(4,128)(2,1)S(1)}, bf16[4,8,16,192]{3,0,2,1:T(4,128)(2,1)S(1)}, u32[]{:S(2)}, u32[]{:S(2)}) %collective-permute-start) | collective-permute-done | bytes 196640 | tf_op jit(solution)/shard_map/ppermute | solution.py:31
  10.4 0.2 fusion.39
  10.5 4.6 %collective-permute-start.1 = (bf16[8,2,16,192]{3,0,2,1:T(8,128)(2,1)S(1)}, bf16[8,2,16,192]{3,0,2,1:T(8,128)(2,1)S(1)}, u32[]{:S(2)}, u32[]{:S(2)}) collective-permute-start(bf16[8,2,16,192]{3,0,2,1:T(8,128)(2,1)S(1)} %get-tuple-element.7), channel_id=1, source_target_pairs={{0,1},{1,2},{2,3},{4,5},{5,6},{6,7},{8,9},{9,10},{10,11},{12,13},{... | collective-permute-start | bytes 294920 | tf_op jit(solution)/shard_map/ppermute | solution.py:31
  15.1 1.9 %collective-permute-start.2 = (bf16[8,2,16,192]{3,0,2,1:T(8,128)(2,1)S(1)}, bf16[8,2,16,192]{3,0,2,1:T(8,128)(2,1)S(1)}, u32[]{:S(2)}, u32[]{:S(2)}) collective-permute-start(bf16[8,2,16,192]{3,0,2,1:T(8,128)(2,1)S(1)} %get-tuple-element.8), channel_id=1, source_target_pairs={{1,0},{2,1},{3,2},{5,4},{6,5},{7,6},{9,8},{10,9},{11,10},{13,12},{... | collective-permute-start | bytes 294920 | tf_op jit(solution)/shard_map/ppermute | solution.py:31
  17.0 0.3 fusion.35
  17.3 4.0 %collective-permute-done.2 = bf16[8,2,16,192]{3,0,2,1:T(8,128)(2,1)S(1)} collective-permute-done((bf16[8,2,16,192]{3,0,2,1:T(8,128)(2,1)S(1)}, bf16[8,2,16,192]{3,0,2,1:T(8,128)(2,1)S(1)}, u32[]{:S(2)}, u32[]{:S(2)}) %collective-permute-start.2) | collective-permute-done | bytes 98336 | tf_op jit(solution)/shard_map/ppermute | solution.py:31
  21.4 0.5 %fusion.33 = bf16[8,12,1,16,192]{4,0,3,1,2:T(8,128)(2,1)S(1)} fusion(bf16[1,8,2,16,192]{4,1,3,2,0:T(8,128)(2,1)S(1)} %bitcast.35, bf16[1,8,8,16,192]{4,1,3,2,0:T(8,128)(2,1)S(1)} %fusion.35, bf16[1,8,2,16,192]{4,1,3,2,0:T(8,128)(2,1)S(1)} %bitcast.34), kind=kLoop, calls=%fused_computation.30 | loop fusion | flops 2064384 | bytes 1179648 | tf_op jit(solution)/shard_map/convert_element_type | solution.py:57
  21.9 0.2 pad
  22.1 0.0 copy-start.4
  22.1 0.0 copy-start.5
  22.1 0.2 copy.10
  22.4 0.2 slice.16
  22.6 0.2 copy-done.4
  22.8 4.6 %fusion.18 = bf16[6,10,1,8,3,192]{5,3,4,1,0,2:T(8,128)(2,1)S(1)} fusion(bf16[3,3,3,192,192]{4,3,2,1,0:T(8,128)(2,1)S(1)} %copy-done, bf16[8,12,1,7,2,192]{5,3,4,1,0,2:T(8,128)(2,1)S(1)} %slice.16, bf16[8,12,1,8,3,192]{5,3,4,1,0,2:T(8,128)(2,1)S(1)} %copy.10, f32[192]{0:T(256)S(1)} %copy-done.4, pred[8,3]{0,1:T(4,128)(4,1)S(1)} %copy-done.5, ...), kind=kOutput, calls=%fused_computation.19 | convolution fusion | flops 2873180160 | bytes 3945300 | tf_op jit(solution)/shard_map/conv_general_dilated | solution.py:35
  27.4 0.1 fusion.50
  27.5 2.4 %fusion.23 = f32[4,8,8,3,192]{4,2,3,1,0:T(8,128)S(1)} fusion(bf16[3,3,3,192,192]{4,3,2,1,0:T(8,128)(2,1)S(1)} %copy-done.3, bf16[6,10,1,7,1,192]{5,3,4,1,0,2:T(8,128)(2,1)S(1)} %get-tuple-element.6, bf16[6,10,1,7,1,192]{5,3,4,1,0,2:T(8,128)(2,1)S(1)} %get-tuple-element.5, bf16[6,10,1,8,3,192]{5,3,4,1,0,2:T(8,128)(2,1)S(1)} %fusion.18), kind=kOutput, calls=%fused_computation.22 | convolution fusion | flops 1533431808 | bytes 3456000 | tf_op jit(solution)/shard_map/conv_general_dilated | solution.py:35
  29.9 0.0 copy-start.1
  29.9 0.2 copy.11
  30.2 0.7 %copy-done.1 = bf16[4,8,16,192]{3,2,1,0:T(8,128)(2,1)S(1)} copy-done((bf16[4,8,16,192]{3,2,1,0:T(8,128)(2,1)S(1)}, bf16[4,8,16,192]{3,2,1,0:T(8,128)(2,1)}, u32[]{:S(2)}) %copy-start.1) | copy-done | bytes 196632
  30.9 0.1 fusion.38
  31.0 0.8 %copy.12 = bf16[4,8,16,192]{3,2,1,0:T(8,128)(2,1)} copy(bf16[4,8,16,192]{3,1,2,0:T(8,128)(2,1)S(1)} %fusion.38) | data formatting | bytes 393216 | tf_op jit(solution)/shard_map/convert_element_type | solution.py:63
  (10 shorter events, 0.0 us)
Async XLA Ops:
  0.0 22.6 %copy-start = (bf16[3,3,3,192,192]{4,3,2,1,0:T(8,128)(2,1)S(1)}, bf16[3,3,3,192,192]{4,3,2,1,0:T(8,128)(2,1)}, u32[]{:S(2)}) copy-start(bf16[3,3,3,192,192]{4,3,2,1,0:T(8,128)(2,1)} %param.6) | copy-start | bytes 5971972
  1.3 9.1 %collective-permute-start = (bf16[4,8,16,192]{3,0,2,1:T(4,128)(2,1)S(1)}, bf16[4,8,16,192]{3,0,2,1:T(4,128)(2,1)S(1)}, u32[]{:S(2)}, u32[]{:S(2)}) collective-permute-start(bf16[4,8,16,192]{3,0,2,1:T(4,128)(2,1)S(1)} %copy.7), channel_id=1, source_target_pairs={{0,4},{4,8},{8,12},{1,5},{5,9},{9,13},{2,6},{6,10},{10,14},{3,7},{... | collective-permute-start | bytes 589832 | tf_op jit(solution)/shard_map/ppermute | solution.py:31
  10.5 6.8 %collective-permute-start.1 = (bf16[8,2,16,192]{3,0,2,1:T(8,128)(2,1)S(1)}, bf16[8,2,16,192]{3,0,2,1:T(8,128)(2,1)S(1)}, u32[]{:S(2)}, u32[]{:S(2)}) collective-permute-start(bf16[8,2,16,192]{3,0,2,1:T(8,128)(2,1)S(1)} %get-tuple-element.7), channel_id=1, source_target_pairs={{0,1},{1,2},{2,3},{4,5},{5,6},{6,7},{8,9},{9,10},{10,11},{12,13},{... | collective-permute-start | bytes 294920 | tf_op jit(solution)/shard_map/ppermute | solution.py:31
  15.1 6.3 %collective-permute-start.2 = (bf16[8,2,16,192]{3,0,2,1:T(8,128)(2,1)S(1)}, bf16[8,2,16,192]{3,0,2,1:T(8,128)(2,1)S(1)}, u32[]{:S(2)}, u32[]{:S(2)}) collective-permute-start(bf16[8,2,16,192]{3,0,2,1:T(8,128)(2,1)S(1)} %get-tuple-element.8), channel_id=1, source_target_pairs={{1,0},{2,1},{3,2},{5,4},{6,5},{7,6},{9,8},{10,9},{11,10},{13,12},{... | collective-permute-start | bytes 294920 | tf_op jit(solution)/shard_map/ppermute | solution.py:31
  22.1 0.7 %copy-start.4 = (f32[192]{0:T(256)S(1)}, f32[192]{0:T(256)}, u32[]{:S(2)}) copy-start(f32[192]{0:T(256)} %param.7) | copy-start | bytes 2308
  22.1 0.7 %copy-start.5 = (pred[8,3]{0,1:T(4,128)(4,1)S(1)}, pred[8,3]{0,1:T(4,128)(4,1)}, u32[]{:S(2)}) copy-start(pred[8,3]{0,1:T(4,128)(4,1)} %constant.35) | copy-start | bytes 76
  22.8 4.7 %copy-start.3 = (bf16[3,3,3,192,192]{4,3,2,1,0:T(8,128)(2,1)S(1)}, bf16[3,3,3,192,192]{4,3,2,1,0:T(8,128)(2,1)}, u32[]{:S(2)}) copy-start(bf16[3,3,3,192,192]{4,3,2,1,0:T(8,128)(2,1)} %param.8) | copy-start | bytes 5971972
  29.9 1.0 %copy-start.1 = (bf16[4,8,16,192]{3,2,1,0:T(8,128)(2,1)S(1)}, bf16[4,8,16,192]{3,2,1,0:T(8,128)(2,1)}, u32[]{:S(2)}) copy-start(bf16[4,8,16,192]{3,2,1,0:T(8,128)(2,1)} %param.5) | copy-start | bytes 589828
  29.9 0.9 %copy-start.2 = (f32[192]{0:T(256)S(1)}, f32[192]{0:T(256)}, u32[]{:S(2)}) copy-start(f32[192]{0:T(256)} %param.9) | copy-start | bytes 2308

commit v4 on v3

v4 whole, which is shorter than its diff:
```python
import functools

import jax
import jax.numpy as jnp
from jax import lax
from jax.experimental import pallas as pl
from jax.experimental.pallas import tpu as pltpu
from jax.sharding import PartitionSpec as P


def silu(value):
    value = value.astype(jnp.float32)
    return value / (1 + jnp.exp(-value))


def neighbour(value, axis, step):
    size = lax.axis_size(axis)
    pairs = [(i, i + step) for i in range(size) if 0 <= i + step < size]
    return lax.ppermute(value, axis, pairs)


def column_taps(flat, cols, store):
    count = flat.shape[0]
    col = lax.broadcasted_iota(jnp.int32, flat.shape, 0) % cols
    store(0, jnp.where(col == 0, 0.0, pltpu.roll(flat, 1, 0)).astype(jnp.bfloat16))
    store(1, flat.astype(jnp.bfloat16))
    store(2, jnp.where(col == cols - 1, 0.0, pltpu.roll(flat, count - 1, 0)).astype(jnp.bfloat16))


def conv_taps(taps, weight, frames, rows):
    cols, chans = taps.shape[3], taps.shape[4]
    total = None
    for a in range(3):
        for b in range(3):
            for e in range(3):
                lhs = taps[e, a : a + frames, b : b + rows].reshape(frames * rows * cols, chans)
                term = jnp.dot(lhs, weight[(a * 3 + b) * 3 + e], preferred_element_type=jnp.float32)
                total = term if total is None else total + term
    return total


def block_kernel(flags, earlier, own, top, bottom, w_first, b_first, w_second, b_second, out, field, taps1, taps2):
    frames, rows, cols, chans = own.shape
    field[0:frames, 2 : rows + 2] = silu(earlier[...])
    field[frames:, 2 : rows + 2] = silu(own[...])
    field[:, 0:2] = silu(top[...])
    field[:, rows + 2 :] = silu(bottom[...])
    flat = field[...].reshape(2 * frames * (rows + 4) * cols, chans)

    def store1(e, value):
        taps1[e] = value.reshape(2 * frames, rows + 4, cols, chans)

    column_taps(flat, cols, store1)
    hidden = conv_taps(taps1, w_first, frames + 2, rows + 2) + b_first[...]

    def store2(e, value):
        taps2[e] = value.reshape(frames + 2, rows + 2, cols, chans)

    column_taps(silu(hidden), cols, store2)

    @pl.when(flags[0] != 0)
    def _():
        taps2[:, 0:2] = jnp.zeros((3, 2, rows + 2, cols, chans), jnp.bfloat16)

    @pl.when(flags[1] != 0)
    def _():
        taps2[:, :, 0:1] = jnp.zeros((3, frames + 2, 1, cols, chans), jnp.bfloat16)

    @pl.when(flags[2] != 0)
    def _():
        taps2[:, :, rows + 1 :] = jnp.zeros((3, frames + 2, 1, cols, chans), jnp.bfloat16)

    second = conv_taps(taps2, w_second, frames, rows) + b_second[...]
    result = own[...].astype(jnp.float32).reshape(frames * rows * cols, chans) + second
    out[...] = result.astype(jnp.bfloat16).reshape(frames, rows, cols, chans)


def block(flags, earlier, own, top, bottom, w_first, b_first, w_second, b_second):
    frames, rows, cols, chans = own.shape
    taps = w_first.shape[0] * w_first.shape[1] * w_first.shape[2]
    w_first = w_first.reshape(taps, chans, chans)
    w_second = w_second.reshape(taps, chans, chans)
    positions = (frames + 2) * (rows + 2) * cols + frames * rows * cols
    vmem = pl.BlockSpec(memory_space=pltpu.VMEM)
    return pl.pallas_call(
        block_kernel,
        out_shape=jax.ShapeDtypeStruct(own.shape, own.dtype),
        in_specs=[pl.BlockSpec(memory_space=pltpu.SMEM)] + [vmem] * 8,
        out_specs=vmem,
        scratch_shapes=[
            pltpu.VMEM((2 * frames, rows + 4, cols, chans), jnp.float32),
            pltpu.VMEM((3, 2 * frames, rows + 4, cols, chans), jnp.bfloat16),
            pltpu.VMEM((3, frames + 2, rows + 2, cols, chans), jnp.bfloat16),
        ],
        cost_estimate=pl.CostEstimate(
            flops=2 * positions * taps * chans * chans,
            transcendentals=2 * positions * chans,
            bytes_accessed=2 * (2 * taps * chans * chans + 4 * own.size),
        ),
    )(flags, earlier, own, top, bottom, w_first, b_first.reshape(1, chans), w_second, b_second.reshape(1, chans))


def local(clip_frames, w_first, b_first, w_second, b_second):
    rows = clip_frames.shape[1]
    x = clip_frames
    earlier = neighbour(x, "tm", 1)
    extended = jnp.concatenate([earlier, x], 0)
    top = neighbour(extended[:, rows - 2 :], "height", 1)
    bottom = neighbour(extended[:, :2], "height", -1)
    t, h = lax.axis_index("tm"), lax.axis_index("height")
    flags = jnp.stack([t == 0, h == 0, h == lax.axis_size("height") - 1]).astype(jnp.int32)
    return block(flags, earlier, x, top, bottom, w_first, b_first, w_second, b_second)


def solution(mesh):
    return jax.shard_map(
        local,
        mesh=mesh,
        in_specs=(P(("clips", "tm"), "height", None, None), P(), P(), P(), P()),
        out_specs=P(("clips", "tm"), "height", None, None),
        check_vma=False,
    )
```

time: 32 us -> 33.6 us (1.050)
  the two profiles are of different devices: /device:TPU:17 before, /device:TPU:10 now
where the time goes in v4:
time: 33.6 us; the launch traced here: 33.4 us
  Pallas kernels  13.3 us (40%)
  waiting for transfers between devices  9.93 us (30%)
  starting transfers between devices  7.8 us (23%)
  local copies, waits for them, and re-layouts  1.75 us (5%)
  other arithmetic  0.58 us (2%)
    pallas_call x1, Pallas kernels, block(): pl.pallas_call(block_kernel, out_shape=jax.ShapeDtypeStruct(own.shape, ow...  13.3 us
    ppermute x3, waiting for transfers between devices, neighbour(): return lax.ppermute(value, axis, pairs)  9.93 us
    ppermute x3, starting transfers between devices, neighbour(): return lax.ppermute(value, axis, pairs)  7.8 us
    concatenate x1, local copies, waits for them, and re-layouts, local(): extended = jnp.concatenate([earlier, x], 0)  1.06 us
  transfers between devices with their start and end apart: 3, of which 2 were waited for; matrix products, arithmetic and copies ran while one was open for 2% of the time, Pallas kernels for 0%

profile of v4, /device:TPU:10, one launch (start us, length us, event | category | flops | bytes accessed | tf_op | source)
XLA Modules:
  0.0 33.4 jit_solution(4444394911810359858)
XLA Ops:
  0.0 3.5 %collective-permute-start = (bf16[4,8,16,192]{3,2,1,0:T(8,128)(2,1)}, bf16[4,8,16,192]{3,2,1,0:T(8,128)(2,1)S(1)}, u32[]{:S(2)}, u32[]{:S(2)}) collective-permute-start(bf16[4,8,16,192]{3,2,1,0:T(8,128)(2,1)} %own.1), channel_id=1, source_target_pairs={{0,4},{4,8},{8,12},{1,5},{5,9},{9,13},{2,6},{6,10},{10,14},{3,7},{... | collective-permute-start | bytes 589832 | tf_op jit(solution)/shard_map/ppermute | solution.py:19
  3.5 6.6 %collective-permute-done.earlier = bf16[4,8,16,192]{3,2,1,0:T(8,128)(2,1)S(1)} collective-permute-done((bf16[4,8,16,192]{3,2,1,0:T(8,128)(2,1)}, bf16[4,8,16,192]{3,2,1,0:T(8,128)(2,1)S(1)}, u32[]{:S(2)}, u32[]{:S(2)}) %collective-permute-start) | collective-permute-done | bytes 196640 | tf_op jit(solution)/shard_map/ppermute | solution.py:19
  10.1 0.0 copy-start
  10.2 1.1 %constant_dynamic-update-slice_fusion = bf16[8,8,16,192]{3,2,1,0:T(8,128)(2,1)S(1)} fusion(bf16[8,8,16,192]{3,2,1,0:T(8,128)(2,1)S(1)} %constant_dynamic-update-slice_fusion.1, bf16[4,8,16,192]{3,2,1,0:T(8,128)(2,1)} %own.1), kind=kLoop, calls=%fused_computation | loop fusion | bytes 458752 | tf_op jit(solution)/shard_map/concatenate | solution.py:107
  11.3 1.9 %collective-permute-start.2 = (bf16[8,2,16,192]{3,2,1,0:T(8,128)(2,1)S(1)}, bf16[8,2,16,192]{3,2,1,0:T(8,128)(2,1)S(1)}, u32[]{:S(2)}, u32[]{:S(2)}) collective-permute-start(bf16[8,2,16,192]{3,2,1,0:T(8,128)(2,1)S(1)} %get-tuple-element.5), channel_id=1, source_target_pairs={{1,0},{2,1},{3,2},{5,4},{6,5},{7,6},{9,8},{10,9},{11,10},{13,12},{... | collective-permute-start | bytes 294920 | tf_op jit(solution)/shard_map/ppermute | solution.py:19
  13.2 2.4 %collective-permute-start.1 = (bf16[8,2,16,192]{3,2,1,0:T(8,128)(2,1)S(1)}, bf16[8,2,16,192]{3,2,1,0:T(8,128)(2,1)S(1)}, u32[]{:S(2)}, u32[]{:S(2)}) collective-permute-start(bf16[8,2,16,192]{3,2,1,0:T(8,128)(2,1)S(1)} %get-tuple-element.6), channel_id=1, source_target_pairs={{0,1},{1,2},{2,3},{4,5},{5,6},{6,7},{8,9},{9,10},{10,11},{12,13},{... | collective-permute-start | bytes 294920 | tf_op jit(solution)/shard_map/ppermute | solution.py:19
  15.6 0.6 %add_convert_fusion.flags = s32[3]{0:T(128)} fusion(pred[1]{0:T(512)(128)(4,1)} %bitcast.2, pred[1]{0:T(512)(128)(4,1)} %bitcast.1, pred[1]{0:T(512)(128)(4,1)} %bitcast), kind=kLoop, calls=%fused_computation.2 | loop fusion | flops 9 | bytes 15 | tf_op jit(solution)/shard_map/convert_element_type | solution.py:111
  16.2 0.0 collective-permute-done.2.bottom
  16.2 0.0 copy-start.1
  16.2 3.3 %collective-permute-done.1.top = bf16[8,2,16,192]{3,2,1,0:T(8,128)(2,1)S(1)} collective-permute-done((bf16[8,2,16,192]{3,2,1,0:T(8,128)(2,1)S(1)}, bf16[8,2,16,192]{3,2,1,0:T(8,128)(2,1)S(1)}, u32[]{:S(2)}, u32[]{:S(2)}) %collective-permute-start.1) | collective-permute-done | bytes 98336 | tf_op jit(solution)/shard_map/ppermute | solution.py:19
  19.5 0.0 copy-start.2
  19.5 0.0 copy-done
  19.5 0.0 copy-done.1
  19.5 0.6 %copy-done.2 = bf16[8,2,16,192]{3,2,1,0:T(8,128)(2,1)} copy-done((bf16[8,2,16,192]{3,2,1,0:T(8,128)(2,1)}, bf16[8,2,16,192]{3,2,1,0:T(8,128)(2,1)S(1)}, u32[]{:S(2)}) %copy-start.2) | copy-done | bytes 98328
  20.1 13.3 %shard_map.55 = bf16[4,8,16,192]{3,2,1,0:T(8,128)(2,1)} custom-call(s32[3]{0:T(128)} %add_convert_fusion.flags, bf16[4,8,16,192]{3,2,1,0:T(8,128)(2,1)} %copy-done, bf16[4,8,16,192]{3,2,1,0:T(8,128)(2,1)} %own.1, bf16[8,2,16,192]{3,2,1,0:T(8,128)(2,1)} %copy-done.2, bf16[8,2,16,192]{3,2,1,0:T(8,128)(2,1)} %copy-done.1, bf16[27,192,192]{2,1,0:T(8,128)(2,1)} %bitcast.7, ...), custom_call_target="tpu_custom_call" | custom-call | flops 2930245632 | bytes 4767744 | tf_op jit(solution)/shard_map/pallas_call | solution.py:85
  (2 shorter events, 0.0 us)
Async XLA Ops:
  0.0 10.1 %collective-permute-start = (bf16[4,8,16,192]{3,2,1,0:T(8,128)(2,1)}, bf16[4,8,16,192]{3,2,1,0:T(8,128)(2,1)S(1)}, u32[]{:S(2)}, u32[]{:S(2)}) collective-permute-start(bf16[4,8,16,192]{3,2,1,0:T(8,128)(2,1)} %own.1), channel_id=1, source_target_pairs={{0,4},{4,8},{8,12},{1,5},{5,9},{9,13},{2,6},{6,10},{10,14},{3,7},{... | collective-permute-start | bytes 589832 | tf_op jit(solution)/shard_map/ppermute | solution.py:19
  10.1 9.3 %copy-start = (bf16[4,8,16,192]{3,2,1,0:T(8,128)(2,1)}, bf16[4,8,16,192]{3,2,1,0:T(8,128)(2,1)S(1)}, u32[]{:S(2)}) copy-start(bf16[4,8,16,192]{3,2,1,0:T(8,128)(2,1)S(1)} %collective-permute-done.earlier) | copy-start | bytes 589828
  11.3 4.9 %collective-permute-start.2 = (bf16[8,2,16,192]{3,2,1,0:T(8,128)(2,1)S(1)}, bf16[8,2,16,192]{3,2,1,0:T(8,128)(2,1)S(1)}, u32[]{:S(2)}, u32[]{:S(2)}) collective-permute-start(bf16[8,2,16,192]{3,2,1,0:T(8,128)(2,1)S(1)} %get-tuple-element.5), channel_id=1, source_target_pairs={{1,0},{2,1},{3,2},{5,4},{6,5},{7,6},{9,8},{10,9},{11,10},{13,12},{... | collective-permute-start | bytes 294920 | tf_op jit(solution)/shard_map/ppermute | solution.py:19
  13.2 6.3 %collective-permute-start.1 = (bf16[8,2,16,192]{3,2,1,0:T(8,128)(2,1)S(1)}, bf16[8,2,16,192]{3,2,1,0:T(8,128)(2,1)S(1)}, u32[]{:S(2)}, u32[]{:S(2)}) collective-permute-start(bf16[8,2,16,192]{3,2,1,0:T(8,128)(2,1)S(1)} %get-tuple-element.6), channel_id=1, source_target_pairs={{0,1},{1,2},{2,3},{4,5},{5,6},{6,7},{8,9},{9,10},{10,11},{12,13},{... | collective-permute-start | bytes 294920 | tf_op jit(solution)/shard_map/ppermute | solution.py:19
  16.2 3.3 %copy-start.1 = (bf16[8,2,16,192]{3,2,1,0:T(8,128)(2,1)}, bf16[8,2,16,192]{3,2,1,0:T(8,128)(2,1)S(1)}, u32[]{:S(2)}) copy-start(bf16[8,2,16,192]{3,2,1,0:T(8,128)(2,1)S(1)} %collective-permute-done.2.bottom) | copy-start | bytes 294916
  19.5 0.6 %copy-start.2 = (bf16[8,2,16,192]{3,2,1,0:T(8,128)(2,1)}, bf16[8,2,16,192]{3,2,1,0:T(8,128)(2,1)S(1)}, u32[]{:S(2)}) copy-start(bf16[8,2,16,192]{3,2,1,0:T(8,128)(2,1)S(1)} %collective-permute-done.1.top) | copy-start | bytes 294916

commit v5 on v4

v5 whole, which is shorter than its diff:
```python
import functools

import jax
import jax.numpy as jnp
from jax import lax
from jax.experimental import pallas as pl
from jax.experimental.pallas import tpu as pltpu
from jax.sharding import PartitionSpec as P


def silu(value):
    value = value.astype(jnp.float32)
    return value / (1 + jnp.exp(-value))


def neighbour(value, axis, step):
    size = lax.axis_size(axis)
    pairs = [(i, i + step) for i in range(size) if 0 <= i + step < size]
    return lax.ppermute(value, axis, pairs)


def spread_taps(flat, cols, rows, buf):
    count, lanes = flat.shape
    col = lax.broadcasted_iota(jnp.int32, flat.shape, 0) % cols
    shifted = (
        jnp.where(col == 0, 0.0, pltpu.roll(flat, 1, 0)),
        flat,
        jnp.where(col == cols - 1, 0.0, pltpu.roll(flat, count - 1, 0)),
    )
    frames = buf.shape[0]
    for e in range(3):
        value = shifted[e].astype(jnp.bfloat16).reshape(frames, rows + 2, cols, lanes)
        for b in range(3):
            k = 3 * b + e
            buf[:, :, :, k * lanes : (k + 1) * lanes] = value[:, b : b + rows]


def conv_time_taps(buf, weight, frames):
    rows, cols, depth = buf.shape[1], buf.shape[2], buf.shape[3]
    total = None
    for a in range(3):
        lhs = buf[a : a + frames].reshape(frames * rows * cols, depth)
        term = jnp.dot(lhs, weight[a], preferred_element_type=jnp.float32)
        total = term if total is None else total + term
    return total


def block_kernel(
    flags, earlier, own, top, bottom, w_first, b_first, w_second, b_second, out, field, buf1, gated, buf2
):
    frames, rows, cols, chans = own.shape
    lanes = field.shape[3]
    field[:, :, :, chans:] = jnp.zeros(field.shape[:3] + (lanes - chans,), jnp.float32)
    field[0:frames, 2 : rows + 2, :, 0:chans] = silu(earlier[...])
    field[frames:, 2 : rows + 2, :, 0:chans] = silu(own[...])
    field[:, 0:2, :, 0:chans] = silu(top[...])
    field[:, rows + 2 :, :, 0:chans] = silu(bottom[...])
    spread_taps(field[...].reshape(2 * frames * (rows + 4) * cols, lanes), cols, rows + 2, buf1)
    hidden = conv_time_taps(buf1, w_first, frames + 2) + b_first[...]
    gated[...] = silu(hidden).reshape(frames + 2, rows + 2, cols, lanes)

    @pl.when(flags[0] != 0)
    def _():
        gated[0:2] = jnp.zeros((2, rows + 2, cols, lanes), jnp.float32)

    @pl.when(flags[1] != 0)
    def _():
        gated[:, 0:1] = jnp.zeros((frames + 2, 1, cols, lanes), jnp.float32)

    @pl.when(flags[2] != 0)
    def _():
        gated[:, rows + 1 :] = jnp.zeros((frames + 2, 1, cols, lanes), jnp.float32)

    spread_taps(gated[...].reshape((frames + 2) * (rows + 2) * cols, lanes), cols, rows, buf2)
    second = conv_time_taps(buf2, w_second, frames) + b_second[...]
    result = own[...].astype(jnp.float32).reshape(frames * rows * cols, chans) + second
    out[...] = result.astype(jnp.bfloat16).reshape(frames, rows, cols, chans)


def block(flags, earlier, own, top, bottom, w_first, b_first, w_second, b_second):
    frames, rows, cols, chans = own.shape
    lanes = -(-chans // 256) * 256
    extra = lanes - chans
    w_first = jnp.pad(w_first, ((0, 0),) * 3 + ((0, extra), (0, extra))).reshape(3, 9 * lanes, lanes)
    w_second = jnp.pad(w_second, ((0, 0),) * 3 + ((0, extra), (0, 0))).reshape(3, 9 * lanes, chans)
    b_first = jnp.pad(b_first, (0, extra)).reshape(1, lanes)
    positions = (frames + 2) * (rows + 2) * cols + frames * rows * cols
    vmem = pl.BlockSpec(memory_space=pltpu.VMEM)
    return pl.pallas_call(
        block_kernel,
        out_shape=jax.ShapeDtypeStruct(own.shape, own.dtype),
        in_specs=[pl.BlockSpec(memory_space=pltpu.SMEM)] + [vmem] * 8,
        out_specs=vmem,
        scratch_shapes=[
            pltpu.VMEM((2 * frames, rows + 4, cols, lanes), jnp.float32),
            pltpu.VMEM((2 * frames, rows + 2, cols, 9 * lanes), jnp.bfloat16),
            pltpu.VMEM((frames + 2, rows + 2, cols, lanes), jnp.float32),
            pltpu.VMEM((frames + 2, rows, cols, 9 * lanes), jnp.bfloat16),
        ],
        compiler_params=pltpu.CompilerParams(vmem_limit_bytes=48 * 1024 * 1024),
        cost_estimate=pl.CostEstimate(
            flops=2 * positions * 27 * chans * chans,
            transcendentals=2 * positions * chans,
            bytes_accessed=2 * (54 * lanes * lanes + 4 * own.size),
        ),
    )(flags, earlier, own, top, bottom, w_first, b_first, w_second, b_second.reshape(1, chans))


def local(clip_frames, w_first, b_first, w_second, b_second):
    rows = clip_frames.shape[1]
    x = clip_frames
    earlier = neighbour(x, "tm", 1)
    extended = jnp.concatenate([earlier, x], 0)
    top = neighbour(extended[:, rows - 2 :], "height", 1)
    bottom = neighbour(extended[:, :2], "height", -1)
    t, h = lax.axis_index("tm"), lax.axis_index("height")
    flags = jnp.stack([t == 0, h == 0, h == lax.axis_size("height") - 1]).astype(jnp.int32)
    return block(flags, earlier, x, top, bottom, w_first, b_first, w_second, b_second)


def solution(mesh):
    return jax.shard_map(
        local,
        mesh=mesh,
        in_specs=(P(("clips", "tm"), "height", None, None), P(), P(), P(), P()),
        out_specs=P(("clips", "tm"), "height", None, None),
        check_vma=False,
    )
```

time: 33.6 us -> 31.1 us (0.926)
  waiting for transfers between devices: 9.93 us -> 5.6 us
  local copies, waits for them, and re-layouts: 1.75 us -> 4.86 us
  Pallas kernels: 13.3 us -> 12.2 us
  other arithmetic: 0.58 us -> 0.08 us
    pad x0 -> x3, local copies, waits for them, and re-layouts: none -> 4.78 us  [the longest x1 2.42 us: block(): jnp.pad(w_first, ((0, 0),) * 3 + ((0, extra), (0, extra)))]
    ppermute x3, waiting for transfers between devices: 9.93 us -> 5.6 us  [neighbour(): return lax.ppermute(value, axis, pairs)]
    pallas_call x1, Pallas kernels: 13.3 us -> 12.2 us  [block(): pl.pallas_call(block_kernel, out_shape=jax.ShapeDtypeStruct(own.shape, ow...]
    concatenate x1, local copies, waits for them, and re-layouts: 1.06 us -> 0.02 us  [local(): extended = jnp.concatenate([earlier, x], 0)]
    unnamed x7 -> x9, local copies, waits for them, and re-layouts: 0.67 us -> 0.04 us
    convert_element_type x1, other arithmetic: 0.58 us -> 0.08 us  [local(): jnp.stack([t == 0, h == 0, h == lax.axis_size('height') - 1])]
  transfers between devices with their start and end apart: 3 -> 3, of which waited for: 2 -> 2; matrix products, arithmetic and copies ran while one was open for 2% -> 16% of each run, Pallas kernels for 0% -> 0%
where the time goes in v5:
time: 31.1 us; the launch traced here: 30.9 us
  Pallas kernels  12.2 us (39%)
  starting transfers between devices  8.07 us (26%)
  waiting for transfers between devices  5.6 us (18%)
  local copies, waits for them, and re-layouts  4.86 us (16%)
    pallas_call x1, Pallas kernels, block(): pl.pallas_call(block_kernel, out_shape=jax.ShapeDtypeStruct(own.shape, ow...  12.2 us
    ppermute x3, starting transfers between devices, neighbour(): return lax.ppermute(value, axis, pairs)  8.07 us
    ppermute x3, waiting for transfers between devices, neighbour(): return lax.ppermute(value, axis, pairs)  5.6 us
    pad x1, local copies, waits for them, and re-layouts, block(): jnp.pad(w_first, ((0, 0),) * 3 + ((0, extra), (0, extra)))  2.42 us
    pad x1, local copies, waits for them, and re-layouts, block(): jnp.pad(w_second, ((0, 0),) * 3 + ((0, extra), (0, 0)))  2.36 us
  transfers between devices with their start and end apart: 3, of which 2 were waited for; matrix products, arithmetic and copies ran while one was open for 16% of the time, Pallas kernels for 0%

profile of v5, /device:TPU:10, one launch (start us, length us, event | category | flops | bytes accessed | tf_op | source)
XLA Modules:
  0.0 30.9 jit_solution(4819714969624811480)
XLA Ops:
  0.0 0.0 copy-start.2
  0.0 3.7 %collective-permute-start = (bf16[4,8,16,192]{3,2,1,0:T(8,128)(2,1)}, bf16[4,8,16,192]{3,2,1,0:T(8,128)(2,1)S(1)}, u32[]{:S(2)}, u32[]{:S(2)}) collective-permute-start(bf16[4,8,16,192]{3,2,1,0:T(8,128)(2,1)} %own.1), channel_id=1, source_target_pairs={{0,4},{4,8},{8,12},{1,5},{5,9},{9,13},{2,6},{6,10},{10,14},{3,7},{... | collective-permute-start | bytes 589832 | tf_op jit(solution)/shard_map/ppermute | solution.py:19
  3.8 2.4 %pad.12 = bf16[3,3,3,256,256]{4,3,2,1,0:T(8,128)(2,1)S(1)} pad(bf16[3,3,3,192,192]{4,3,2,1,0:T(8,128)(2,1)} %param.6, bf16[]{:T(256)} %constant.13.clone.1), padding=0_0x0_0x0_0x0_64x0_64 | pad | bytes 5529602 | tf_op jit(solution)/shard_map/jit(_pad)/pad | solution.py:84
  6.2 0.0 copy-done.2
  6.2 0.0 copy-start.3
  6.2 0.0 copy-start
  6.2 0.0 copy-start.1
  6.2 2.4 %pad.14 = bf16[3,3,3,256,192]{4,3,2,1,0:T(8,128)(2,1)} pad(bf16[3,3,3,192,192]{4,3,2,1,0:T(8,128)(2,1)S(1)} %copy-done.2, bf16[]{:T(256)} %constant.13.clone.1), padding=0_0x0_0x0_0x0_64x0_0 | pad | bytes 4644866 | tf_op jit(solution)/shard_map/jit(_pad)/pad | solution.py:85
  8.6 0.0 copy-done.3
  8.6 1.8 %collective-permute-done.earlier = bf16[4,8,16,192]{3,2,1,0:T(8,128)(2,1)S(1)} collective-permute-done((bf16[4,8,16,192]{3,2,1,0:T(8,128)(2,1)}, bf16[4,8,16,192]{3,2,1,0:T(8,128)(2,1)S(1)}, u32[]{:S(2)}, u32[]{:S(2)}) %collective-permute-start) | collective-permute-done | bytes 196640 | tf_op jit(solution)/shard_map/ppermute | solution.py:19
  10.4 0.0 copy-done
  10.5 1.9 %collective-permute-start.2 = (bf16[8,2,16,192]{3,2,1,0:T(8,128)(2,1)S(1)}, bf16[8,2,16,192]{3,2,1,0:T(8,128)(2,1)S(1)}, u32[]{:S(2)}, u32[]{:S(2)}) collective-permute-start(bf16[8,2,16,192]{3,2,1,0:T(8,128)(2,1)S(1)} %get-tuple-element.5), channel_id=1, source_target_pairs={{1,0},{2,1},{3,2},{5,4},{6,5},{7,6},{9,8},{10,9},{11,10},{13,12},{... | collective-permute-start | bytes 294920 | tf_op jit(solution)/shard_map/ppermute | solution.py:19
  12.4 2.4 %collective-permute-start.1 = (bf16[8,2,16,192]{3,2,1,0:T(8,128)(2,1)S(1)}, bf16[8,2,16,192]{3,2,1,0:T(8,128)(2,1)S(1)}, u32[]{:S(2)}, u32[]{:S(2)}) collective-permute-start(bf16[8,2,16,192]{3,2,1,0:T(8,128)(2,1)S(1)} %get-tuple-element.6), channel_id=1, source_target_pairs={{0,1},{1,2},{2,3},{4,5},{5,6},{6,7},{8,9},{9,10},{10,11},{12,13},{... | collective-permute-start | bytes 294920 | tf_op jit(solution)/shard_map/ppermute | solution.py:19
  14.8 0.1 add_convert_fusion.flags
  14.9 0.0 collective-permute-done.2.bottom
  14.9 3.8 %collective-permute-done.1.top = bf16[8,2,16,192]{3,2,1,0:T(8,128)(2,1)S(1)} collective-permute-done((bf16[8,2,16,192]{3,2,1,0:T(8,128)(2,1)S(1)}, bf16[8,2,16,192]{3,2,1,0:T(8,128)(2,1)S(1)}, u32[]{:S(2)}, u32[]{:S(2)}) %collective-permute-start.1) | collective-permute-done | bytes 98336 | tf_op jit(solution)/shard_map/ppermute | solution.py:19
  18.7 0.0 copy-done.1
  18.7 12.2 %shard_map.55 = bf16[4,8,16,192]{3,2,1,0:T(8,128)(2,1)} custom-call(s32[3]{0:T(128)S(1)} %add_convert_fusion.flags, bf16[4,8,16,192]{3,2,1,0:T(8,128)(2,1)S(1)} %collective-permute-done.earlier, bf16[4,8,16,192]{3,2,1,0:T(8,128)(2,1)S(1)} %copy-done, bf16[8,2,16,192]{3,2,1,0:T(8,128)(2,1)S(1)} %collective-permute-done.1.top, ...), custom_call_target="tpu_custom_call" | custom-call | flops 2930245632 | bytes 7864320 | tf_op jit(solution)/shard_map/pallas_call | solution.py:89
  (4 shorter events, 0.1 us)
Async XLA Ops:
  0.0 6.2 %copy-start.2 = (bf16[3,3,3,192,192]{4,3,2,1,0:T(8,128)(2,1)S(1)}, bf16[3,3,3,192,192]{4,3,2,1,0:T(8,128)(2,1)}, u32[]{:S(2)}) copy-start(bf16[3,3,3,192,192]{4,3,2,1,0:T(8,128)(2,1)} %param.8) | copy-start | bytes 5971972
  0.0 10.4 %collective-permute-start = (bf16[4,8,16,192]{3,2,1,0:T(8,128)(2,1)}, bf16[4,8,16,192]{3,2,1,0:T(8,128)(2,1)S(1)}, u32[]{:S(2)}, u32[]{:S(2)}) collective-permute-start(bf16[4,8,16,192]{3,2,1,0:T(8,128)(2,1)} %own.1), channel_id=1, source_target_pairs={{0,4},{4,8},{8,12},{1,5},{5,9},{9,13},{2,6},{6,10},{10,14},{3,7},{... | collective-permute-start | bytes 589832 | tf_op jit(solution)/shard_map/ppermute | solution.py:19
  6.2 2.4 %copy-start.3 = (f32[192]{0:T(256)S(1)}, f32[192]{0:T(256)}, u32[]{:S(2)}) copy-start(f32[192]{0:T(256)} %param.7) | copy-start | bytes 2308
  6.2 4.2 %copy-start = (bf16[4,8,16,192]{3,2,1,0:T(8,128)(2,1)S(1)}, bf16[4,8,16,192]{3,2,1,0:T(8,128)(2,1)}, u32[]{:S(2)}) copy-start(bf16[4,8,16,192]{3,2,1,0:T(8,128)(2,1)} %own.1) | copy-start | bytes 589828
  6.2 12.5 %copy-start.1 = (f32[192]{0:T(256)S(1)}, f32[192]{0:T(256)}, u32[]{:S(2)}) copy-start(f32[192]{0:T(256)} %param.9) | copy-start | bytes 2308
  10.5 4.4 %collective-permute-start.2 = (bf16[8,2,16,192]{3,2,1,0:T(8,128)(2,1)S(1)}, bf16[8,2,16,192]{3,2,1,0:T(8,128)(2,1)S(1)}, u32[]{:S(2)}, u32[]{:S(2)}) collective-permute-start(bf16[8,2,16,192]{3,2,1,0:T(8,128)(2,1)S(1)} %get-tuple-element.5), channel_id=1, source_target_pairs={{1,0},{2,1},{3,2},{5,4},{6,5},{7,6},{9,8},{10,9},{11,10},{13,12},{... | collective-permute-start | bytes 294920 | tf_op jit(solution)/shard_map/ppermute | solution.py:19
  12.4 6.3 %collective-permute-start.1 = (bf16[8,2,16,192]{3,2,1,0:T(8,128)(2,1)S(1)}, bf16[8,2,16,192]{3,2,1,0:T(8,128)(2,1)S(1)}, u32[]{:S(2)}, u32[]{:S(2)}) collective-permute-start(bf16[8,2,16,192]{3,2,1,0:T(8,128)(2,1)S(1)} %get-tuple-element.6), channel_id=1, source_target_pairs={{0,1},{1,2},{2,3},{4,5},{5,6},{6,7},{8,9},{9,10},{10,11},{12,13},{... | collective-permute-start | bytes 294920 | tf_op jit(solution)/shard_map/ppermute | solution.py:19

commit v6 on v5

--- a/solution.py
+++ b/solution.py
@@ -35,14 +35,18 @@
             buf[:, :, :, k * lanes : (k + 1) * lanes] = value[:, b : b + rows]
 
 
-def conv_time_taps(buf, weight, frames):
+def conv_time_taps(buf, weight, frames, chains=2):
     rows, cols, depth = buf.shape[1], buf.shape[2], buf.shape[3]
-    total = None
-    for a in range(3):
-        lhs = buf[a : a + frames].reshape(frames * rows * cols, depth)
-        term = jnp.dot(lhs, weight[a], preferred_element_type=jnp.float32)
-        total = term if total is None else total + term
-    return total
+    bounds = [frames * i // chains for i in range(chains + 1)]
+    parts = []
+    for lo, hi in zip(bounds[:-1], bounds[1:]):
+        total = None
+        for a in range(3):
+            lhs = buf[a + lo : a + hi].reshape((hi - lo) * rows * cols, depth)
+            term = jnp.dot(lhs, weight[a], preferred_element_type=jnp.float32)
+            total = term if total is None else total + term
+        parts.append(total)
+    return jnp.concatenate(parts, 0)
 
 
 def block_kernel(
@@ -72,7 +76,7 @@
         gated[:, rows + 1 :] = jnp.zeros((frames + 2, 1, cols, lanes), jnp.float32)
 
     spread_taps(gated[...].reshape((frames + 2) * (rows + 2) * cols, lanes), cols, rows, buf2)
-    second = conv_time_taps(buf2, w_second, frames) + b_second[...]
+    second = conv_time_taps(buf2, w_second, frames)[:, 0:chans] + b_second[...]
     result = own[...].astype(jnp.float32).reshape(frames * rows * cols, chans) + second
     out[...] = result.astype(jnp.bfloat16).reshape(frames, rows, cols, chans)
 
@@ -82,7 +86,7 @@
     lanes = -(-chans // 256) * 256
     extra = lanes - chans
     w_first = jnp.pad(w_first, ((0, 0),) * 3 + ((0, extra), (0, extra))).reshape(3, 9 * lanes, lanes)
-    w_second = jnp.pad(w_second, ((0, 0),) * 3 + ((0, extra), (0, 0))).reshape(3, 9 * lanes, chans)
+    w_second = jnp.pad(w_second, ((0, 0),) * 3 + ((0, extra), (0, extra))).reshape(3, 9 * lanes, lanes)
     b_first = jnp.pad(b_first, (0, extra)).reshape(1, lanes)
     positions = (frames + 2) * (rows + 2) * cols + frames * rows * cols
     vmem = pl.BlockSpec(memory_space=pltpu.VMEM)

time: 31.1 us -> 27.9 us (0.90)
  Pallas kernels: 12.2 us -> 8.9 us
    pallas_call x1, Pallas kernels: 12.2 us -> 8.9 us  [block(): pl.pallas_call(block_kernel, out_shape=jax.ShapeDtypeStruct(own.shape, ow...]
  transfers between devices with their start and end apart: 3 -> 3, of which waited for: 2 -> 2; matrix products, arithmetic and copies ran while one was open for 16% -> 18% of each run, Pallas kernels for 0% -> 0%
where the time goes in v6:
time: 27.9 us; the launch traced here: 27.6 us
  Pallas kernels  8.9 us (32%)
  starting transfers between devices  8.07 us (29%)
  waiting for transfers between devices  5.6 us (20%)
  local copies, waits for them, and re-layouts  4.86 us (17%)
    pallas_call x1, Pallas kernels, block(): pl.pallas_call(block_kernel, out_shape=jax.ShapeDtypeStruct(own.shape, ow...  8.9 us
    ppermute x3, starting transfers between devices, neighbour(): return lax.ppermute(value, axis, pairs)  8.07 us
    ppermute x3, waiting for transfers between devices, neighbour(): return lax.ppermute(value, axis, pairs)  5.6 us
    pad x1, local copies, waits for them, and re-layouts, block(): jnp.pad(w_first, ((0, 0),) * 3 + ((0, extra), (0, extra)))  2.42 us
    pad x1, local copies, waits for them, and re-layouts, block(): jnp.pad(w_second, ((0, 0),) * 3 + ((0, extra), (0, extra)))  2.36 us
  transfers between devices with their start and end apart: 3, of which 2 were waited for; matrix products, arithmetic and copies ran while one was open for 18% of the time, Pallas kernels for 0%

profile of v6, /device:TPU:10, one launch (start us, length us, event | category | flops | bytes accessed | tf_op | source)
XLA Modules:
  0.0 27.6 jit_solution(5827230544067424432)
XLA Ops:
  0.0 0.0 copy-start.2
  0.0 3.7 %collective-permute-start = (bf16[4,8,16,192]{3,2,1,0:T(8,128)(2,1)}, bf16[4,8,16,192]{3,2,1,0:T(8,128)(2,1)S(1)}, u32[]{:S(2)}, u32[]{:S(2)}) collective-permute-start(bf16[4,8,16,192]{3,2,1,0:T(8,128)(2,1)} %own.1), channel_id=1, source_target_pairs={{0,4},{4,8},{8,12},{1,5},{5,9},{9,13},{2,6},{6,10},{10,14},{3,7},{... | collective-permute-start | bytes 589832 | tf_op jit(solution)/shard_map/ppermute | solution.py:19
  3.8 2.4 %pad.11 = bf16[3,3,3,256,256]{4,3,2,1,0:T(8,128)(2,1)S(1)} pad(bf16[3,3,3,192,192]{4,3,2,1,0:T(8,128)(2,1)} %param.6, bf16[]{:T(256)} %constant.13.clone.1), padding=0_0x0_0x0_0x0_64x0_64 | pad | bytes 5529602 | tf_op jit(solution)/shard_map/jit(_pad)/pad | solution.py:88
  6.2 0.0 copy-done.2
  6.2 0.0 copy-start.3
  6.2 0.0 copy-start
  6.2 0.0 copy-start.1
  6.2 2.4 %pad.13 = bf16[3,3,3,256,256]{4,3,2,1,0:T(8,128)(2,1)} pad(bf16[3,3,3,192,192]{4,3,2,1,0:T(8,128)(2,1)S(1)} %copy-done.2, bf16[]{:T(256)} %constant.13.clone.1), padding=0_0x0_0x0_0x0_64x0_64 | pad | bytes 5529602 | tf_op jit(solution)/shard_map/jit(_pad)/pad | solution.py:89
  8.6 0.0 copy-done.3
  8.6 1.8 %collective-permute-done.earlier = bf16[4,8,16,192]{3,2,1,0:T(8,128)(2,1)S(1)} collective-permute-done((bf16[4,8,16,192]{3,2,1,0:T(8,128)(2,1)}, bf16[4,8,16,192]{3,2,1,0:T(8,128)(2,1)S(1)}, u32[]{:S(2)}, u32[]{:S(2)}) %collective-permute-start) | collective-permute-done | bytes 196640 | tf_op jit(solution)/shard_map/ppermute | solution.py:19
  10.4 0.0 copy-done
  10.5 1.9 %collective-permute-start.2 = (bf16[8,2,16,192]{3,2,1,0:T(8,128)(2,1)S(1)}, bf16[8,2,16,192]{3,2,1,0:T(8,128)(2,1)S(1)}, u32[]{:S(2)}, u32[]{:S(2)}) collective-permute-start(bf16[8,2,16,192]{3,2,1,0:T(8,128)(2,1)S(1)} %get-tuple-element.5), channel_id=1, source_target_pairs={{1,0},{2,1},{3,2},{5,4},{6,5},{7,6},{9,8},{10,9},{11,10},{13,12},{... | collective-permute-start | bytes 294920 | tf_op jit(solution)/shard_map/ppermute | solution.py:19
  12.4 2.4 %collective-permute-start.1 = (bf16[8,2,16,192]{3,2,1,0:T(8,128)(2,1)S(1)}, bf16[8,2,16,192]{3,2,1,0:T(8,128)(2,1)S(1)}, u32[]{:S(2)}, u32[]{:S(2)}) collective-permute-start(bf16[8,2,16,192]{3,2,1,0:T(8,128)(2,1)S(1)} %get-tuple-element.6), channel_id=1, source_target_pairs={{0,1},{1,2},{2,3},{4,5},{5,6},{6,7},{8,9},{9,10},{10,11},{12,13},{... | collective-permute-start | bytes 294920 | tf_op jit(solution)/shard_map/ppermute | solution.py:19
  14.8 0.1 add_convert_fusion.flags
  14.9 0.0 collective-permute-done.2.bottom
  14.9 3.8 %collective-permute-done.1.top = bf16[8,2,16,192]{3,2,1,0:T(8,128)(2,1)S(1)} collective-permute-done((bf16[8,2,16,192]{3,2,1,0:T(8,128)(2,1)S(1)}, bf16[8,2,16,192]{3,2,1,0:T(8,128)(2,1)S(1)}, u32[]{:S(2)}, u32[]{:S(2)}) %collective-permute-start.1) | collective-permute-done | bytes 98336 | tf_op jit(solution)/shard_map/ppermute | solution.py:19
  18.7 0.0 copy-done.1
  18.7 8.9 %shard_map.55 = bf16[4,8,16,192]{3,2,1,0:T(8,128)(2,1)} custom-call(s32[3]{0:T(128)S(1)} %add_convert_fusion.flags, bf16[4,8,16,192]{3,2,1,0:T(8,128)(2,1)S(1)} %collective-permute-done.earlier, bf16[4,8,16,192]{3,2,1,0:T(8,128)(2,1)S(1)} %copy-done, bf16[8,2,16,192]{3,2,1,0:T(8,128)(2,1)S(1)} %collective-permute-done.1.top, ...), custom_call_target="tpu_custom_call" | custom-call | flops 2930245632 | bytes 7864320 | tf_op jit(solution)/shard_map/pallas_call | solution.py:93
  (4 shorter events, 0.1 us)
Async XLA Ops:
  0.0 6.2 %copy-start.2 = (bf16[3,3,3,192,192]{4,3,2,1,0:T(8,128)(2,1)S(1)}, bf16[3,3,3,192,192]{4,3,2,1,0:T(8,128)(2,1)}, u32[]{:S(2)}) copy-start(bf16[3,3,3,192,192]{4,3,2,1,0:T(8,128)(2,1)} %param.8) | copy-start | bytes 5971972
  0.0 10.4 %collective-permute-start = (bf16[4,8,16,192]{3,2,1,0:T(8,128)(2,1)}, bf16[4,8,16,192]{3,2,1,0:T(8,128)(2,1)S(1)}, u32[]{:S(2)}, u32[]{:S(2)}) collective-permute-start(bf16[4,8,16,192]{3,2,1,0:T(8,128)(2,1)} %own.1), channel_id=1, source_target_pairs={{0,4},{4,8},{8,12},{1,5},{5,9},{9,13},{2,6},{6,10},{10,14},{3,7},{... | collective-permute-start | bytes 589832 | tf_op jit(solution)/shard_map/ppermute | solution.py:19
  6.2 2.4 %copy-start.3 = (f32[192]{0:T(256)S(1)}, f32[192]{0:T(256)}, u32[]{:S(2)}) copy-start(f32[192]{0:T(256)} %param.7) | copy-start | bytes 2308
  6.2 4.2 %copy-start = (bf16[4,8,16,192]{3,2,1,0:T(8,128)(2,1)S(1)}, bf16[4,8,16,192]{3,2,1,0:T(8,128)(2,1)}, u32[]{:S(2)}) copy-start(bf16[4,8,16,192]{3,2,1,0:T(8,128)(2,1)} %own.1) | copy-start | bytes 589828
  6.2 12.5 %copy-start.1 = (f32[192]{0:T(256)S(1)}, f32[192]{0:T(256)}, u32[]{:S(2)}) copy-start(f32[192]{0:T(256)} %param.9) | copy-start | bytes 2308
  10.5 4.4 %collective-permute-start.2 = (bf16[8,2,16,192]{3,2,1,0:T(8,128)(2,1)S(1)}, bf16[8,2,16,192]{3,2,1,0:T(8,128)(2,1)S(1)}, u32[]{:S(2)}, u32[]{:S(2)}) collective-permute-start(bf16[8,2,16,192]{3,2,1,0:T(8,128)(2,1)S(1)} %get-tuple-element.5), channel_id=1, source_target_pairs={{1,0},{2,1},{3,2},{5,4},{6,5},{7,6},{9,8},{10,9},{11,10},{13,12},{... | collective-permute-start | bytes 294920 | tf_op jit(solution)/shard_map/ppermute | solution.py:19
  12.4 6.3 %collective-permute-start.1 = (bf16[8,2,16,192]{3,2,1,0:T(8,128)(2,1)S(1)}, bf16[8,2,16,192]{3,2,1,0:T(8,128)(2,1)S(1)}, u32[]{:S(2)}, u32[]{:S(2)}) collective-permute-start(bf16[8,2,16,192]{3,2,1,0:T(8,128)(2,1)S(1)} %get-tuple-element.6), channel_id=1, source_target_pairs={{0,1},{1,2},{2,3},{4,5},{5,6},{6,7},{8,9},{9,10},{10,11},{12,13},{... | collective-permute-start | bytes 294920 | tf_op jit(solution)/shard_map/ppermute | solution.py:19

commit v7 on v6

--- a/solution.py
+++ b/solution.py
@@ -110,13 +110,24 @@
     )(flags, earlier, own, top, bottom, w_first, b_first, w_second, b_second.reshape(1, chans))
 
 
+def row_exchange(value, rows_up, rows_down):
+    size = lax.axis_size("height")
+    h = lax.axis_index("height")
+    peer = lax.broadcasted_iota(jnp.int32, (size,) + (1,) * value.ndim, 0)
+    send = jnp.where(peer == h + 1, value[:, value.shape[1] - rows_up :][None], 0)
+    send = jnp.where(peer == h - 1, value[:, :rows_down][None], send)
+    got = lax.all_to_all(send, "height", 0, 0, tiled=False)
+    top = lax.dynamic_index_in_dim(got, (h + size - 1) % size, 0, keepdims=False)
+    bottom = lax.dynamic_index_in_dim(got, (h + 1) % size, 0, keepdims=False)
+    top = jnp.where(h > 0, top, 0)
+    bottom = jnp.where(h < size - 1, bottom, 0)
+    return top, bottom
+
+
 def local(clip_frames, w_first, b_first, w_second, b_second):
-    rows = clip_frames.shape[1]
     x = clip_frames
     earlier = neighbour(x, "tm", 1)
-    extended = jnp.concatenate([earlier, x], 0)
-    top = neighbour(extended[:, rows - 2 :], "height", 1)
-    bottom = neighbour(extended[:, :2], "height", -1)
+    top, bottom = row_exchange(jnp.concatenate([earlier, x], 0), 2, 2)
     t, h = lax.axis_index("tm"), lax.axis_index("height")
     flags = jnp.stack([t == 0, h == 0, h == lax.axis_size("height") - 1]).astype(jnp.int32)
     return block(flags, earlier, x, top, bottom, w_first, b_first, w_second, b_second)

time: 27.9 us -> 38 us (1.36)
  the two profiles are of different devices: /device:TPU:10 before, /device:TPU:0 now
where the time goes in v7:
time: 38 us; the launch traced here: 37.6 us
  local copies, waits for them, and re-layouts  9.47 us (25%)
  starting transfers between devices  9.08 us (24%)
  Pallas kernels  8.88 us (23%)
  waiting for transfers between devices  8.1 us (21%)
  other arithmetic  1.98 us (5%)
    pallas_call x1, Pallas kernels, block(): pl.pallas_call(block_kernel, out_shape=jax.ShapeDtypeStruct(own.shape, ow...  8.88 us
    ppermute x1, waiting for transfers between devices, neighbour(): return lax.ppermute(value, axis, pairs)  5.83 us
    ppermute x1, starting transfers between devices, neighbour(): return lax.ppermute(value, axis, pairs)  4.93 us
    all_to_all x1, starting transfers between devices, row_exchange(): got = lax.all_to_all(send, 'height', 0, 0, tiled=False)  4.14 us
    pad x1, local copies, waits for them, and re-layouts, block(): jnp.pad(w_second, ((0, 0),) * 3 + ((0, extra), (0, extra)))  4.12 us
    pad x1, local copies, waits for them, and re-layouts, block(): jnp.pad(w_first, ((0, 0),) * 3 + ((0, extra), (0, extra)))  2.34 us
    all_to_all x1, waiting for transfers between devices, row_exchange(): got = lax.all_to_all(send, 'height', 0, 0, tiled=False)  2.28 us
    unnamed x11, local copies, waits for them, and re-layouts  1.93 us
  transfers between devices with their start and end apart: 2, of which 2 were waited for; matrix products, arithmetic and copies ran while one was open for 17% of the time, Pallas kernels for 0%

profile of v7, /device:TPU:0, one launch (start us, length us, event | category | flops | bytes accessed | tf_op | source)
XLA Modules:
  0.0 37.6 jit_solution(17488852669968435712)
XLA Ops:
  0.0 4.9 %collective-permute-start = (bf16[4,8,16,192]{3,2,1,0:T(8,128)(2,1)}, bf16[4,8,16,192]{3,2,1,0:T(8,128)(2,1)S(1)}, u32[]{:S(2)}, u32[]{:S(2)}) collective-permute-start(bf16[4,8,16,192]{3,2,1,0:T(8,128)(2,1)} %own.1), channel_id=1, source_target_pairs={{0,4},{4,8},{8,12},{1,5},{5,9},{9,13},{2,6},{6,10},{10,14},{3,7},{... | collective-permute-start | bytes 589832 | tf_op jit(solution)/shard_map/ppermute | solution.py:19
  5.0 5.8 %collective-permute-done.earlier = bf16[4,8,16,192]{3,2,1,0:T(8,128)(2,1)S(1)} collective-permute-done((bf16[4,8,16,192]{3,2,1,0:T(8,128)(2,1)}, bf16[4,8,16,192]{3,2,1,0:T(8,128)(2,1)S(1)}, u32[]{:S(2)}, u32[]{:S(2)}) %collective-permute-start) | collective-permute-done | bytes 196640 | tf_op jit(solution)/shard_map/ppermute | solution.py:19
  10.8 0.0 copy-start.1
  10.8 1.1 %constant_dynamic-update-slice_fusion = bf16[8,8,16,192]{3,2,1,0:T(8,128)(2,1)S(1)} fusion(bf16[8,8,16,192]{3,2,1,0:T(8,128)(2,1)S(1)} %constant_dynamic-update-slice_fusion.1, bf16[4,8,16,192]{3,2,1,0:T(8,128)(2,1)} %own.1), kind=kLoop, calls=%fused_computation.3 | loop fusion | bytes 458752 | tf_op jit(solution)/shard_map/concatenate | solution.py:130
  11.9 0.9 %select_select_fusion = bf16[4,8,2,16,192]{4,3,2,1,0:T(8,128)(2,1)} fusion(pred[4]{0:T(512)(128)(4,1)S(1)} %get-tuple-element.9, pred[4]{0:T(512)(128)(4,1)S(1)} %get-tuple-element.10, bf16[8,2,16,192]{3,2,1,0:T(8,128)(2,1)S(1)} %get-tuple-element.8, bf16[8,2,16,192]{3,2,1,0:T(8,128)(2,1)S(1)} %get-tuple-element.7), kind=kLoop, calls=%fused_computation | loop fusion | flops 393216 | bytes 589832 | tf_op jit(solution)/shard_map/jit(_where)/select_n | solution.py:118
  12.8 4.1 %all-to-all-start = ((bf16[4,8,2,16,192]{4,3,2,1,0:T(8,128)(2,1)}), bf16[4,8,2,16,192]{4,3,2,1,0:T(8,128)(2,1)}, u32[]{:S(2)}, u32[]{:S(2)}) async-start(bf16[4,8,2,16,192]{4,3,2,1,0:T(8,128)(2,1)} %select_select_fusion), calls=%async_computation | async-start | bytes 1048576 | tf_op jit(solution)/shard_map/all_to_all | solution.py:119
  17.0 0.0 copy-done.1
  17.0 2.3 %pad.11 = bf16[3,3,3,256,256]{4,3,2,1,0:T(8,128)(2,1)S(1)} pad(bf16[3,3,3,192,192]{4,3,2,1,0:T(8,128)(2,1)} %param.6, bf16[]{:T(256)} %constant.39.clone.1), padding=0_0x0_0x0_0x0_64x0_64 | pad | bytes 5529602 | tf_op jit(solution)/shard_map/jit(_pad)/pad | solution.py:88
  19.4 0.0 copy-start.4
  19.4 0.0 copy-start.3
  19.4 4.1 %pad.13 = bf16[3,3,3,256,256]{4,3,2,1,0:T(8,128)(2,1)} pad(bf16[3,3,3,192,192]{4,3,2,1,0:T(8,128)(2,1)} %param.8, bf16[]{:T(256)} %constant.39.clone.1), padding=0_0x0_0x0_0x0_64x0_64 | pad | bytes 5529602 | tf_op jit(solution)/shard_map/jit(_pad)/pad | solution.py:89
  23.5 0.0 copy-done.4
  23.5 0.1 add_convert_fusion.flags
  23.6 2.3 %all-to-all-done = bf16[4,8,2,16,192]{4,3,2,1,0:T(8,128)(2,1)} async-done(((bf16[4,8,2,16,192]{4,3,2,1,0:T(8,128)(2,1)}), bf16[4,8,2,16,192]{4,3,2,1,0:T(8,128)(2,1)}, u32[]{:S(2)}, u32[]{:S(2)}) %all-to-all-start) | async-done | bytes 393248 | tf_op jit(solution)/shard_map/all_to_all | solution.py:119
  25.9 1.0 %select_bitcast_fusion = (bf16[8,2,16,192]{3,2,1,0:T(8,128)(2,1)S(1)}, bf16[8,2,16,192]{3,2,1,0:T(8,128)(2,1)S(1)}) fusion(bf16[4,8,2,16,192]{4,3,2,1,0:T(8,128)(2,1)} %all-to-all-done, s32[]{:T(128)S(6)} %select_n.53, pred[]{:T(512)S(6)} %lt.22, s32[]{:T(128)S(6)} %select_n.48, pred[]{:T(512)S(6)} %gt.3), kind=kLoop, calls=%fused_computation.1 | loop fusion | flops 98304 | bytes 393226 | tf_op jit(solution)/shard_map/jit(_where)/select_n | solution.py:123
  26.9 0.0 copy-done.3
  26.9 0.0 copy-start
  26.9 0.9 %copy-done = bf16[4,8,16,192]{3,2,1,0:T(8,128)(2,1)S(1)} copy-done((bf16[4,8,16,192]{3,2,1,0:T(8,128)(2,1)S(1)}, bf16[4,8,16,192]{3,2,1,0:T(8,128)(2,1)}, u32[]{:S(2)}) %copy-start) | copy-done | bytes 196632
  27.8 0.0 copy-start.2
  27.8 0.9 %copy-done.2 = bf16[4,8,16,192]{3,2,1,0:T(8,128)(2,1)S(1)} copy-done((bf16[4,8,16,192]{3,2,1,0:T(8,128)(2,1)S(1)}, bf16[4,8,16,192]{3,2,1,0:T(8,128)(2,1)}, u32[]{:S(2)}) %copy-start.2) | copy-done | bytes 196632
  28.8 8.9 %shard_map.55 = bf16[4,8,16,192]{3,2,1,0:T(8,128)(2,1)} custom-call(s32[3]{0:T(128)S(1)} %add_convert_fusion.flags, bf16[4,8,16,192]{3,2,1,0:T(8,128)(2,1)S(1)} %copy-done.2, bf16[4,8,16,192]{3,2,1,0:T(8,128)(2,1)S(1)} %copy-done, bf16[8,2,16,192]{3,2,1,0:T(8,128)(2,1)S(1)} %get-tuple-element.6.top, bf16[8,2,16,192]{3,2,1,0:T(8,128)(2,1)S(1)} %get-tuple-element.5.bottom, ...), custom_call_target="tpu_custom_call" | custom-call | flops 2930245632 | bytes 7864320 | tf_op jit(solution)/shard_map/pallas_call | solution.py:93
  (4 shorter events, 0.0 us)
Async XLA Ops:
  0.0 10.8 %collective-permute-start = (bf16[4,8,16,192]{3,2,1,0:T(8,128)(2,1)}, bf16[4,8,16,192]{3,2,1,0:T(8,128)(2,1)S(1)}, u32[]{:S(2)}, u32[]{:S(2)}) collective-permute-start(bf16[4,8,16,192]{3,2,1,0:T(8,128)(2,1)} %own.1), channel_id=1, source_target_pairs={{0,4},{4,8},{8,12},{1,5},{5,9},{9,13},{2,6},{6,10},{10,14},{3,7},{... | collective-permute-start | bytes 589832 | tf_op jit(solution)/shard_map/ppermute | solution.py:19
  10.8 6.2 %copy-start.1 = (bf16[4,8,16,192]{3,2,1,0:T(8,128)(2,1)}, bf16[4,8,16,192]{3,2,1,0:T(8,128)(2,1)S(1)}, u32[]{:S(2)}) copy-start(bf16[4,8,16,192]{3,2,1,0:T(8,128)(2,1)S(1)} %collective-permute-done.earlier) | copy-start | bytes 589828
  12.8 13.1 %all-to-all-start = ((bf16[4,8,2,16,192]{4,3,2,1,0:T(8,128)(2,1)}), bf16[4,8,2,16,192]{4,3,2,1,0:T(8,128)(2,1)}, u32[]{:S(2)}, u32[]{:S(2)}) async-start(bf16[4,8,2,16,192]{4,3,2,1,0:T(8,128)(2,1)} %select_select_fusion), calls=%async_computation | async-start | bytes 1048576 | tf_op jit(solution)/shard_map/all_to_all | solution.py:119
  19.4 4.1 %copy-start.4 = (f32[192]{0:T(256)S(1)}, f32[192]{0:T(256)}, u32[]{:S(2)}) copy-start(f32[192]{0:T(256)} %param.7) | copy-start | bytes 2308
  19.4 7.5 %copy-start.3 = (f32[192]{0:T(256)S(1)}, f32[192]{0:T(256)}, u32[]{:S(2)}) copy-start(f32[192]{0:T(256)} %param.9) | copy-start | bytes 2308
  26.9 1.0 %copy-start = (bf16[4,8,16,192]{3,2,1,0:T(8,128)(2,1)S(1)}, bf16[4,8,16,192]{3,2,1,0:T(8,128)(2,1)}, u32[]{:S(2)}) copy-start(bf16[4,8,16,192]{3,2,1,0:T(8,128)(2,1)} %own.1) | copy-start | bytes 589828
  27.8 0.9 %copy-start.2 = (bf16[4,8,16,192]{3,2,1,0:T(8,128)(2,1)S(1)}, bf16[4,8,16,192]{3,2,1,0:T(8,128)(2,1)}, u32[]{:S(2)}) copy-start(bf16[4,8,16,192]{3,2,1,0:T(8,128)(2,1)} %copy-done.1) | copy-start | bytes 589828

commit v8 on v6

--- a/solution.py
+++ b/solution.py
@@ -28,11 +28,28 @@
         jnp.where(col == cols - 1, 0.0, pltpu.roll(flat, count - 1, 0)),
     )
     frames = buf.shape[0]
-    for e in range(3):
-        value = shifted[e].astype(jnp.bfloat16).reshape(frames, rows + 2, cols, lanes)
-        for b in range(3):
-            k = 3 * b + e
-            buf[:, :, :, k * lanes : (k + 1) * lanes] = value[:, b : b + rows]
+    view = (frames, rows + 2, cols, 128)
+    low = [v[:, 0:128].astype(jnp.bfloat16).reshape(view) for v in shifted]
+    high = [v[:, 128:256] for v in shifted]
+    turned = [pltpu.roll(v, 64, 1) for v in high]
+    for k in range(9):
+        b, e = divmod(k, 3)
+        buf[:, :, :, 128 * k : 128 * (k + 1)] = low[e][:, b : b + rows]
+    for j in range(5):
+        b, e = divmod(2 * j, 3)
+        packed = high[e].reshape(view)[:, b : b + rows]
+        if 2 * j + 1 < 9:
+            b, e = divmod(2 * j + 1, 3)
+            packed = packed + turned[e].reshape(view)[:, b : b + rows]
+        buf[:, :, :, 128 * (9 + j) : 128 * (10 + j)] = packed.astype(jnp.bfloat16)
+
+
+def dense_weight(weight, lanes):
+    taps, chans, out = 9, weight.shape[3], weight.shape[4]
+    weight = weight.reshape(3, taps, chans, out)
+    low = weight[:, :, 0:128].reshape(3, taps * 128, out)
+    high = jnp.pad(weight[:, :, 128:], ((0, 0), (0, 1), (0, 0), (0, 0))).reshape(3, (taps + 1) * (chans - 128), out)
+    return jnp.pad(jnp.concatenate([low, high], 1), ((0, 0), (0, 0), (0, lanes - out)))
 
 
 def conv_time_taps(buf, weight, frames, chains=2):
@@ -85,9 +102,10 @@
     frames, rows, cols, chans = own.shape
     lanes = -(-chans // 256) * 256
     extra = lanes - chans
-    w_first = jnp.pad(w_first, ((0, 0),) * 3 + ((0, extra), (0, extra))).reshape(3, 9 * lanes, lanes)
-    w_second = jnp.pad(w_second, ((0, 0),) * 3 + ((0, extra), (0, extra))).reshape(3, 9 * lanes, lanes)
+    w_first = dense_weight(w_first, lanes)
+    w_second = dense_weight(w_second, lanes)
     b_first = jnp.pad(b_first, (0, extra)).reshape(1, lanes)
+    depth = 9 * 128 + 5 * 128
     positions = (frames + 2) * (rows + 2) * cols + frames * rows * cols
     vmem = pl.BlockSpec(memory_space=pltpu.VMEM)
     return pl.pallas_call(
@@ -97,9 +115,9 @@
         out_specs=vmem,
         scratch_shapes=[
             pltpu.VMEM((2 * frames, rows + 4, cols, lanes), jnp.float32),
-            pltpu.VMEM((2 * frames, rows + 2, cols, 9 * lanes), jnp.bfloat16),
+            pltpu.VMEM((2 * frames, rows + 2, cols, depth), jnp.bfloat16),
             pltpu.VMEM((frames + 2, rows + 2, cols, lanes), jnp.float32),
-            pltpu.VMEM((frames + 2, rows, cols, 9 * lanes), jnp.bfloat16),
+            pltpu.VMEM((frames + 2, rows, cols, depth), jnp.bfloat16),
         ],
         compiler_params=pltpu.CompilerParams(vmem_limit_bytes=48 * 1024 * 1024),
         cost_estimate=pl.CostEstimate(

time: 27.9 us -> 30.4 us (1.090)
  the two profiles are of different devices: /device:TPU:10 before, /device:TPU:1 now
where the time goes in v8:
time: 30.4 us; the launch traced here: 30.1 us
  starting transfers between devices  10.2 us (34%)
  Pallas kernels  7.67 us (25%)
  other arithmetic  4.41 us (15%)
  waiting for transfers between devices  4.28 us (14%)
  local copies, waits for them, and re-layouts  3.47 us (11%)
    ppermute x3, starting transfers between devices, neighbour(): return lax.ppermute(value, axis, pairs)  10.2 us
    pallas_call x1, Pallas kernels, block(): pl.pallas_call(block_kernel, out_shape=jax.ShapeDtypeStruct(own.shape, ow...  7.67 us
    concatenate x1, other arithmetic, dense_weight(): jnp.concatenate([low, high], 1)  4.33 us
    ppermute x3, waiting for transfers between devices, neighbour(): return lax.ppermute(value, axis, pairs)  4.28 us
    slice x2, local copies, waits for them, and re-layouts, dense_weight(): low = weight[:, :, 0:128].reshape(3, taps * 128, out)  1.72 us
    slice x2, local copies, waits for them, and re-layouts, dense_weight(): weight[:, :, 128:]  1.32 us
  transfers between devices with their start and end apart: 3, of which 1 were waited for; matrix products, arithmetic and copies ran while one was open for 26% of the time, Pallas kernels for 0%

profile of v8, /device:TPU:1, one launch (start us, length us, event | category | flops | bytes accessed | tf_op | source)
XLA Modules:
  0.0 30.1 jit_solution(14736479595032355751)
XLA Ops:
  0.0 0.0 copy-start.2
  0.0 4.3 %collective-permute-start = (bf16[4,8,16,192]{3,2,1,0:T(8,128)(2,1)}, bf16[4,8,16,192]{3,2,1,0:T(8,128)(2,1)S(1)}, u32[]{:S(2)}, u32[]{:S(2)}) collective-permute-start(bf16[4,8,16,192]{3,2,1,0:T(8,128)(2,1)} %own.1), channel_id=1, source_target_pairs={{0,4},{4,8},{8,12},{1,5},{5,9},{9,13},{2,6},{6,10},{10,14},{3,7},{... | collective-permute-start | bytes 589832 | tf_op jit(solution)/shard_map/ppermute | solution.py:19
  4.3 1.2 %slice.27 = bf16[3,9,64,192]{3,2,1,0:T(8,128)(2,1)S(1)} slice(bf16[3,9,192,192]{3,2,1,0:T(8,128)(2,1)} %bitcast.17), slice={[0:3], [0:9], [128:192], [0:192]} | slice | bytes 1327104 | tf_op jit(solution)/shard_map/slice | solution.py:51
  5.5 1.6 %slice.26 = bf16[3,9,128,192]{3,2,1,0:T(8,128)(2,1)S(1)} slice(bf16[3,9,192,192]{3,2,1,0:T(8,128)(2,1)} %bitcast.18), slice={[0:3], [0:9], [0:128], [0:192]} | slice | bytes 2654208 | tf_op jit(solution)/shard_map/slice | solution.py:50
  7.2 0.0 copy-done.2
  7.2 0.1 slice.29
  7.3 0.1 slice.28
  7.4 0.2 pad.18
  7.6 0.2 pad.21
  7.7 0.0 copy-start.3
  7.8 0.0 copy-start
  7.8 0.0 copy-start.1
  7.8 4.3 %fusion.4 = (bf16[3,1792,256]{2,1,0:T(8,128)(2,1)S(1)}, bf16[3,1792,256]{2,1,0:T(8,128)(2,1)}) fusion(bf16[3,640,192]{2,1,0:T(8,128)(2,1)S(1)} %bitcast.15, bf16[3,1152,192]{2,1,0:T(8,128)(2,1)S(1)} %bitcast.13, bf16[3,640,192]{2,1,0:T(8,128)(2,1)S(1)} %bitcast.16, bf16[3,1152,192]{2,1,0:T(8,128)(2,1)S(1)} %bitcast.14), kind=kLoop, calls=%fused_computation.5 | loop fusion | flops 17891328 | bytes 9633792 | tf_op jit(solution)/shard_map/concatenate | solution.py:52
  12.1 0.0 copy-done.3
  12.1 0.0 collective-permute-done.earlier
  12.2 0.0 copy-done
  12.2 4.0 %collective-permute-start.1 = (bf16[8,2,16,192]{3,2,1,0:T(8,128)(2,1)S(1)}, bf16[8,2,16,192]{3,2,1,0:T(8,128)(2,1)S(1)}, u32[]{:S(2)}, u32[]{:S(2)}) collective-permute-start(bf16[8,2,16,192]{3,2,1,0:T(8,128)(2,1)S(1)} %get-tuple-element.6), channel_id=1, source_target_pairs={{0,1},{1,2},{2,3},{4,5},{5,6},{6,7},{8,9},{9,10},{10,11},{12,13},{... | collective-permute-start | bytes 294920 | tf_op jit(solution)/shard_map/ppermute | solution.py:19
  16.2 1.9 %collective-permute-start.2 = (bf16[8,2,16,192]{3,2,1,0:T(8,128)(2,1)S(1)}, bf16[8,2,16,192]{3,2,1,0:T(8,128)(2,1)S(1)}, u32[]{:S(2)}, u32[]{:S(2)}) collective-permute-start(bf16[8,2,16,192]{3,2,1,0:T(8,128)(2,1)S(1)} %get-tuple-element.5), channel_id=1, source_target_pairs={{1,0},{2,1},{3,2},{5,4},{6,5},{7,6},{9,8},{10,9},{11,10},{13,12},{... | collective-permute-start | bytes 294920 | tf_op jit(solution)/shard_map/ppermute | solution.py:19
  18.1 0.1 add_convert_fusion.flags
  18.2 0.0 collective-permute-done.1.top
  18.2 4.3 %collective-permute-done.2.bottom = bf16[8,2,16,192]{3,2,1,0:T(8,128)(2,1)S(1)} collective-permute-done((bf16[8,2,16,192]{3,2,1,0:T(8,128)(2,1)S(1)}, bf16[8,2,16,192]{3,2,1,0:T(8,128)(2,1)S(1)}, u32[]{:S(2)}, u32[]{:S(2)}) %collective-permute-start.2) | collective-permute-done | bytes 98336 | tf_op jit(solution)/shard_map/ppermute | solution.py:19
  22.5 0.0 copy-done.1
  22.5 7.7 %shard_map.55 = bf16[4,8,16,192]{3,2,1,0:T(8,128)(2,1)} custom-call(s32[3]{0:T(128)S(1)} %add_convert_fusion.flags, bf16[4,8,16,192]{3,2,1,0:T(8,128)(2,1)S(1)} %collective-permute-done.earlier, bf16[4,8,16,192]{3,2,1,0:T(8,128)(2,1)S(1)} %copy-done, bf16[8,2,16,192]{3,2,1,0:T(8,128)(2,1)S(1)} %collective-permute-done.1.top, ...), custom_call_target="tpu_custom_call" | custom-call | flops 2930245632 | bytes 7864320 | tf_op jit(solution)/shard_map/pallas_call | solution.py:111
  (4 shorter events, 0.1 us)
Async XLA Ops:
  0.0 7.2 %copy-start.2 = (bf16[3,3,3,192,192]{4,3,2,1,0:T(8,128)(2,1)S(1)}, bf16[3,3,3,192,192]{4,3,2,1,0:T(8,128)(2,1)}, u32[]{:S(2)}) copy-start(bf16[3,3,3,192,192]{4,3,2,1,0:T(8,128)(2,1)} %param.8) | copy-start | bytes 5971972
  0.0 12.1 %collective-permute-start = (bf16[4,8,16,192]{3,2,1,0:T(8,128)(2,1)}, bf16[4,8,16,192]{3,2,1,0:T(8,128)(2,1)S(1)}, u32[]{:S(2)}, u32[]{:S(2)}) collective-permute-start(bf16[4,8,16,192]{3,2,1,0:T(8,128)(2,1)} %own.1), channel_id=1, source_target_pairs={{0,4},{4,8},{8,12},{1,5},{5,9},{9,13},{2,6},{6,10},{10,14},{3,7},{... | collective-permute-start | bytes 589832 | tf_op jit(solution)/shard_map/ppermute | solution.py:19
  7.7 4.4 %copy-start.3 = (f32[192]{0:T(256)S(1)}, f32[192]{0:T(256)}, u32[]{:S(2)}) copy-start(f32[192]{0:T(256)} %param.7) | copy-start | bytes 2308
  7.8 4.4 %copy-start = (bf16[4,8,16,192]{3,2,1,0:T(8,128)(2,1)S(1)}, bf16[4,8,16,192]{3,2,1,0:T(8,128)(2,1)}, u32[]{:S(2)}) copy-start(bf16[4,8,16,192]{3,2,1,0:T(8,128)(2,1)} %own.1) | copy-start | bytes 589828
  7.8 14.7 %copy-start.1 = (f32[192]{0:T(256)S(1)}, f32[192]{0:T(256)}, u32[]{:S(2)}) copy-start(f32[192]{0:T(256)} %param.9) | copy-start | bytes 2308
  12.2 6.0 %collective-permute-start.1 = (bf16[8,2,16,192]{3,2,1,0:T(8,128)(2,1)S(1)}, bf16[8,2,16,192]{3,2,1,0:T(8,128)(2,1)S(1)}, u32[]{:S(2)}, u32[]{:S(2)}) collective-permute-start(bf16[8,2,16,192]{3,2,1,0:T(8,128)(2,1)S(1)} %get-tuple-element.6), channel_id=1, source_target_pairs={{0,1},{1,2},{2,3},{4,5},{5,6},{6,7},{8,9},{9,10},{10,11},{12,13},{... | collective-permute-start | bytes 294920 | tf_op jit(solution)/shard_map/ppermute | solution.py:19
  16.2 6.3 %collective-permute-start.2 = (bf16[8,2,16,192]{3,2,1,0:T(8,128)(2,1)S(1)}, bf16[8,2,16,192]{3,2,1,0:T(8,128)(2,1)S(1)}, u32[]{:S(2)}, u32[]{:S(2)}) collective-permute-start(bf16[8,2,16,192]{3,2,1,0:T(8,128)(2,1)S(1)} %get-tuple-element.5), channel_id=1, source_target_pairs={{1,0},{2,1},{3,2},{5,4},{6,5},{7,6},{9,8},{10,9},{11,10},{13,12},{... | collective-permute-start | bytes 294920 | tf_op jit(solution)/shard_map/ppermute | solution.py:19

commit v9 on v8

--- a/solution.py
+++ b/solution.py
@@ -44,26 +44,25 @@
         buf[:, :, :, 128 * (9 + j) : 128 * (10 + j)] = packed.astype(jnp.bfloat16)
 
 
-def dense_weight(weight, lanes):
-    taps, chans, out = 9, weight.shape[3], weight.shape[4]
-    weight = weight.reshape(3, taps, chans, out)
-    low = weight[:, :, 0:128].reshape(3, taps * 128, out)
-    high = jnp.pad(weight[:, :, 128:], ((0, 0), (0, 1), (0, 0), (0, 0))).reshape(3, (taps + 1) * (chans - 128), out)
-    return jnp.pad(jnp.concatenate([low, high], 1), ((0, 0), (0, 0), (0, lanes - out)))
+def dense_rows(weight, a):
+    chans = weight.shape[1] // 9
+    low = [weight[a, chans * k : chans * k + 128] for k in range(9)]
+    high = [weight[a, chans * k + 128 : chans * (k + 1)] for k in range(9)]
+    pad = jnp.zeros((128 - (chans - 128), weight.shape[2]), weight.dtype)
+    return jnp.concatenate(low + high + [pad], 0)
 
 
 def conv_time_taps(buf, weight, frames, chains=2):
     rows, cols, depth = buf.shape[1], buf.shape[2], buf.shape[3]
     bounds = [frames * i // chains for i in range(chains + 1)]
-    parts = []
-    for lo, hi in zip(bounds[:-1], bounds[1:]):
-        total = None
-        for a in range(3):
+    totals = [None] * chains
+    for a in range(3):
+        rhs = dense_rows(weight, a)
+        for i, (lo, hi) in enumerate(zip(bounds[:-1], bounds[1:])):
             lhs = buf[a + lo : a + hi].reshape((hi - lo) * rows * cols, depth)
-            term = jnp.dot(lhs, weight[a], preferred_element_type=jnp.float32)
-            total = term if total is None else total + term
-        parts.append(total)
-    return jnp.concatenate(parts, 0)
+            term = jnp.dot(lhs, rhs, preferred_element_type=jnp.float32)
+            totals[i] = term if totals[i] is None else totals[i] + term
+    return jnp.concatenate(totals, 0)
 
 
 def block_kernel(
@@ -78,7 +77,8 @@
     field[:, rows + 2 :, :, 0:chans] = silu(bottom[...])
     spread_taps(field[...].reshape(2 * frames * (rows + 4) * cols, lanes), cols, rows + 2, buf1)
     hidden = conv_time_taps(buf1, w_first, frames + 2) + b_first[...]
-    gated[...] = silu(hidden).reshape(frames + 2, rows + 2, cols, lanes)
+    gated[:, :, :, chans:] = jnp.zeros(gated.shape[:3] + (lanes - chans,), jnp.float32)
+    gated[:, :, :, 0:chans] = silu(hidden).reshape(frames + 2, rows + 2, cols, chans)
 
     @pl.when(flags[0] != 0)
     def _():
@@ -93,7 +93,7 @@
         gated[:, rows + 1 :] = jnp.zeros((frames + 2, 1, cols, lanes), jnp.float32)
 
     spread_taps(gated[...].reshape((frames + 2) * (rows + 2) * cols, lanes), cols, rows, buf2)
-    second = conv_time_taps(buf2, w_second, frames)[:, 0:chans] + b_second[...]
+    second = conv_time_taps(buf2, w_second, frames) + b_second[...]
     result = own[...].astype(jnp.float32).reshape(frames * rows * cols, chans) + second
     out[...] = result.astype(jnp.bfloat16).reshape(frames, rows, cols, chans)
 
@@ -101,10 +101,9 @@
 def block(flags, earlier, own, top, bottom, w_first, b_first, w_second, b_second):
     frames, rows, cols, chans = own.shape
     lanes = -(-chans // 256) * 256
-    extra = lanes - chans
-    w_first = dense_weight(w_first, lanes)
-    w_second = dense_weight(w_second, lanes)
-    b_first = jnp.pad(b_first, (0, extra)).reshape(1, lanes)
+    w_first = w_first.reshape(3, 9 * chans, chans)
+    w_second = w_second.reshape(3, 9 * chans, chans)
+    b_first = b_first.reshape(1, chans)
     depth = 9 * 128 + 5 * 128
     positions = (frames + 2) * (rows + 2) * cols + frames * rows * cols
     vmem = pl.BlockSpec(memory_space=pltpu.VMEM)

time: 30.4 us -> 32 us (1.053)
  the two profiles are of different devices: /device:TPU:1 before, /device:TPU:10 now
where the time goes in v9:
time: 32 us; the launch traced here: 31.7 us
  waiting for transfers between devices  10.4 us (32%)
  starting transfers between devices  7.8 us (24%)
  local copies, waits for them, and re-layouts  6.81 us (21%)
  Pallas kernels  6.49 us (20%)
    ppermute x3, waiting for transfers between devices, neighbour(): return lax.ppermute(value, axis, pairs)  10.4 us
    ppermute x3, starting transfers between devices, neighbour(): return lax.ppermute(value, axis, pairs)  7.8 us
    pallas_call x1, Pallas kernels, block(): pl.pallas_call(block_kernel, out_shape=jax.ShapeDtypeStruct(own.shape, ow...  6.49 us
    unnamed x11, local copies, waits for them, and re-layouts  5.82 us
    concatenate x1, local copies, waits for them, and re-layouts, local(): extended = jnp.concatenate([earlier, x], 0)  0.97 us
  transfers between devices with their start and end apart: 3, of which 2 were waited for; matrix products, arithmetic and copies ran while one was open for 0% of the time, Pallas kernels for 0%

profile of v9, /device:TPU:10, one launch (start us, length us, event | category | flops | bytes accessed | tf_op | source)
XLA Modules:
  0.0 31.7 jit_solution(9884005209159503854)
XLA Ops:
  0.0 3.5 %collective-permute-start = (bf16[4,8,16,192]{3,2,1,0:T(8,128)(2,1)}, bf16[4,8,16,192]{3,2,1,0:T(8,128)(2,1)S(1)}, u32[]{:S(2)}, u32[]{:S(2)}) collective-permute-start(bf16[4,8,16,192]{3,2,1,0:T(8,128)(2,1)} %own.1), channel_id=1, source_target_pairs={{0,4},{4,8},{8,12},{1,5},{5,9},{9,13},{2,6},{6,10},{10,14},{3,7},{... | collective-permute-start | bytes 589832 | tf_op jit(solution)/shard_map/ppermute | solution.py:19
  3.5 6.6 %collective-permute-done.earlier = bf16[4,8,16,192]{3,2,1,0:T(8,128)(2,1)S(1)} collective-permute-done((bf16[4,8,16,192]{3,2,1,0:T(8,128)(2,1)}, bf16[4,8,16,192]{3,2,1,0:T(8,128)(2,1)S(1)}, u32[]{:S(2)}, u32[]{:S(2)}) %collective-permute-start) | collective-permute-done | bytes 196640 | tf_op jit(solution)/shard_map/ppermute | solution.py:19
  10.2 1.0 %constant_dynamic-update-slice_fusion = bf16[8,8,16,192]{3,2,1,0:T(8,128)(2,1)S(1)} fusion(bf16[8,8,16,192]{3,2,1,0:T(8,128)(2,1)S(1)} %constant_dynamic-update-slice_fusion.1, bf16[4,8,16,192]{3,2,1,0:T(8,128)(2,1)} %own.1), kind=kLoop, calls=%fused_computation | loop fusion | bytes 458752 | tf_op jit(solution)/shard_map/concatenate | solution.py:134
  11.2 1.9 %collective-permute-start.2 = (bf16[8,2,16,192]{3,2,1,0:T(8,128)(2,1)S(1)}, bf16[8,2,16,192]{3,2,1,0:T(8,128)(2,1)S(1)}, u32[]{:S(2)}, u32[]{:S(2)}) collective-permute-start(bf16[8,2,16,192]{3,2,1,0:T(8,128)(2,1)S(1)} %get-tuple-element.5), channel_id=1, source_target_pairs={{1,0},{2,1},{3,2},{5,4},{6,5},{7,6},{9,8},{10,9},{11,10},{13,12},{... | collective-permute-start | bytes 294920 | tf_op jit(solution)/shard_map/ppermute | solution.py:19
  13.1 2.4 %collective-permute-start.1 = (bf16[8,2,16,192]{3,2,1,0:T(8,128)(2,1)S(1)}, bf16[8,2,16,192]{3,2,1,0:T(8,128)(2,1)S(1)}, u32[]{:S(2)}, u32[]{:S(2)}) collective-permute-start(bf16[8,2,16,192]{3,2,1,0:T(8,128)(2,1)S(1)} %get-tuple-element.6), channel_id=1, source_target_pairs={{0,1},{1,2},{2,3},{4,5},{5,6},{6,7},{8,9},{9,10},{10,11},{12,13},{... | collective-permute-start | bytes 294920 | tf_op jit(solution)/shard_map/ppermute | solution.py:19
  15.5 0.1 add_convert_fusion.flags
  15.6 0.0 collective-permute-done.2.bottom
  15.6 3.8 %collective-permute-done.1.top = bf16[8,2,16,192]{3,2,1,0:T(8,128)(2,1)S(1)} collective-permute-done((bf16[8,2,16,192]{3,2,1,0:T(8,128)(2,1)S(1)}, bf16[8,2,16,192]{3,2,1,0:T(8,128)(2,1)S(1)}, u32[]{:S(2)}, u32[]{:S(2)}) %collective-permute-start.1) | collective-permute-done | bytes 98336 | tf_op jit(solution)/shard_map/ppermute | solution.py:19
  19.4 0.0 copy-start
  19.4 0.9 %copy-done = bf16[4,8,16,192]{3,2,1,0:T(8,128)(2,1)S(1)} copy-done((bf16[4,8,16,192]{3,2,1,0:T(8,128)(2,1)S(1)}, bf16[4,8,16,192]{3,2,1,0:T(8,128)(2,1)}, u32[]{:S(2)}) %copy-start) | copy-done | bytes 196632
  20.3 0.0 copy-start.1
  20.3 1.7 %copy-done.1 = bf16[3,3,3,192,192]{4,3,2,1,0:T(8,128)(2,1)S(1)} copy-done((bf16[3,3,3,192,192]{4,3,2,1,0:T(8,128)(2,1)S(1)}, bf16[3,3,3,192,192]{4,3,2,1,0:T(8,128)(2,1)}, u32[]{:S(2)}) %copy-start.1) | copy-done | bytes 1990680
  22.1 0.0 copy-start.2
  22.1 1.7 %copy-done.2 = bf16[3,3,3,192,192]{4,3,2,1,0:T(8,128)(2,1)S(1)} copy-done((bf16[3,3,3,192,192]{4,3,2,1,0:T(8,128)(2,1)S(1)}, bf16[3,3,3,192,192]{4,3,2,1,0:T(8,128)(2,1)}, u32[]{:S(2)}) %copy-start.2) | copy-done | bytes 1990680
  23.8 0.0 copy-start.3
  23.8 0.7 %copy-done.3 = f32[192]{0:T(256)S(1)} copy-done((f32[192]{0:T(256)S(1)}, f32[192]{0:T(256)}, u32[]{:S(2)}) %copy-start.3) | copy-done | bytes 792
  24.5 0.0 copy-start.4
  24.5 0.7 %copy-done.4 = f32[192]{0:T(256)S(1)} copy-done((f32[192]{0:T(256)S(1)}, f32[192]{0:T(256)}, u32[]{:S(2)}) %copy-start.4) | copy-done | bytes 792
  25.2 6.5 %shard_map.55 = bf16[4,8,16,192]{3,2,1,0:T(8,128)(2,1)} custom-call(s32[3]{0:T(128)S(1)} %add_convert_fusion.flags, bf16[4,8,16,192]{3,2,1,0:T(8,128)(2,1)S(1)} %collective-permute-done.earlier, bf16[4,8,16,192]{3,2,1,0:T(8,128)(2,1)S(1)} %copy-done, bf16[8,2,16,192]{3,2,1,0:T(8,128)(2,1)S(1)} %collective-permute-done.1.top, ...), custom_call_target="tpu_custom_call" | custom-call | flops 2930245632 | bytes 7864320 | tf_op jit(solution)/shard_map/pallas_call | solution.py:110
  (2 shorter events, 0.0 us)
Async XLA Ops:
  0.0 10.1 %collective-permute-start = (bf16[4,8,16,192]{3,2,1,0:T(8,128)(2,1)}, bf16[4,8,16,192]{3,2,1,0:T(8,128)(2,1)S(1)}, u32[]{:S(2)}, u32[]{:S(2)}) collective-permute-start(bf16[4,8,16,192]{3,2,1,0:T(8,128)(2,1)} %own.1), channel_id=1, source_target_pairs={{0,4},{4,8},{8,12},{1,5},{5,9},{9,13},{2,6},{6,10},{10,14},{3,7},{... | collective-permute-start | bytes 589832 | tf_op jit(solution)/shard_map/ppermute | solution.py:19
  11.2 4.4 %collective-permute-start.2 = (bf16[8,2,16,192]{3,2,1,0:T(8,128)(2,1)S(1)}, bf16[8,2,16,192]{3,2,1,0:T(8,128)(2,1)S(1)}, u32[]{:S(2)}, u32[]{:S(2)}) collective-permute-start(bf16[8,2,16,192]{3,2,1,0:T(8,128)(2,1)S(1)} %get-tuple-element.5), channel_id=1, source_target_pairs={{1,0},{2,1},{3,2},{5,4},{6,5},{7,6},{9,8},{10,9},{11,10},{13,12},{... | collective-permute-start | bytes 294920 | tf_op jit(solution)/shard_map/ppermute | solution.py:19
  13.1 6.3 %collective-permute-start.1 = (bf16[8,2,16,192]{3,2,1,0:T(8,128)(2,1)S(1)}, bf16[8,2,16,192]{3,2,1,0:T(8,128)(2,1)S(1)}, u32[]{:S(2)}, u32[]{:S(2)}) collective-permute-start(bf16[8,2,16,192]{3,2,1,0:T(8,128)(2,1)S(1)} %get-tuple-element.6), channel_id=1, source_target_pairs={{0,1},{1,2},{2,3},{4,5},{5,6},{6,7},{8,9},{9,10},{10,11},{12,13},{... | collective-permute-start | bytes 294920 | tf_op jit(solution)/shard_map/ppermute | solution.py:19
  19.4 1.0 %copy-start = (bf16[4,8,16,192]{3,2,1,0:T(8,128)(2,1)S(1)}, bf16[4,8,16,192]{3,2,1,0:T(8,128)(2,1)}, u32[]{:S(2)}) copy-start(bf16[4,8,16,192]{3,2,1,0:T(8,128)(2,1)} %own.1) | copy-start | bytes 589828
  20.3 1.7 %copy-start.1 = (bf16[3,3,3,192,192]{4,3,2,1,0:T(8,128)(2,1)S(1)}, bf16[3,3,3,192,192]{4,3,2,1,0:T(8,128)(2,1)}, u32[]{:S(2)}) copy-start(bf16[3,3,3,192,192]{4,3,2,1,0:T(8,128)(2,1)} %param.6) | copy-start | bytes 5971972
  22.1 1.7 %copy-start.2 = (bf16[3,3,3,192,192]{4,3,2,1,0:T(8,128)(2,1)S(1)}, bf16[3,3,3,192,192]{4,3,2,1,0:T(8,128)(2,1)}, u32[]{:S(2)}) copy-start(bf16[3,3,3,192,192]{4,3,2,1,0:T(8,128)(2,1)} %param.8) | copy-start | bytes 5971972
  23.8 0.7 %copy-start.3 = (f32[192]{0:T(256)S(1)}, f32[192]{0:T(256)}, u32[]{:S(2)}) copy-start(f32[192]{0:T(256)} %param.7) | copy-start | bytes 2308
  24.5 0.7 %copy-start.4 = (f32[192]{0:T(256)S(1)}, f32[192]{0:T(256)}, u32[]{:S(2)}) copy-start(f32[192]{0:T(256)} %param.9) | copy-start | bytes 2308

commit v10 on v9

--- a/solution.py
+++ b/solution.py
@@ -66,17 +66,29 @@
 
 
 def block_kernel(
-    flags, earlier, own, top, bottom, w_first, b_first, w_second, b_second, out, field, buf1, gated, buf2
+    flags, earlier, top, bottom, own_hbm, w_first_hbm, w_second_hbm, biases_hbm, out,
+    own, w_first, w_second, biases, sems, field, buf1, gated, buf2,
 ):
+    copies = [
+        pltpu.make_async_copy(src, dst, sems.at[i])
+        for i, (src, dst) in enumerate(
+            [(own_hbm, own), (biases_hbm, biases), (w_first_hbm, w_first), (w_second_hbm, w_second)]
+        )
+    ]
+    for copy in copies:
+        copy.start()
     frames, rows, cols, chans = own.shape
     lanes = field.shape[3]
     field[:, :, :, chans:] = jnp.zeros(field.shape[:3] + (lanes - chans,), jnp.float32)
     field[0:frames, 2 : rows + 2, :, 0:chans] = silu(earlier[...])
-    field[frames:, 2 : rows + 2, :, 0:chans] = silu(own[...])
     field[:, 0:2, :, 0:chans] = silu(top[...])
     field[:, rows + 2 :, :, 0:chans] = silu(bottom[...])
+    copies[0].wait()
+    copies[1].wait()
+    field[frames:, 2 : rows + 2, :, 0:chans] = silu(own[...])
     spread_taps(field[...].reshape(2 * frames * (rows + 4) * cols, lanes), cols, rows + 2, buf1)
-    hidden = conv_time_taps(buf1, w_first, frames + 2) + b_first[...]
+    copies[2].wait()
+    hidden = conv_time_taps(buf1, w_first, frames + 2) + biases[0:1, :]
     gated[:, :, :, chans:] = jnp.zeros(gated.shape[:3] + (lanes - chans,), jnp.float32)
     gated[:, :, :, 0:chans] = silu(hidden).reshape(frames + 2, rows + 2, cols, chans)
 
@@ -93,7 +105,8 @@
         gated[:, rows + 1 :] = jnp.zeros((frames + 2, 1, cols, lanes), jnp.float32)
 
     spread_taps(gated[...].reshape((frames + 2) * (rows + 2) * cols, lanes), cols, rows, buf2)
-    second = conv_time_taps(buf2, w_second, frames) + b_second[...]
+    copies[3].wait()
+    second = conv_time_taps(buf2, w_second, frames) + biases[1:2, :]
     result = own[...].astype(jnp.float32).reshape(frames * rows * cols, chans) + second
     out[...] = result.astype(jnp.bfloat16).reshape(frames, rows, cols, chans)
 
@@ -103,28 +116,33 @@
     lanes = -(-chans // 256) * 256
     w_first = w_first.reshape(3, 9 * chans, chans)
     w_second = w_second.reshape(3, 9 * chans, chans)
-    b_first = b_first.reshape(1, chans)
+    biases = jnp.stack([b_first, b_second])
     depth = 9 * 128 + 5 * 128
     positions = (frames + 2) * (rows + 2) * cols + frames * rows * cols
     vmem = pl.BlockSpec(memory_space=pltpu.VMEM)
+    hbm = pl.BlockSpec(memory_space=pltpu.HBM)
     return pl.pallas_call(
         block_kernel,
         out_shape=jax.ShapeDtypeStruct(own.shape, own.dtype),
-        in_specs=[pl.BlockSpec(memory_space=pltpu.SMEM)] + [vmem] * 8,
+        in_specs=[pl.BlockSpec(memory_space=pltpu.SMEM)] + [vmem] * 3 + [hbm] * 4,
         out_specs=vmem,
         scratch_shapes=[
+            pltpu.VMEM(own.shape, own.dtype),
+            pltpu.VMEM(w_first.shape, w_first.dtype),
+            pltpu.VMEM(w_second.shape, w_second.dtype),
+            pltpu.VMEM(biases.shape, biases.dtype),
+            pltpu.SemaphoreType.DMA((4,)),
             pltpu.VMEM((2 * frames, rows + 4, cols, lanes), jnp.float32),
             pltpu.VMEM((2 * frames, rows + 2, cols, depth), jnp.bfloat16),
             pltpu.VMEM((frames + 2, rows + 2, cols, lanes), jnp.float32),
             pltpu.VMEM((frames + 2, rows, cols, depth), jnp.bfloat16),
         ],
-        compiler_params=pltpu.CompilerParams(vmem_limit_bytes=48 * 1024 * 1024),
         cost_estimate=pl.CostEstimate(
             flops=2 * positions * 27 * chans * chans,
             transcendentals=2 * positions * chans,
-            bytes_accessed=2 * (54 * lanes * lanes + 4 * own.size),
+            bytes_accessed=2 * (54 * chans * chans + 4 * own.size),
         ),
-    )(flags, earlier, own, top, bottom, w_first, b_first, w_second, b_second.reshape(1, chans))
+    )(flags, earlier, top, bottom, own, w_first, w_second, biases)
 
 
 def local(clip_frames, w_first, b_first, w_second, b_second):

time: 32 us -> 31.3 us (0.978)
  the two profiles are of different devices: /device:TPU:10 before, /device:TPU:1 now
where the time goes in v10:
time: 31.3 us; the launch traced here: 31 us
  starting transfers between devices  10.5 us (34%)
  Pallas kernels  9.12 us (29%)
  waiting for transfers between devices  7.7 us (25%)
  other arithmetic  1.9 us (6%)
  local copies, waits for them, and re-layouts  1.75 us (6%)
    ppermute x3, starting transfers between devices, neighbour(): return lax.ppermute(value, axis, pairs)  10.5 us
    pallas_call x1, Pallas kernels, block(): pl.pallas_call(block_kernel, out_shape=jax.ShapeDtypeStruct(own.shape, ow...  9.12 us
    ppermute x3, waiting for transfers between devices, neighbour(): return lax.ppermute(value, axis, pairs)  7.7 us
    another operation x1, other arithmetic, block(): biases = jnp.stack([b_first, b_second])  1.29 us
    concatenate x1, local copies, waits for them, and re-layouts, local(): extended = jnp.concatenate([earlier, x], 0)  1.06 us
    unnamed x7, local copies, waits for them, and re-layouts  0.67 us
  transfers between devices with their start and end apart: 3, of which 2 were waited for; matrix products, arithmetic and copies ran while one was open for 6% of the time, Pallas kernels for 0%

profile of v10, /device:TPU:1, one launch (start us, length us, event | category | flops | bytes accessed | tf_op | source)
XLA Modules:
  0.0 31.0 jit_solution(10712693800763138103)
XLA Ops:
  0.0 4.0 %collective-permute-start = (bf16[4,8,16,192]{3,2,1,0:T(8,128)(2,1)}, bf16[4,8,16,192]{3,2,1,0:T(8,128)(2,1)S(1)}, u32[]{:S(2)}, u32[]{:S(2)}) collective-permute-start(bf16[4,8,16,192]{3,2,1,0:T(8,128)(2,1)} %own_hbm.1), channel_id=1, source_target_pairs={{0,4},{4,8},{8,12},{1,5},{5,9},{9,13},{2,6},{6,10},{10,14},{3,7},{... | collective-permute-start | bytes 589832 | tf_op jit(solution)/shard_map/ppermute | solution.py:19
  4.1 1.3 %pad_maximum_fusion.biases_hbm = f32[2,192]{1,0:T(2,128)} fusion(f32[1,192]{1,0:T(1,128)} %bitcast.7, f32[1,192]{1,0:T(1,128)} %bitcast.8), kind=kLoop, calls=%fused_computation.2 | loop fusion | flops 384 | bytes 3072 | tf_op jit(solution)/shard_map/stack | solution.py:119
  5.3 4.0 %collective-permute-done.earlier = bf16[4,8,16,192]{3,2,1,0:T(8,128)(2,1)S(1)} collective-permute-done((bf16[4,8,16,192]{3,2,1,0:T(8,128)(2,1)}, bf16[4,8,16,192]{3,2,1,0:T(8,128)(2,1)S(1)}, u32[]{:S(2)}, u32[]{:S(2)}) %collective-permute-start) | collective-permute-done | bytes 196640 | tf_op jit(solution)/shard_map/ppermute | solution.py:19
  9.3 0.0 copy-start
  9.3 1.1 %constant_dynamic-update-slice_fusion = bf16[8,8,16,192]{3,2,1,0:T(8,128)(2,1)S(1)} fusion(bf16[8,8,16,192]{3,2,1,0:T(8,128)(2,1)S(1)} %constant_dynamic-update-slice_fusion.1, bf16[4,8,16,192]{3,2,1,0:T(8,128)(2,1)} %own_hbm.1), kind=kLoop, calls=%fused_computation | loop fusion | bytes 458752 | tf_op jit(solution)/shard_map/concatenate | solution.py:152
  10.4 4.6 %collective-permute-start.1 = (bf16[8,2,16,192]{3,2,1,0:T(8,128)(2,1)S(1)}, bf16[8,2,16,192]{3,2,1,0:T(8,128)(2,1)S(1)}, u32[]{:S(2)}, u32[]{:S(2)}) collective-permute-start(bf16[8,2,16,192]{3,2,1,0:T(8,128)(2,1)S(1)} %get-tuple-element.6), channel_id=1, source_target_pairs={{0,1},{1,2},{2,3},{4,5},{5,6},{6,7},{8,9},{9,10},{10,11},{12,13},{... | collective-permute-start | bytes 294920 | tf_op jit(solution)/shard_map/ppermute | solution.py:19
  15.0 1.9 %collective-permute-start.2 = (bf16[8,2,16,192]{3,2,1,0:T(8,128)(2,1)S(1)}, bf16[8,2,16,192]{3,2,1,0:T(8,128)(2,1)S(1)}, u32[]{:S(2)}, u32[]{:S(2)}) collective-permute-start(bf16[8,2,16,192]{3,2,1,0:T(8,128)(2,1)S(1)} %get-tuple-element.5), channel_id=1, source_target_pairs={{1,0},{2,1},{3,2},{5,4},{6,5},{7,6},{9,8},{10,9},{11,10},{13,12},{... | collective-permute-start | bytes 294920 | tf_op jit(solution)/shard_map/ppermute | solution.py:19
  16.9 0.6 %add_convert_fusion.flags = s32[3]{0:T(128)} fusion(pred[1]{0:T(512)(128)(4,1)} %bitcast.2, pred[1]{0:T(512)(128)(4,1)} %bitcast.1, pred[1]{0:T(512)(128)(4,1)} %bitcast), kind=kLoop, calls=%fused_computation.3 | loop fusion | flops 9 | bytes 15 | tf_op jit(solution)/shard_map/convert_element_type | solution.py:156
  17.5 0.0 collective-permute-done.1.top
  17.5 0.0 copy-start.1
  17.5 3.7 %collective-permute-done.2.bottom = bf16[8,2,16,192]{3,2,1,0:T(8,128)(2,1)S(1)} collective-permute-done((bf16[8,2,16,192]{3,2,1,0:T(8,128)(2,1)S(1)}, bf16[8,2,16,192]{3,2,1,0:T(8,128)(2,1)S(1)}, u32[]{:S(2)}, u32[]{:S(2)}) %collective-permute-start.2) | collective-permute-done | bytes 98336 | tf_op jit(solution)/shard_map/ppermute | solution.py:19
  21.3 0.0 copy-start.2
  21.3 0.0 copy-done
  21.3 0.0 copy-done.1
  21.3 0.6 %copy-done.2 = bf16[8,2,16,192]{3,2,1,0:T(8,128)(2,1)} copy-done((bf16[8,2,16,192]{3,2,1,0:T(8,128)(2,1)}, bf16[8,2,16,192]{3,2,1,0:T(8,128)(2,1)S(1)}, u32[]{:S(2)}) %copy-start.2) | copy-done | bytes 98328
  21.9 9.1 %shard_map.55 = bf16[4,8,16,192]{3,2,1,0:T(8,128)(2,1)} custom-call(s32[3]{0:T(128)} %add_convert_fusion.flags, bf16[4,8,16,192]{3,2,1,0:T(8,128)(2,1)} %copy-done, bf16[8,2,16,192]{3,2,1,0:T(8,128)(2,1)} %copy-done.1, bf16[8,2,16,192]{3,2,1,0:T(8,128)(2,1)} %copy-done.2, bf16[4,8,16,192]{3,2,1,0:T(8,128)(2,1)} %own_hbm.1, bf16[3,1728,192]{2,1,0:T(8,128)(2,1)} %bitcast.9, ...), custom_call_target="tpu_custom_call" | custom-call | flops 2930245632 | bytes 4767744 | tf_op jit(solution)/shard_map/pallas_call | solution.py:124
  (2 shorter events, 0.0 us)
Async XLA Ops:
  0.0 9.3 %collective-permute-start = (bf16[4,8,16,192]{3,2,1,0:T(8,128)(2,1)}, bf16[4,8,16,192]{3,2,1,0:T(8,128)(2,1)S(1)}, u32[]{:S(2)}, u32[]{:S(2)}) collective-permute-start(bf16[4,8,16,192]{3,2,1,0:T(8,128)(2,1)} %own_hbm.1), channel_id=1, source_target_pairs={{0,4},{4,8},{8,12},{1,5},{5,9},{9,13},{2,6},{6,10},{10,14},{3,7},{... | collective-permute-start | bytes 589832 | tf_op jit(solution)/shard_map/ppermute | solution.py:19
  9.3 12.0 %copy-start = (bf16[4,8,16,192]{3,2,1,0:T(8,128)(2,1)}, bf16[4,8,16,192]{3,2,1,0:T(8,128)(2,1)S(1)}, u32[]{:S(2)}) copy-start(bf16[4,8,16,192]{3,2,1,0:T(8,128)(2,1)S(1)} %collective-permute-done.earlier) | copy-start | bytes 589828
  10.4 7.1 %collective-permute-start.1 = (bf16[8,2,16,192]{3,2,1,0:T(8,128)(2,1)S(1)}, bf16[8,2,16,192]{3,2,1,0:T(8,128)(2,1)S(1)}, u32[]{:S(2)}, u32[]{:S(2)}) collective-permute-start(bf16[8,2,16,192]{3,2,1,0:T(8,128)(2,1)S(1)} %get-tuple-element.6), channel_id=1, source_target_pairs={{0,1},{1,2},{2,3},{4,5},{5,6},{6,7},{8,9},{9,10},{10,11},{12,13},{... | collective-permute-start | bytes 294920 | tf_op jit(solution)/shard_map/ppermute | solution.py:19
  15.0 6.3 %collective-permute-start.2 = (bf16[8,2,16,192]{3,2,1,0:T(8,128)(2,1)S(1)}, bf16[8,2,16,192]{3,2,1,0:T(8,128)(2,1)S(1)}, u32[]{:S(2)}, u32[]{:S(2)}) collective-permute-start(bf16[8,2,16,192]{3,2,1,0:T(8,128)(2,1)S(1)} %get-tuple-element.5), channel_id=1, source_target_pairs={{1,0},{2,1},{3,2},{5,4},{6,5},{7,6},{9,8},{10,9},{11,10},{13,12},{... | collective-permute-start | bytes 294920 | tf_op jit(solution)/shard_map/ppermute | solution.py:19
  17.5 3.8 %copy-start.1 = (bf16[8,2,16,192]{3,2,1,0:T(8,128)(2,1)}, bf16[8,2,16,192]{3,2,1,0:T(8,128)(2,1)S(1)}, u32[]{:S(2)}) copy-start(bf16[8,2,16,192]{3,2,1,0:T(8,128)(2,1)S(1)} %collective-permute-done.1.top) | copy-start | bytes 294916
  21.3 0.7 %copy-start.2 = (bf16[8,2,16,192]{3,2,1,0:T(8,128)(2,1)}, bf16[8,2,16,192]{3,2,1,0:T(8,128)(2,1)S(1)}, u32[]{:S(2)}) copy-start(bf16[8,2,16,192]{3,2,1,0:T(8,128)(2,1)S(1)} %collective-permute-done.2.bottom) | copy-start | bytes 294916

commit v11 on v9

--- a/solution.py
+++ b/solution.py
@@ -77,8 +77,7 @@
     field[:, rows + 2 :, :, 0:chans] = silu(bottom[...])
     spread_taps(field[...].reshape(2 * frames * (rows + 4) * cols, lanes), cols, rows + 2, buf1)
     hidden = conv_time_taps(buf1, w_first, frames + 2) + b_first[...]
-    gated[:, :, :, chans:] = jnp.zeros(gated.shape[:3] + (lanes - chans,), jnp.float32)
-    gated[:, :, :, 0:chans] = silu(hidden).reshape(frames + 2, rows + 2, cols, chans)
+    gated[...] = silu(hidden).reshape(frames + 2, rows + 2, cols, lanes)
 
     @pl.when(flags[0] != 0)
     def _():
@@ -93,7 +92,7 @@
         gated[:, rows + 1 :] = jnp.zeros((frames + 2, 1, cols, lanes), jnp.float32)
 
     spread_taps(gated[...].reshape((frames + 2) * (rows + 2) * cols, lanes), cols, rows, buf2)
-    second = conv_time_taps(buf2, w_second, frames) + b_second[...]
+    second = conv_time_taps(buf2, w_second, frames)[:, 0:chans] + b_second[...]
     result = own[...].astype(jnp.float32).reshape(frames * rows * cols, chans) + second
     out[...] = result.astype(jnp.bfloat16).reshape(frames, rows, cols, chans)
 
@@ -101,9 +100,9 @@
 def block(flags, earlier, own, top, bottom, w_first, b_first, w_second, b_second):
     frames, rows, cols, chans = own.shape
     lanes = -(-chans // 256) * 256
-    w_first = w_first.reshape(3, 9 * chans, chans)
-    w_second = w_second.reshape(3, 9 * chans, chans)
-    b_first = b_first.reshape(1, chans)
+    w_first = jnp.pad(w_first.reshape(3, 9 * chans, chans), ((0, 0), (0, 0), (0, lanes - chans)))
+    w_second = jnp.pad(w_second.reshape(3, 9 * chans, chans), ((0, 0), (0, 0), (0, lanes - chans)))
+    b_first = jnp.pad(b_first, (0, lanes - chans)).reshape(1, lanes)
     depth = 9 * 128 + 5 * 128
     positions = (frames + 2) * (rows + 2) * cols + frames * rows * cols
     vmem = pl.BlockSpec(memory_space=pltpu.VMEM)

time: 32 us -> 25.1 us (0.78)
  local copies, waits for them, and re-layouts: 6.81 us -> 3.27 us
  waiting for transfers between devices: 10.4 us -> 7.2 us
    unnamed x11 -> x9, local copies, waits for them, and re-layouts: 5.82 us -> 0.44 us
    ppermute x3, waiting for transfers between devices: 10.4 us -> 7.2 us  [neighbour(): return lax.ppermute(value, axis, pairs)]
    pad x0 -> x3, local copies, waits for them, and re-layouts: none -> 2.79 us  [the longest x1 2.33 us: block(): jnp.pad(w_first.reshape(3, 9 * chans, chans), ((0, 0), (0, 0), (0, lanes...]
    concatenate x1, local copies, waits for them, and re-layouts: 0.97 us -> 0.02 us  [local(): extended = jnp.concatenate([earlier, x], 0)]
  transfers between devices with their start and end apart: 3 -> 3, of which waited for: 2 -> 2; matrix products, arithmetic and copies ran while one was open for 0% -> 12% of each run, Pallas kernels for 0% -> 0%
where the time goes in v11:
time: 25.1 us; the launch traced here: 24.9 us
  starting transfers between devices  7.8 us (31%)
  waiting for transfers between devices  7.2 us (29%)
  Pallas kernels  6.47 us (26%)
  local copies, waits for them, and re-layouts  3.27 us (13%)
    ppermute x3, starting transfers between devices, neighbour(): return lax.ppermute(value, axis, pairs)  7.8 us
    ppermute x3, waiting for transfers between devices, neighbour(): return lax.ppermute(value, axis, pairs)  7.2 us
    pallas_call x1, Pallas kernels, block(): pl.pallas_call(block_kernel, out_shape=jax.ShapeDtypeStruct(own.shape, ow...  6.47 us
    pad x1, local copies, waits for them, and re-layouts, block(): jnp.pad(w_first.reshape(3, 9 * chans, chans), ((0, 0), (0, 0), (0, lanes...  2.33 us
  transfers between devices with their start and end apart: 3, of which 2 were waited for; matrix products, arithmetic and copies ran while one was open for 12% of the time, Pallas kernels for 0%

profile of v11, /device:TPU:10, one launch (start us, length us, event | category | flops | bytes accessed | tf_op | source)
XLA Modules:
  0.0 24.9 jit_solution(3145292342119097578)
XLA Ops:
  0.0 3.5 %collective-permute-start = (bf16[4,8,16,192]{3,2,1,0:T(8,128)(2,1)}, bf16[4,8,16,192]{3,2,1,0:T(8,128)(2,1)S(1)}, u32[]{:S(2)}, u32[]{:S(2)}) collective-permute-start(bf16[4,8,16,192]{3,2,1,0:T(8,128)(2,1)} %own.1), channel_id=1, source_target_pairs={{0,4},{4,8},{8,12},{1,5},{5,9},{9,13},{2,6},{6,10},{10,14},{3,7},{... | collective-permute-start | bytes 589832 | tf_op jit(solution)/shard_map/ppermute | solution.py:19
  3.5 0.0 copy-start.2
  3.5 2.3 %pad.11.w_first = bf16[3,1728,256]{2,1,0:T(8,128)(2,1)S(1)} pad(bf16[3,1728,192]{2,1,0:T(8,128)(2,1)} %bitcast.9, bf16[]{:T(256)} %constant.13.clone.1), padding=0_0x0_0x0_64 | pad | bytes 4644866 | tf_op jit(solution)/shard_map/jit(_pad)/pad | solution.py:103
  5.8 0.2 copy-done.2
  6.0 0.0 copy-start.3
  6.0 0.0 copy-start
  6.0 0.0 copy-start.1
  6.0 0.5 %pad.13.w_second = bf16[3,1728,256]{2,1,0:T(8,128)(2,1)S(1)} pad(bf16[3,1728,192]{2,1,0:T(8,128)(2,1)S(1)} %bitcast.10, bf16[]{:T(256)} %constant.13.clone.1), padding=0_0x0_0x0_64 | pad | bytes 4644866 | tf_op jit(solution)/shard_map/jit(_pad)/pad | solution.py:104
  6.5 0.2 copy-done.3
  6.7 3.4 %collective-permute-done.earlier = bf16[4,8,16,192]{3,2,1,0:T(8,128)(2,1)S(1)} collective-permute-done((bf16[4,8,16,192]{3,2,1,0:T(8,128)(2,1)}, bf16[4,8,16,192]{3,2,1,0:T(8,128)(2,1)S(1)}, u32[]{:S(2)}, u32[]{:S(2)}) %collective-permute-start) | collective-permute-done | bytes 196640 | tf_op jit(solution)/shard_map/ppermute | solution.py:19
  10.2 0.0 copy-done
  10.2 1.9 %collective-permute-start.2 = (bf16[8,2,16,192]{3,2,1,0:T(8,128)(2,1)S(1)}, bf16[8,2,16,192]{3,2,1,0:T(8,128)(2,1)S(1)}, u32[]{:S(2)}, u32[]{:S(2)}) collective-permute-start(bf16[8,2,16,192]{3,2,1,0:T(8,128)(2,1)S(1)} %get-tuple-element.5), channel_id=1, source_target_pairs={{1,0},{2,1},{3,2},{5,4},{6,5},{7,6},{9,8},{10,9},{11,10},{13,12},{... | collective-permute-start | bytes 294920 | tf_op jit(solution)/shard_map/ppermute | solution.py:19
  12.2 2.4 %collective-permute-start.1 = (bf16[8,2,16,192]{3,2,1,0:T(8,128)(2,1)S(1)}, bf16[8,2,16,192]{3,2,1,0:T(8,128)(2,1)S(1)}, u32[]{:S(2)}, u32[]{:S(2)}) collective-permute-start(bf16[8,2,16,192]{3,2,1,0:T(8,128)(2,1)S(1)} %get-tuple-element.6), channel_id=1, source_target_pairs={{0,1},{1,2},{2,3},{4,5},{5,6},{6,7},{8,9},{9,10},{10,11},{12,13},{... | collective-permute-start | bytes 294920 | tf_op jit(solution)/shard_map/ppermute | solution.py:19
  14.6 0.1 add_convert_fusion.flags
  14.7 0.0 collective-permute-done.2.bottom
  14.7 3.8 %collective-permute-done.1.top = bf16[8,2,16,192]{3,2,1,0:T(8,128)(2,1)S(1)} collective-permute-done((bf16[8,2,16,192]{3,2,1,0:T(8,128)(2,1)S(1)}, bf16[8,2,16,192]{3,2,1,0:T(8,128)(2,1)S(1)}, u32[]{:S(2)}, u32[]{:S(2)}) %collective-permute-start.1) | collective-permute-done | bytes 98336 | tf_op jit(solution)/shard_map/ppermute | solution.py:19
  18.4 0.0 copy-done.1
  18.4 6.5 %shard_map.55 = bf16[4,8,16,192]{3,2,1,0:T(8,128)(2,1)} custom-call(s32[3]{0:T(128)S(1)} %add_convert_fusion.flags, bf16[4,8,16,192]{3,2,1,0:T(8,128)(2,1)S(1)} %collective-permute-done.earlier, bf16[4,8,16,192]{3,2,1,0:T(8,128)(2,1)S(1)} %copy-done, bf16[8,2,16,192]{3,2,1,0:T(8,128)(2,1)S(1)} %collective-permute-done.1.top, ...), custom_call_target="tpu_custom_call" | custom-call | flops 2930245632 | bytes 7864320 | tf_op jit(solution)/shard_map/pallas_call | solution.py:109
  (4 shorter events, 0.1 us)
Async XLA Ops:
  0.0 10.1 %collective-permute-start = (bf16[4,8,16,192]{3,2,1,0:T(8,128)(2,1)}, bf16[4,8,16,192]{3,2,1,0:T(8,128)(2,1)S(1)}, u32[]{:S(2)}, u32[]{:S(2)}) collective-permute-start(bf16[4,8,16,192]{3,2,1,0:T(8,128)(2,1)} %own.1), channel_id=1, source_target_pairs={{0,4},{4,8},{8,12},{1,5},{5,9},{9,13},{2,6},{6,10},{10,14},{3,7},{... | collective-permute-start | bytes 589832 | tf_op jit(solution)/shard_map/ppermute | solution.py:19
  3.5 2.5 %copy-start.2 = (bf16[3,3,3,192,192]{4,3,2,1,0:T(8,128)(2,1)S(1)}, bf16[3,3,3,192,192]{4,3,2,1,0:T(8,128)(2,1)}, u32[]{:S(2)}) copy-start(bf16[3,3,3,192,192]{4,3,2,1,0:T(8,128)(2,1)} %param.8) | copy-start | bytes 5971972
  6.0 0.7 %copy-start.3 = (f32[192]{0:T(256)S(1)}, f32[192]{0:T(256)}, u32[]{:S(2)}) copy-start(f32[192]{0:T(256)} %param.7) | copy-start | bytes 2308
  6.0 4.1 %copy-start = (bf16[4,8,16,192]{3,2,1,0:T(8,128)(2,1)S(1)}, bf16[4,8,16,192]{3,2,1,0:T(8,128)(2,1)}, u32[]{:S(2)}) copy-start(bf16[4,8,16,192]{3,2,1,0:T(8,128)(2,1)} %own.1) | copy-start | bytes 589828
  6.0 12.4 %copy-start.1 = (f32[192]{0:T(256)S(1)}, f32[192]{0:T(256)}, u32[]{:S(2)}) copy-start(f32[192]{0:T(256)} %param.9) | copy-start | bytes 2308
  10.2 4.4 %collective-permute-start.2 = (bf16[8,2,16,192]{3,2,1,0:T(8,128)(2,1)S(1)}, bf16[8,2,16,192]{3,2,1,0:T(8,128)(2,1)S(1)}, u32[]{:S(2)}, u32[]{:S(2)}) collective-permute-start(bf16[8,2,16,192]{3,2,1,0:T(8,128)(2,1)S(1)} %get-tuple-element.5), channel_id=1, source_target_pairs={{1,0},{2,1},{3,2},{5,4},{6,5},{7,6},{9,8},{10,9},{11,10},{13,12},{... | collective-permute-start | bytes 294920 | tf_op jit(solution)/shard_map/ppermute | solution.py:19
  12.2 6.3 %collective-permute-start.1 = (bf16[8,2,16,192]{3,2,1,0:T(8,128)(2,1)S(1)}, bf16[8,2,16,192]{3,2,1,0:T(8,128)(2,1)S(1)}, u32[]{:S(2)}, u32[]{:S(2)}) collective-permute-start(bf16[8,2,16,192]{3,2,1,0:T(8,128)(2,1)S(1)} %get-tuple-element.6), channel_id=1, source_target_pairs={{0,1},{1,2},{2,3},{4,5},{5,6},{6,7},{8,9},{9,10},{10,11},{12,13},{... | collective-permute-start | bytes 294920 | tf_op jit(solution)/shard_map/ppermute | solution.py:19

commit v12 on v11

--- a/solution.py
+++ b/solution.py
@@ -71,10 +71,10 @@
     frames, rows, cols, chans = own.shape
     lanes = field.shape[3]
     field[:, :, :, chans:] = jnp.zeros(field.shape[:3] + (lanes - chans,), jnp.float32)
-    field[0:frames, 2 : rows + 2, :, 0:chans] = silu(earlier[...])
+    field[0:frames, :, :, 0:chans] = silu(earlier[...])
     field[frames:, 2 : rows + 2, :, 0:chans] = silu(own[...])
-    field[:, 0:2, :, 0:chans] = silu(top[...])
-    field[:, rows + 2 :, :, 0:chans] = silu(bottom[...])
+    field[frames:, 0:2, :, 0:chans] = silu(top[...])
+    field[frames:, rows + 2 :, :, 0:chans] = silu(bottom[...])
     spread_taps(field[...].reshape(2 * frames * (rows + 4) * cols, lanes), cols, rows + 2, buf1)
     hidden = conv_time_taps(buf1, w_first, frames + 2) + b_first[...]
     gated[...] = silu(hidden).reshape(frames + 2, rows + 2, cols, lanes)
@@ -129,10 +129,9 @@
 def local(clip_frames, w_first, b_first, w_second, b_second):
     rows = clip_frames.shape[1]
     x = clip_frames
-    earlier = neighbour(x, "tm", 1)
-    extended = jnp.concatenate([earlier, x], 0)
-    top = neighbour(extended[:, rows - 2 :], "height", 1)
-    bottom = neighbour(extended[:, :2], "height", -1)
+    top = neighbour(x[:, rows - 2 :], "height", 1)
+    bottom = neighbour(x[:, :2], "height", -1)
+    earlier = neighbour(jnp.concatenate([top, x, bottom], 1), "tm", 1)
     t, h = lax.axis_index("tm"), lax.axis_index("height")
     flags = jnp.stack([t == 0, h == 0, h == lax.axis_size("height") - 1]).astype(jnp.int32)
     return block(flags, earlier, x, top, bottom, w_first, b_first, w_second, b_second)

time: 25.1 us -> 28.9 us (1.15)
  the two profiles are of different devices: /device:TPU:10 before, /device:TPU:1 now
where the time goes in v12:
time: 28.9 us; the launch traced here: 28.7 us
  starting transfers between devices  9.65 us (33%)
  waiting for transfers between devices  7.26 us (25%)
  Pallas kernels  6.48 us (22%)
  local copies, waits for them, and re-layouts  4.09 us (14%)
  other arithmetic  1.1 us (4%)
    ppermute x3, starting transfers between devices, neighbour(): return lax.ppermute(value, axis, pairs)  9.65 us
    ppermute x3, waiting for transfers between devices, neighbour(): return lax.ppermute(value, axis, pairs)  7.26 us
    pallas_call x1, Pallas kernels, block(): pl.pallas_call(block_kernel, out_shape=jax.ShapeDtypeStruct(own.shape, ow...  6.48 us
    pad x1, local copies, waits for them, and re-layouts, block(): jnp.pad(w_first.reshape(3, 9 * chans, chans), ((0, 0), (0, 0), (0, lanes...  2.34 us
    concatenate x1, other arithmetic, local(): earlier = neighbour(jnp.concatenate([top, x, bottom], 1), 'tm', 1)  1.03 us
    slice x1, local copies, waits for them, and re-layouts, local(): top = neighbour(x[:, rows - 2:], 'height', 1)  0.88 us
  transfers between devices with their start and end apart: 3, of which 2 were waited for; matrix products, arithmetic and copies ran while one was open for 10% of the time, Pallas kernels for 0%

profile of v12, /device:TPU:1, one launch (start us, length us, event | category | flops | bytes accessed | tf_op | source)
XLA Modules:
  0.0 28.7 jit_solution(8260167876050220701)
XLA Ops:
  0.0 0.9 %fusion = (bf16[4,2,16,192]{3,2,1,0:T(8,128)(2,1)S(1)}, bf16[4,2,16,192]{3,2,1,0:T(8,128)(2,1)S(1)}) fusion(bf16[4,8,16,192]{3,2,1,0:T(8,128)(2,1)} %own.1), kind=kLoop, calls=%fused_computation.2 | loop fusion | bytes 196608 | tf_op jit(solution)/shard_map/slice | solution.py:132
  0.9 4.5 %collective-permute-start = (bf16[4,2,16,192]{3,2,1,0:T(8,128)(2,1)S(1)}, bf16[4,2,16,192]{3,2,1,0:T(8,128)(2,1)S(1)}, u32[]{:S(2)}, u32[]{:S(2)}) collective-permute-start(bf16[4,2,16,192]{3,2,1,0:T(8,128)(2,1)S(1)} %get-tuple-element.5), channel_id=1, source_target_pairs={{0,1},{1,2},{2,3},{4,5},{5,6},{6,7},{8,9},{9,10},{10,11},{12,13},{... | collective-permute-start | bytes 147464 | tf_op jit(solution)/shard_map/ppermute | solution.py:19
  5.4 1.9 %collective-permute-start.1 = (bf16[4,2,16,192]{3,2,1,0:T(8,128)(2,1)S(1)}, bf16[4,2,16,192]{3,2,1,0:T(8,128)(2,1)S(1)}, u32[]{:S(2)}, u32[]{:S(2)}) collective-permute-start(bf16[4,2,16,192]{3,2,1,0:T(8,128)(2,1)S(1)} %get-tuple-element.6), channel_id=1, source_target_pairs={{1,0},{2,1},{3,2},{5,4},{6,5},{7,6},{9,8},{10,9},{11,10},{13,12},{... | collective-permute-start | bytes 147464 | tf_op jit(solution)/shard_map/ppermute | solution.py:19
  7.3 0.0 collective-permute-done.top
  7.3 3.6 %collective-permute-done.1.bottom = bf16[4,2,16,192]{3,2,1,0:T(8,128)(2,1)S(1)} collective-permute-done((bf16[4,2,16,192]{3,2,1,0:T(8,128)(2,1)S(1)}, bf16[4,2,16,192]{3,2,1,0:T(8,128)(2,1)S(1)}, u32[]{:S(2)}, u32[]{:S(2)}) %collective-permute-start.1) | collective-permute-done | bytes 49184 | tf_op jit(solution)/shard_map/ppermute | solution.py:19
  11.0 1.0 %pad_maximum_fusion = bf16[4,12,16,192]{3,2,1,0:T(8,128)(2,1)S(1)} fusion(bf16[4,2,16,192]{3,2,1,0:T(8,128)(2,1)S(1)} %collective-permute-done.1.bottom, bf16[4,8,16,192]{3,2,1,0:T(8,128)(2,1)} %own.1, bf16[4,2,16,192]{3,2,1,0:T(8,128)(2,1)S(1)} %collective-permute-done.top), kind=kLoop, calls=%fused_computation | loop fusion | flops 294912 | bytes 589824 | tf_op jit(solution)/shard_map/concatenate | solution.py:134
  12.0 3.2 %collective-permute-start.2 = (bf16[4,12,16,192]{3,2,1,0:T(8,128)(2,1)S(1)}, bf16[4,12,16,192]{3,2,1,0:T(8,128)(2,1)S(1)}, u32[]{:S(2)}, u32[]{:S(2)}) collective-permute-start(bf16[4,12,16,192]{3,2,1,0:T(8,128)(2,1)S(1)} %pad_maximum_fusion), channel_id=1, source_target_pairs={{0,4},{4,8},{8,12},{1,5},{5,9},{9,13},{2,6},{6,10},{10,14},{3,7},{... | collective-permute-start | bytes 884744 | tf_op jit(solution)/shard_map/ppermute | solution.py:19
  15.3 0.0 copy-start.2
  15.3 2.3 %pad.11.w_first = bf16[3,1728,256]{2,1,0:T(8,128)(2,1)S(1)} pad(bf16[3,1728,192]{2,1,0:T(8,128)(2,1)} %bitcast.9, bf16[]{:T(256)} %constant.13.clone.1), padding=0_0x0_0x0_64 | pad | bytes 4644866 | tf_op jit(solution)/shard_map/jit(_pad)/pad | solution.py:103
  17.6 0.2 copy-done.2
  17.8 0.0 copy-start.3
  17.8 0.0 copy-start
  17.8 0.0 copy-start.1
  17.8 0.5 %pad.13.w_second = bf16[3,1728,256]{2,1,0:T(8,128)(2,1)S(1)} pad(bf16[3,1728,192]{2,1,0:T(8,128)(2,1)S(1)} %bitcast.10, bf16[]{:T(256)} %constant.13.clone.1), padding=0_0x0_0x0_64 | pad | bytes 4644866 | tf_op jit(solution)/shard_map/jit(_pad)/pad | solution.py:104
  18.3 0.2 copy-done.3
  18.5 0.1 add_convert_fusion.flags
  18.6 3.6 %collective-permute-done.2.earlier = bf16[4,12,16,192]{3,2,1,0:T(8,128)(2,1)S(1)} collective-permute-done((bf16[4,12,16,192]{3,2,1,0:T(8,128)(2,1)S(1)}, bf16[4,12,16,192]{3,2,1,0:T(8,128)(2,1)S(1)}, u32[]{:S(2)}, u32[]{:S(2)}) %collective-permute-start.2) | collective-permute-done | bytes 294944 | tf_op jit(solution)/shard_map/ppermute | solution.py:19
  22.2 0.0 copy-done
  22.2 0.0 copy-done.1
  22.2 6.5 %shard_map.55 = bf16[4,8,16,192]{3,2,1,0:T(8,128)(2,1)} custom-call(s32[3]{0:T(128)S(1)} %add_convert_fusion.flags, bf16[4,12,16,192]{3,2,1,0:T(8,128)(2,1)S(1)} %collective-permute-done.2.earlier, bf16[4,8,16,192]{3,2,1,0:T(8,128)(2,1)S(1)} %copy-done, bf16[4,2,16,192]{3,2,1,0:T(8,128)(2,1)S(1)} %collective-permute-done.top, ...), custom_call_target="tpu_custom_call" | custom-call | flops 2930245632 | bytes 7864320 | tf_op jit(solution)/shard_map/pallas_call | solution.py:109
  (1 shorter events, 0.0 us)
Async XLA Ops:
  0.9 6.4 %collective-permute-start = (bf16[4,2,16,192]{3,2,1,0:T(8,128)(2,1)S(1)}, bf16[4,2,16,192]{3,2,1,0:T(8,128)(2,1)S(1)}, u32[]{:S(2)}, u32[]{:S(2)}) collective-permute-start(bf16[4,2,16,192]{3,2,1,0:T(8,128)(2,1)S(1)} %get-tuple-element.5), channel_id=1, source_target_pairs={{0,1},{1,2},{2,3},{4,5},{5,6},{6,7},{8,9},{9,10},{10,11},{12,13},{... | collective-permute-start | bytes 147464 | tf_op jit(solution)/shard_map/ppermute | solution.py:19
  5.4 5.6 %collective-permute-start.1 = (bf16[4,2,16,192]{3,2,1,0:T(8,128)(2,1)S(1)}, bf16[4,2,16,192]{3,2,1,0:T(8,128)(2,1)S(1)}, u32[]{:S(2)}, u32[]{:S(2)}) collective-permute-start(bf16[4,2,16,192]{3,2,1,0:T(8,128)(2,1)S(1)} %get-tuple-element.6), channel_id=1, source_target_pairs={{1,0},{2,1},{3,2},{5,4},{6,5},{7,6},{9,8},{10,9},{11,10},{13,12},{... | collective-permute-start | bytes 147464 | tf_op jit(solution)/shard_map/ppermute | solution.py:19
  12.0 10.2 %collective-permute-start.2 = (bf16[4,12,16,192]{3,2,1,0:T(8,128)(2,1)S(1)}, bf16[4,12,16,192]{3,2,1,0:T(8,128)(2,1)S(1)}, u32[]{:S(2)}, u32[]{:S(2)}) collective-permute-start(bf16[4,12,16,192]{3,2,1,0:T(8,128)(2,1)S(1)} %pad_maximum_fusion), channel_id=1, source_target_pairs={{0,4},{4,8},{8,12},{1,5},{5,9},{9,13},{2,6},{6,10},{10,14},{3,7},{... | collective-permute-start | bytes 884744 | tf_op jit(solution)/shard_map/ppermute | solution.py:19
  15.3 2.6 %copy-start.2 = (bf16[3,3,3,192,192]{4,3,2,1,0:T(8,128)(2,1)S(1)}, bf16[3,3,3,192,192]{4,3,2,1,0:T(8,128)(2,1)}, u32[]{:S(2)}) copy-start(bf16[3,3,3,192,192]{4,3,2,1,0:T(8,128)(2,1)} %param.8) | copy-start | bytes 5971972
  17.8 0.7 %copy-start.3 = (f32[192]{0:T(256)S(1)}, f32[192]{0:T(256)}, u32[]{:S(2)}) copy-start(f32[192]{0:T(256)} %param.7) | copy-start | bytes 2308
  17.8 4.4 %copy-start = (bf16[4,8,16,192]{3,2,1,0:T(8,128)(2,1)S(1)}, bf16[4,8,16,192]{3,2,1,0:T(8,128)(2,1)}, u32[]{:S(2)}) copy-start(bf16[4,8,16,192]{3,2,1,0:T(8,128)(2,1)} %own.1) | copy-start | bytes 589828
  17.8 4.4 %copy-start.1 = (f32[192]{0:T(256)S(1)}, f32[192]{0:T(256)}, u32[]{:S(2)}) copy-start(f32[192]{0:T(256)} %param.9) | copy-start | bytes 2308

commit v13 on v11

--- a/solution.py
+++ b/solution.py
@@ -11,6 +11,12 @@
 def silu(value):
     value = value.astype(jnp.float32)
     return value / (1 + jnp.exp(-value))
+
+
+def silu_tanh(value):
+    value = value.astype(jnp.float32)
+    half = 0.5 * value
+    return half + half * jnp.tanh(half)
 
 
 def neighbour(value, axis, step):
@@ -62,7 +68,7 @@
             lhs = buf[a + lo : a + hi].reshape((hi - lo) * rows * cols, depth)
             term = jnp.dot(lhs, rhs, preferred_element_type=jnp.float32)
             totals[i] = term if totals[i] is None else totals[i] + term
-    return jnp.concatenate(totals, 0)
+    return totals, bounds
 
 
 def block_kernel(
@@ -71,13 +77,14 @@
     frames, rows, cols, chans = own.shape
     lanes = field.shape[3]
     field[:, :, :, chans:] = jnp.zeros(field.shape[:3] + (lanes - chans,), jnp.float32)
-    field[0:frames, 2 : rows + 2, :, 0:chans] = silu(earlier[...])
-    field[frames:, 2 : rows + 2, :, 0:chans] = silu(own[...])
-    field[:, 0:2, :, 0:chans] = silu(top[...])
-    field[:, rows + 2 :, :, 0:chans] = silu(bottom[...])
+    field[0:frames, 2 : rows + 2, :, 0:chans] = silu_tanh(earlier[...])
+    field[frames:, 2 : rows + 2, :, 0:chans] = silu_tanh(own[...])
+    field[:, 0:2, :, 0:chans] = silu_tanh(top[...])
+    field[:, rows + 2 :, :, 0:chans] = silu_tanh(bottom[...])
     spread_taps(field[...].reshape(2 * frames * (rows + 4) * cols, lanes), cols, rows + 2, buf1)
-    hidden = conv_time_taps(buf1, w_first, frames + 2) + b_first[...]
-    gated[...] = silu(hidden).reshape(frames + 2, rows + 2, cols, lanes)
+    totals, bounds = conv_time_taps(buf1, w_first, frames + 2)
+    for total, lo, hi in zip(totals, bounds[:-1], bounds[1:]):
+        gated[lo:hi] = silu_tanh(total + b_first[...]).reshape(hi - lo, rows + 2, cols, lanes)
 
     @pl.when(flags[0] != 0)
     def _():
@@ -92,7 +99,7 @@
         gated[:, rows + 1 :] = jnp.zeros((frames + 2, 1, cols, lanes), jnp.float32)
 
     spread_taps(gated[...].reshape((frames + 2) * (rows + 2) * cols, lanes), cols, rows, buf2)
-    second = conv_time_taps(buf2, w_second, frames)[:, 0:chans] + b_second[...]
+    second = jnp.concatenate(conv_time_taps(buf2, w_second, frames)[0], 0)[:, 0:chans] + b_second[...]
     result = own[...].astype(jnp.float32).reshape(frames * rows * cols, chans) + second
     out[...] = result.astype(jnp.bfloat16).reshape(frames, rows, cols, chans)
 

time: 25.1 us -> 24.9 us (level)
  no operation moved by 1% of the time
where the time goes in v13:
time: 24.9 us; the launch traced here: 24.7 us
  starting transfers between devices  7.8 us (31%)
  waiting for transfers between devices  7.2 us (29%)
  Pallas kernels  6.27 us (25%)
  local copies, waits for them, and re-layouts  3.27 us (13%)
    ppermute x3, starting transfers between devices, neighbour(): return lax.ppermute(value, axis, pairs)  7.8 us
    ppermute x3, waiting for transfers between devices, neighbour(): return lax.ppermute(value, axis, pairs)  7.2 us
    pallas_call x1, Pallas kernels, block(): pl.pallas_call(block_kernel, out_shape=jax.ShapeDtypeStruct(own.shape, ow...  6.27 us
    pad x1, local copies, waits for them, and re-layouts, block(): jnp.pad(w_first.reshape(3, 9 * chans, chans), ((0, 0), (0, 0), (0, lanes...  2.33 us
  transfers between devices with their start and end apart: 3, of which 2 were waited for; matrix products, arithmetic and copies ran while one was open for 12% of the time, Pallas kernels for 0%

profile of v13, /device:TPU:10, one launch (start us, length us, event | category | flops | bytes accessed | tf_op | source)
XLA Modules:
  0.0 24.7 jit_solution(1510869727792187911)
XLA Ops:
  0.0 3.5 %collective-permute-start = (bf16[4,8,16,192]{3,2,1,0:T(8,128)(2,1)}, bf16[4,8,16,192]{3,2,1,0:T(8,128)(2,1)S(1)}, u32[]{:S(2)}, u32[]{:S(2)}) collective-permute-start(bf16[4,8,16,192]{3,2,1,0:T(8,128)(2,1)} %own.1), channel_id=1, source_target_pairs={{0,4},{4,8},{8,12},{1,5},{5,9},{9,13},{2,6},{6,10},{10,14},{3,7},{... | collective-permute-start | bytes 589832 | tf_op jit(solution)/shard_map/ppermute | solution.py:25
  3.5 0.0 copy-start.2
  3.5 2.3 %pad.11.w_first = bf16[3,1728,256]{2,1,0:T(8,128)(2,1)S(1)} pad(bf16[3,1728,192]{2,1,0:T(8,128)(2,1)} %bitcast.9, bf16[]{:T(256)} %constant.13.clone.1), padding=0_0x0_0x0_64 | pad | bytes 4644866 | tf_op jit(solution)/shard_map/jit(_pad)/pad | solution.py:110
  5.8 0.2 copy-done.2
  6.0 0.0 copy-start.3
  6.0 0.0 copy-start
  6.0 0.0 copy-start.1
  6.0 0.5 %pad.13.w_second = bf16[3,1728,256]{2,1,0:T(8,128)(2,1)S(1)} pad(bf16[3,1728,192]{2,1,0:T(8,128)(2,1)S(1)} %bitcast.10, bf16[]{:T(256)} %constant.13.clone.1), padding=0_0x0_0x0_64 | pad | bytes 4644866 | tf_op jit(solution)/shard_map/jit(_pad)/pad | solution.py:111
  6.5 0.2 copy-done.3
  6.7 3.4 %collective-permute-done.earlier = bf16[4,8,16,192]{3,2,1,0:T(8,128)(2,1)S(1)} collective-permute-done((bf16[4,8,16,192]{3,2,1,0:T(8,128)(2,1)}, bf16[4,8,16,192]{3,2,1,0:T(8,128)(2,1)S(1)}, u32[]{:S(2)}, u32[]{:S(2)}) %collective-permute-start) | collective-permute-done | bytes 196640 | tf_op jit(solution)/shard_map/ppermute | solution.py:25
  10.2 0.0 copy-done
  10.2 1.9 %collective-permute-start.2 = (bf16[8,2,16,192]{3,2,1,0:T(8,128)(2,1)S(1)}, bf16[8,2,16,192]{3,2,1,0:T(8,128)(2,1)S(1)}, u32[]{:S(2)}, u32[]{:S(2)}) collective-permute-start(bf16[8,2,16,192]{3,2,1,0:T(8,128)(2,1)S(1)} %get-tuple-element.5), channel_id=1, source_target_pairs={{1,0},{2,1},{3,2},{5,4},{6,5},{7,6},{9,8},{10,9},{11,10},{13,12},{... | collective-permute-start | bytes 294920 | tf_op jit(solution)/shard_map/ppermute | solution.py:25
  12.2 2.4 %collective-permute-start.1 = (bf16[8,2,16,192]{3,2,1,0:T(8,128)(2,1)S(1)}, bf16[8,2,16,192]{3,2,1,0:T(8,128)(2,1)S(1)}, u32[]{:S(2)}, u32[]{:S(2)}) collective-permute-start(bf16[8,2,16,192]{3,2,1,0:T(8,128)(2,1)S(1)} %get-tuple-element.6), channel_id=1, source_target_pairs={{0,1},{1,2},{2,3},{4,5},{5,6},{6,7},{8,9},{9,10},{10,11},{12,13},{... | collective-permute-start | bytes 294920 | tf_op jit(solution)/shard_map/ppermute | solution.py:25
  14.6 0.1 add_convert_fusion.flags
  14.7 0.0 collective-permute-done.2.bottom
  14.7 3.8 %collective-permute-done.1.top = bf16[8,2,16,192]{3,2,1,0:T(8,128)(2,1)S(1)} collective-permute-done((bf16[8,2,16,192]{3,2,1,0:T(8,128)(2,1)S(1)}, bf16[8,2,16,192]{3,2,1,0:T(8,128)(2,1)S(1)}, u32[]{:S(2)}, u32[]{:S(2)}) %collective-permute-start.1) | collective-permute-done | bytes 98336 | tf_op jit(solution)/shard_map/ppermute | solution.py:25
  18.4 0.0 copy-done.1
  18.4 6.3 %shard_map.55 = bf16[4,8,16,192]{3,2,1,0:T(8,128)(2,1)} custom-call(s32[3]{0:T(128)S(1)} %add_convert_fusion.flags, bf16[4,8,16,192]{3,2,1,0:T(8,128)(2,1)S(1)} %collective-permute-done.earlier, bf16[4,8,16,192]{3,2,1,0:T(8,128)(2,1)S(1)} %copy-done, bf16[8,2,16,192]{3,2,1,0:T(8,128)(2,1)S(1)} %collective-permute-done.1.top, ...), custom_call_target="tpu_custom_call" | custom-call | flops 2930245632 | bytes 7864320 | tf_op jit(solution)/shard_map/pallas_call | solution.py:116
  (4 shorter events, 0.1 us)
Async XLA Ops:
  0.0 10.1 %collective-permute-start = (bf16[4,8,16,192]{3,2,1,0:T(8,128)(2,1)}, bf16[4,8,16,192]{3,2,1,0:T(8,128)(2,1)S(1)}, u32[]{:S(2)}, u32[]{:S(2)}) collective-permute-start(bf16[4,8,16,192]{3,2,1,0:T(8,128)(2,1)} %own.1), channel_id=1, source_target_pairs={{0,4},{4,8},{8,12},{1,5},{5,9},{9,13},{2,6},{6,10},{10,14},{3,7},{... | collective-permute-start | bytes 589832 | tf_op jit(solution)/shard_map/ppermute | solution.py:25
  3.5 2.5 %copy-start.2 = (bf16[3,3,3,192,192]{4,3,2,1,0:T(8,128)(2,1)S(1)}, bf16[3,3,3,192,192]{4,3,2,1,0:T(8,128)(2,1)}, u32[]{:S(2)}) copy-start(bf16[3,3,3,192,192]{4,3,2,1,0:T(8,128)(2,1)} %param.8) | copy-start | bytes 5971972
  6.0 0.7 %copy-start.3 = (f32[192]{0:T(256)S(1)}, f32[192]{0:T(256)}, u32[]{:S(2)}) copy-start(f32[192]{0:T(256)} %param.7) | copy-start | bytes 2308
  6.0 4.1 %copy-start = (bf16[4,8,16,192]{3,2,1,0:T(8,128)(2,1)S(1)}, bf16[4,8,16,192]{3,2,1,0:T(8,128)(2,1)}, u32[]{:S(2)}) copy-start(bf16[4,8,16,192]{3,2,1,0:T(8,128)(2,1)} %own.1) | copy-start | bytes 589828
  6.0 12.4 %copy-start.1 = (f32[192]{0:T(256)S(1)}, f32[192]{0:T(256)}, u32[]{:S(2)}) copy-start(f32[192]{0:T(256)} %param.9) | copy-start | bytes 2308
  10.2 4.4 %collective-permute-start.2 = (bf16[8,2,16,192]{3,2,1,0:T(8,128)(2,1)S(1)}, bf16[8,2,16,192]{3,2,1,0:T(8,128)(2,1)S(1)}, u32[]{:S(2)}, u32[]{:S(2)}) collective-permute-start(bf16[8,2,16,192]{3,2,1,0:T(8,128)(2,1)S(1)} %get-tuple-element.5), channel_id=1, source_target_pairs={{1,0},{2,1},{3,2},{5,4},{6,5},{7,6},{9,8},{10,9},{11,10},{13,12},{... | collective-permute-start | bytes 294920 | tf_op jit(solution)/shard_map/ppermute | solution.py:25
  12.2 6.3 %collective-permute-start.1 = (bf16[8,2,16,192]{3,2,1,0:T(8,128)(2,1)S(1)}, bf16[8,2,16,192]{3,2,1,0:T(8,128)(2,1)S(1)}, u32[]{:S(2)}, u32[]{:S(2)}) collective-permute-start(bf16[8,2,16,192]{3,2,1,0:T(8,128)(2,1)S(1)} %get-tuple-element.6), channel_id=1, source_target_pairs={{0,1},{1,2},{2,3},{4,5},{5,6},{6,7},{8,9},{9,10},{10,11},{12,13},{... | collective-permute-start | bytes 294920 | tf_op jit(solution)/shard_map/ppermute | solution.py:25

commit v14 on v13

--- a/solution.py
+++ b/solution.py
@@ -72,15 +72,18 @@
 
 
 def block_kernel(
-    flags, earlier, own, top, bottom, w_first, b_first, w_second, b_second, out, field, buf1, gated, buf2
+    flags, earlier, own, top, bottom, earlier_top, earlier_bottom, w_first, b_first, w_second, b_second, out,
+    field, buf1, gated, buf2
 ):
     frames, rows, cols, chans = own.shape
     lanes = field.shape[3]
     field[:, :, :, chans:] = jnp.zeros(field.shape[:3] + (lanes - chans,), jnp.float32)
     field[0:frames, 2 : rows + 2, :, 0:chans] = silu_tanh(earlier[...])
     field[frames:, 2 : rows + 2, :, 0:chans] = silu_tanh(own[...])
-    field[:, 0:2, :, 0:chans] = silu_tanh(top[...])
-    field[:, rows + 2 :, :, 0:chans] = silu_tanh(bottom[...])
+    field[0:frames, 0:2, :, 0:chans] = silu_tanh(earlier_top[...])
+    field[0:frames, rows + 2 :, :, 0:chans] = silu_tanh(earlier_bottom[...])
+    field[frames:, 0:2, :, 0:chans] = silu_tanh(top[...])
+    field[frames:, rows + 2 :, :, 0:chans] = silu_tanh(bottom[...])
     spread_taps(field[...].reshape(2 * frames * (rows + 4) * cols, lanes), cols, rows + 2, buf1)
     totals, bounds = conv_time_taps(buf1, w_first, frames + 2)
     for total, lo, hi in zip(totals, bounds[:-1], bounds[1:]):
@@ -104,7 +107,7 @@
     out[...] = result.astype(jnp.bfloat16).reshape(frames, rows, cols, chans)
 
 
-def block(flags, earlier, own, top, bottom, w_first, b_first, w_second, b_second):
+def block(flags, earlier, own, top, bottom, earlier_top, earlier_bottom, w_first, b_first, w_second, b_second):
     frames, rows, cols, chans = own.shape
     lanes = -(-chans // 256) * 256
     w_first = jnp.pad(w_first.reshape(3, 9 * chans, chans), ((0, 0), (0, 0), (0, lanes - chans)))
@@ -116,7 +119,7 @@
     return pl.pallas_call(
         block_kernel,
         out_shape=jax.ShapeDtypeStruct(own.shape, own.dtype),
-        in_specs=[pl.BlockSpec(memory_space=pltpu.SMEM)] + [vmem] * 8,
+        in_specs=[pl.BlockSpec(memory_space=pltpu.SMEM)] + [vmem] * 10,
         out_specs=vmem,
         scratch_shapes=[
             pltpu.VMEM((2 * frames, rows + 4, cols, lanes), jnp.float32),
@@ -130,19 +133,31 @@
             transcendentals=2 * positions * chans,
             bytes_accessed=2 * (54 * lanes * lanes + 4 * own.size),
         ),
-    )(flags, earlier, own, top, bottom, w_first, b_first, w_second, b_second.reshape(1, chans))
+    )(flags, earlier, own, top, bottom, earlier_top, earlier_bottom, w_first, b_first, w_second, b_second.reshape(1, chans))
+
+
+def diagonal(value, step):
+    frames, heights = lax.axis_size("tm"), lax.axis_size("height")
+    pairs = [
+        (t * heights + h, (t + 1) * heights + h + step)
+        for t in range(frames - 1)
+        for h in range(heights)
+        if 0 <= h + step < heights
+    ]
+    return lax.ppermute(value, ("tm", "height"), pairs)
 
 
 def local(clip_frames, w_first, b_first, w_second, b_second):
     rows = clip_frames.shape[1]
     x = clip_frames
     earlier = neighbour(x, "tm", 1)
-    extended = jnp.concatenate([earlier, x], 0)
-    top = neighbour(extended[:, rows - 2 :], "height", 1)
-    bottom = neighbour(extended[:, :2], "height", -1)
+    top = neighbour(x[:, rows - 2 :], "height", 1)
+    bottom = neighbour(x[:, :2], "height", -1)
+    earlier_top = diagonal(x[:, rows - 2 :], 1)
+    earlier_bottom = diagonal(x[:, :2], -1)
     t, h = lax.axis_index("tm"), lax.axis_index("height")
     flags = jnp.stack([t == 0, h == 0, h == lax.axis_size("height") - 1]).astype(jnp.int32)
-    return block(flags, earlier, x, top, bottom, w_first, b_first, w_second, b_second)
+    return block(flags, earlier, x, top, bottom, earlier_top, earlier_bottom, w_first, b_first, w_second, b_second)
 
 
 def solution(mesh):

time: 24.9 us -> 28.1 us (1.13)
  the two profiles are of different devices: /device:TPU:10 before, /device:TPU:0 now
where the time goes in v14:
time: 28.1 us; the launch traced here: 27.8 us
  starting transfers between devices  17 us (60%)
  Pallas kernels  6.27 us (22%)
  local copies, waits for them, and re-layouts  4.35 us (15%)
    ppermute x3, starting transfers between devices, neighbour(): return lax.ppermute(value, axis, pairs)  9.7 us
    ppermute x2, starting transfers between devices, diagonal(): return lax.ppermute(value, ('tm', 'height'), pairs)  7.32 us
    pallas_call x1, Pallas kernels, block(): pl.pallas_call(block_kernel, out_shape=jax.ShapeDtypeStruct(own.shape, ow...  6.27 us
    pad x1, local copies, waits for them, and re-layouts, block(): jnp.pad(w_first.reshape(3, 9 * chans, chans), ((0, 0), (0, 0), (0, lanes...  2.33 us
    slice x1, local copies, waits for them, and re-layouts, local(): bottom = neighbour(x[:, :2], 'height', -1)  0.89 us
    unnamed x8, local copies, waits for them, and re-layouts  0.64 us
  transfers between devices with their start and end apart: 5, of which 0 were waited for; matrix products, arithmetic and copies ran while one was open for 14% of the time, Pallas kernels for 0%

profile of v14, /device:TPU:0, one launch (start us, length us, event | category | flops | bytes accessed | tf_op | source)
XLA Modules:
  0.0 27.8 jit_solution(855528556992280734)
XLA Ops:
  0.0 4.9 %collective-permute-start = (bf16[4,8,16,192]{3,2,1,0:T(8,128)(2,1)}, bf16[4,8,16,192]{3,2,1,0:T(8,128)(2,1)S(1)}, u32[]{:S(2)}, u32[]{:S(2)}) collective-permute-start(bf16[4,8,16,192]{3,2,1,0:T(8,128)(2,1)} %own.1), channel_id=1, source_target_pairs={{0,4},{4,8},{8,12},{1,5},{5,9},{9,13},{2,6},{6,10},{10,14},{3,7},{... | collective-permute-start | bytes 589832 | tf_op jit(solution)/shard_map/ppermute | solution.py:25
  4.9 0.9 %fusion = (bf16[4,2,16,192]{3,2,1,0:T(8,128)(2,1)S(1)}, bf16[4,2,16,192]{3,2,1,0:T(8,128)(2,1)S(1)}) fusion(bf16[4,8,16,192]{3,2,1,0:T(8,128)(2,1)} %own.1), kind=kLoop, calls=%fused_computation.1 | loop fusion | bytes 196608 | tf_op jit(solution)/shard_map/slice | solution.py:155
  5.8 0.7 %collective-permute-start.4 = (bf16[4,2,16,192]{3,2,1,0:T(8,128)(2,1)S(1)}, bf16[4,2,16,192]{3,2,1,0:T(8,128)(2,1)S(1)}, u32[]{:S(2)}, u32[]{:S(2)}) collective-permute-start(bf16[4,2,16,192]{3,2,1,0:T(8,128)(2,1)S(1)} %get-tuple-element.5), channel_id=1, source_target_pairs={{1,4},{2,5},{3,6},{5,8},{6,9},{7,10},{9,12},{10,13},{11,14},{17,20... | collective-permute-start | bytes 147464 | tf_op jit(solution)/shard_map/ppermute | solution.py:147
  6.5 1.3 %collective-permute-start.2 = (bf16[4,2,16,192]{3,2,1,0:T(8,128)(2,1)S(1)}, bf16[4,2,16,192]{3,2,1,0:T(8,128)(2,1)S(1)}, u32[]{:S(2)}, u32[]{:S(2)}) collective-permute-start(bf16[4,2,16,192]{3,2,1,0:T(8,128)(2,1)S(1)} %get-tuple-element.5), channel_id=1, source_target_pairs={{1,0},{2,1},{3,2},{5,4},{6,5},{7,6},{9,8},{10,9},{11,10},{13,12},{... | collective-permute-start | bytes 147464 | tf_op jit(solution)/shard_map/ppermute | solution.py:25
  7.8 6.7 %collective-permute-start.3 = (bf16[4,2,16,192]{3,2,1,0:T(8,128)(2,1)S(1)}, bf16[4,2,16,192]{3,2,1,0:T(8,128)(2,1)S(1)}, u32[]{:S(2)}, u32[]{:S(2)}) collective-permute-start(bf16[4,2,16,192]{3,2,1,0:T(8,128)(2,1)S(1)} %get-tuple-element.6), channel_id=1, source_target_pairs={{0,5},{1,6},{2,7},{4,9},{5,10},{6,11},{8,13},{9,14},{10,15},{16,21... | collective-permute-start | bytes 147464 | tf_op jit(solution)/shard_map/ppermute | solution.py:147
  14.5 3.5 %collective-permute-start.1 = (bf16[4,2,16,192]{3,2,1,0:T(8,128)(2,1)S(1)}, bf16[4,2,16,192]{3,2,1,0:T(8,128)(2,1)S(1)}, u32[]{:S(2)}, u32[]{:S(2)}) collective-permute-start(bf16[4,2,16,192]{3,2,1,0:T(8,128)(2,1)S(1)} %get-tuple-element.6), channel_id=1, source_target_pairs={{0,1},{1,2},{2,3},{4,5},{5,6},{6,7},{8,9},{9,10},{10,11},{12,13},{... | collective-permute-start | bytes 147464 | tf_op jit(solution)/shard_map/ppermute | solution.py:25
  18.0 0.1 add_convert_fusion.flags
  18.0 0.0 copy-start.2
  18.0 2.3 %pad.11.w_first = bf16[3,1728,256]{2,1,0:T(8,128)(2,1)S(1)} pad(bf16[3,1728,192]{2,1,0:T(8,128)(2,1)} %bitcast.9, bf16[]{:T(256)} %constant.13.clone.1), padding=0_0x0_0x0_64 | pad | bytes 4644866 | tf_op jit(solution)/shard_map/jit(_pad)/pad | solution.py:113
  20.4 0.2 copy-done.2
  20.6 0.0 copy-start.3
  20.6 0.0 copy-start
  20.6 0.0 copy-start.1
  20.6 0.5 %pad.13.w_second = bf16[3,1728,256]{2,1,0:T(8,128)(2,1)S(1)} pad(bf16[3,1728,192]{2,1,0:T(8,128)(2,1)S(1)} %bitcast.10, bf16[]{:T(256)} %constant.13.clone.1), padding=0_0x0_0x0_64 | pad | bytes 4644866 | tf_op jit(solution)/shard_map/jit(_pad)/pad | solution.py:114
  21.1 0.2 copy-done.3
  21.3 0.0 collective-permute-done.4.earlier_bottom
  21.3 0.0 collective-permute-done.2.bottom
  21.3 0.0 collective-permute-done.3.earlier_top
  21.3 0.0 collective-permute-done.1.top
  21.3 0.0 collective-permute-done.earlier
  21.3 0.2 copy-done
  21.5 0.0 copy-done.1
  21.6 6.3 %shard_map.55 = bf16[4,8,16,192]{3,2,1,0:T(8,128)(2,1)} custom-call(s32[3]{0:T(128)S(1)} %add_convert_fusion.flags, bf16[4,8,16,192]{3,2,1,0:T(8,128)(2,1)S(1)} %collective-permute-done.earlier, bf16[4,8,16,192]{3,2,1,0:T(8,128)(2,1)S(1)} %copy-done, bf16[4,2,16,192]{3,2,1,0:T(8,128)(2,1)S(1)} %collective-permute-done.1.top, ...), custom_call_target="tpu_custom_call" | custom-call | flops 2930245632 | bytes 7864320 | tf_op jit(solution)/shard_map/pallas_call | solution.py:119
  (1 shorter events, 0.0 us)
Async XLA Ops:
  0.0 21.3 %collective-permute-start = (bf16[4,8,16,192]{3,2,1,0:T(8,128)(2,1)}, bf16[4,8,16,192]{3,2,1,0:T(8,128)(2,1)S(1)}, u32[]{:S(2)}, u32[]{:S(2)}) collective-permute-start(bf16[4,8,16,192]{3,2,1,0:T(8,128)(2,1)} %own.1), channel_id=1, source_target_pairs={{0,4},{4,8},{8,12},{1,5},{5,9},{9,13},{2,6},{6,10},{10,14},{3,7},{... | collective-permute-start | bytes 589832 | tf_op jit(solution)/shard_map/ppermute | solution.py:25
  5.8 15.4 %collective-permute-start.4 = (bf16[4,2,16,192]{3,2,1,0:T(8,128)(2,1)S(1)}, bf16[4,2,16,192]{3,2,1,0:T(8,128)(2,1)S(1)}, u32[]{:S(2)}, u32[]{:S(2)}) collective-permute-start(bf16[4,2,16,192]{3,2,1,0:T(8,128)(2,1)S(1)} %get-tuple-element.5), channel_id=1, source_target_pairs={{1,4},{2,5},{3,6},{5,8},{6,9},{7,10},{9,12},{10,13},{11,14},{17,20... | collective-permute-start | bytes 147464 | tf_op jit(solution)/shard_map/ppermute | solution.py:147
  6.5 14.8 %collective-permute-start.2 = (bf16[4,2,16,192]{3,2,1,0:T(8,128)(2,1)S(1)}, bf16[4,2,16,192]{3,2,1,0:T(8,128)(2,1)S(1)}, u32[]{:S(2)}, u32[]{:S(2)}) collective-permute-start(bf16[4,2,16,192]{3,2,1,0:T(8,128)(2,1)S(1)} %get-tuple-element.5), channel_id=1, source_target_pairs={{1,0},{2,1},{3,2},{5,4},{6,5},{7,6},{9,8},{10,9},{11,10},{13,12},{... | collective-permute-start | bytes 147464 | tf_op jit(solution)/shard_map/ppermute | solution.py:25
  7.8 13.5 %collective-permute-start.3 = (bf16[4,2,16,192]{3,2,1,0:T(8,128)(2,1)S(1)}, bf16[4,2,16,192]{3,2,1,0:T(8,128)(2,1)S(1)}, u32[]{:S(2)}, u32[]{:S(2)}) collective-permute-start(bf16[4,2,16,192]{3,2,1,0:T(8,128)(2,1)S(1)} %get-tuple-element.6), channel_id=1, source_target_pairs={{0,5},{1,6},{2,7},{4,9},{5,10},{6,11},{8,13},{9,14},{10,15},{16,21... | collective-permute-start | bytes 147464 | tf_op jit(solution)/shard_map/ppermute | solution.py:147
  14.5 6.8 %collective-permute-start.1 = (bf16[4,2,16,192]{3,2,1,0:T(8,128)(2,1)S(1)}, bf16[4,2,16,192]{3,2,1,0:T(8,128)(2,1)S(1)}, u32[]{:S(2)}, u32[]{:S(2)}) collective-permute-start(bf16[4,2,16,192]{3,2,1,0:T(8,128)(2,1)S(1)} %get-tuple-element.6), channel_id=1, source_target_pairs={{0,1},{1,2},{2,3},{4,5},{5,6},{6,7},{8,9},{9,10},{10,11},{12,13},{... | collective-permute-start | bytes 147464 | tf_op jit(solution)/shard_map/ppermute | solution.py:25
  18.0 2.5 %copy-start.2 = (bf16[3,3,3,192,192]{4,3,2,1,0:T(8,128)(2,1)S(1)}, bf16[3,3,3,192,192]{4,3,2,1,0:T(8,128)(2,1)}, u32[]{:S(2)}) copy-start(bf16[3,3,3,192,192]{4,3,2,1,0:T(8,128)(2,1)} %param.8) | copy-start | bytes 5971972
  20.6 0.7 %copy-start.3 = (f32[192]{0:T(256)S(1)}, f32[192]{0:T(256)}, u32[]{:S(2)}) copy-start(f32[192]{0:T(256)} %param.7) | copy-start | bytes 2308
  20.6 1.0 %copy-start = (bf16[4,8,16,192]{3,2,1,0:T(8,128)(2,1)S(1)}, bf16[4,8,16,192]{3,2,1,0:T(8,128)(2,1)}, u32[]{:S(2)}) copy-start(bf16[4,8,16,192]{3,2,1,0:T(8,128)(2,1)} %own.1) | copy-start | bytes 589828
  20.6 1.0 %copy-start.1 = (f32[192]{0:T(256)S(1)}, f32[192]{0:T(256)}, u32[]{:S(2)}) copy-start(f32[192]{0:T(256)} %param.9) | copy-start | bytes 2308

commit v15 on v13

--- a/solution.py
+++ b/solution.py
@@ -72,15 +72,18 @@
 
 
 def block_kernel(
-    flags, earlier, own, top, bottom, w_first, b_first, w_second, b_second, out, field, buf1, gated, buf2
+    flags, earlier, own, top, bottom, earlier_edges, w_first, b_first, w_second, b_second, out,
+    field, buf1, gated, buf2
 ):
     frames, rows, cols, chans = own.shape
     lanes = field.shape[3]
     field[:, :, :, chans:] = jnp.zeros(field.shape[:3] + (lanes - chans,), jnp.float32)
     field[0:frames, 2 : rows + 2, :, 0:chans] = silu_tanh(earlier[...])
     field[frames:, 2 : rows + 2, :, 0:chans] = silu_tanh(own[...])
-    field[:, 0:2, :, 0:chans] = silu_tanh(top[...])
-    field[:, rows + 2 :, :, 0:chans] = silu_tanh(bottom[...])
+    field[0:frames, 0:2, :, 0:chans] = silu_tanh(earlier_edges[:, 0:2])
+    field[0:frames, rows + 2 :, :, 0:chans] = silu_tanh(earlier_edges[:, 2:4])
+    field[frames:, 0:2, :, 0:chans] = silu_tanh(top[...])
+    field[frames:, rows + 2 :, :, 0:chans] = silu_tanh(bottom[...])
     spread_taps(field[...].reshape(2 * frames * (rows + 4) * cols, lanes), cols, rows + 2, buf1)
     totals, bounds = conv_time_taps(buf1, w_first, frames + 2)
     for total, lo, hi in zip(totals, bounds[:-1], bounds[1:]):
@@ -104,7 +107,7 @@
     out[...] = result.astype(jnp.bfloat16).reshape(frames, rows, cols, chans)
 
 
-def block(flags, earlier, own, top, bottom, w_first, b_first, w_second, b_second):
+def block(flags, earlier, own, top, bottom, earlier_edges, w_first, b_first, w_second, b_second):
     frames, rows, cols, chans = own.shape
     lanes = -(-chans // 256) * 256
     w_first = jnp.pad(w_first.reshape(3, 9 * chans, chans), ((0, 0), (0, 0), (0, lanes - chans)))
@@ -116,7 +119,7 @@
     return pl.pallas_call(
         block_kernel,
         out_shape=jax.ShapeDtypeStruct(own.shape, own.dtype),
-        in_specs=[pl.BlockSpec(memory_space=pltpu.SMEM)] + [vmem] * 8,
+        in_specs=[pl.BlockSpec(memory_space=pltpu.SMEM)] + [vmem] * 9,
         out_specs=vmem,
         scratch_shapes=[
             pltpu.VMEM((2 * frames, rows + 4, cols, lanes), jnp.float32),
@@ -130,19 +133,19 @@
             transcendentals=2 * positions * chans,
             bytes_accessed=2 * (54 * lanes * lanes + 4 * own.size),
         ),
-    )(flags, earlier, own, top, bottom, w_first, b_first, w_second, b_second.reshape(1, chans))
+    )(flags, earlier, own, top, bottom, earlier_edges, w_first, b_first, w_second, b_second.reshape(1, chans))
 
 
 def local(clip_frames, w_first, b_first, w_second, b_second):
     rows = clip_frames.shape[1]
     x = clip_frames
     earlier = neighbour(x, "tm", 1)
-    extended = jnp.concatenate([earlier, x], 0)
-    top = neighbour(extended[:, rows - 2 :], "height", 1)
-    bottom = neighbour(extended[:, :2], "height", -1)
+    top = neighbour(x[:, rows - 2 :], "height", 1)
+    bottom = neighbour(x[:, :2], "height", -1)
+    earlier_edges = neighbour(jnp.concatenate([top, bottom], 1), "tm", 1)
     t, h = lax.axis_index("tm"), lax.axis_index("height")
     flags = jnp.stack([t == 0, h == 0, h == lax.axis_size("height") - 1]).astype(jnp.int32)
-    return block(flags, earlier, x, top, bottom, w_first, b_first, w_second, b_second)
+    return block(flags, earlier, x, top, bottom, earlier_edges, w_first, b_first, w_second, b_second)
 
 
 def solution(mesh):

time: 24.9 us -> 27.2 us (1.092)
  the two profiles are of different devices: /device:TPU:10 before, /device:TPU:0 now
where the time goes in v15:
time: 27.2 us; the launch traced here: 27 us
  starting transfers between devices  12.7 us (47%)
  Pallas kernels  6.28 us (23%)
  local copies, waits for them, and re-layouts  4.09 us (15%)
  waiting for transfers between devices  3.65 us (13%)
    ppermute x4, starting transfers between devices, neighbour(): return lax.ppermute(value, axis, pairs)  12.7 us
    pallas_call x1, Pallas kernels, block(): pl.pallas_call(block_kernel, out_shape=jax.ShapeDtypeStruct(own.shape, ow...  6.28 us
    ppermute x4, waiting for transfers between devices, neighbour(): return lax.ppermute(value, axis, pairs)  3.65 us
    pad x1, local copies, waits for them, and re-layouts, block(): jnp.pad(w_first.reshape(3, 9 * chans, chans), ((0, 0), (0, 0), (0, lanes...  2.33 us
    slice x1, local copies, waits for them, and re-layouts, local(): bottom = neighbour(x[:, :2], 'height', -1)  0.88 us
  transfers between devices with their start and end apart: 4, of which 1 were waited for; matrix products, arithmetic and copies ran while one was open for 11% of the time, Pallas kernels for 0%

profile of v15, /device:TPU:0, one launch (start us, length us, event | category | flops | bytes accessed | tf_op | source)
XLA Modules:
  0.0 27.0 jit_solution(1849743722321025391)
XLA Ops:
  0.0 0.9 %fusion = (bf16[4,2,16,192]{3,2,1,0:T(8,128)(2,1)S(1)}, bf16[4,2,16,192]{3,2,1,0:T(8,128)(2,1)S(1)}) fusion(bf16[4,8,16,192]{3,2,1,0:T(8,128)(2,1)} %own.1), kind=kLoop, calls=%fused_computation.2 | loop fusion | bytes 196608 | tf_op jit(solution)/shard_map/slice | solution.py:144
  0.9 1.3 %collective-permute-start.2 = (bf16[4,2,16,192]{3,2,1,0:T(8,128)(2,1)S(1)}, bf16[4,2,16,192]{3,2,1,0:T(8,128)(2,1)S(1)}, u32[]{:S(2)}, u32[]{:S(2)}) collective-permute-start(bf16[4,2,16,192]{3,2,1,0:T(8,128)(2,1)S(1)} %get-tuple-element.5), channel_id=1, source_target_pairs={{1,0},{2,1},{3,2},{5,4},{6,5},{7,6},{9,8},{10,9},{11,10},{13,12},{... | collective-permute-start | bytes 147464 | tf_op jit(solution)/shard_map/ppermute | solution.py:25
  2.2 3.0 %collective-permute-start.1 = (bf16[4,2,16,192]{3,2,1,0:T(8,128)(2,1)S(1)}, bf16[4,2,16,192]{3,2,1,0:T(8,128)(2,1)S(1)}, u32[]{:S(2)}, u32[]{:S(2)}) collective-permute-start(bf16[4,2,16,192]{3,2,1,0:T(8,128)(2,1)S(1)} %get-tuple-element.6), channel_id=1, source_target_pairs={{0,1},{1,2},{2,3},{4,5},{5,6},{6,7},{8,9},{9,10},{10,11},{12,13},{... | collective-permute-start | bytes 147464 | tf_op jit(solution)/shard_map/ppermute | solution.py:25
  5.2 4.9 %collective-permute-start = (bf16[4,8,16,192]{3,2,1,0:T(8,128)(2,1)}, bf16[4,8,16,192]{3,2,1,0:T(8,128)(2,1)S(1)}, u32[]{:S(2)}, u32[]{:S(2)}) collective-permute-start(bf16[4,8,16,192]{3,2,1,0:T(8,128)(2,1)} %own.1), channel_id=1, source_target_pairs={{0,4},{4,8},{8,12},{1,5},{5,9},{9,13},{2,6},{6,10},{10,14},{3,7},{... | collective-permute-start | bytes 589832 | tf_op jit(solution)/shard_map/ppermute | solution.py:25
  10.2 0.0 copy-start.2
  10.2 2.3 %pad.11.w_first = bf16[3,1728,256]{2,1,0:T(8,128)(2,1)S(1)} pad(bf16[3,1728,192]{2,1,0:T(8,128)(2,1)} %bitcast.9, bf16[]{:T(256)} %constant.13.clone.1), padding=0_0x0_0x0_64 | pad | bytes 4644866 | tf_op jit(solution)/shard_map/jit(_pad)/pad | solution.py:113
  12.5 0.2 copy-done.2
  12.7 0.0 copy-start.3
  12.7 0.0 copy-start
  12.7 0.0 copy-start.1
  12.7 0.5 %pad.13.w_second = bf16[3,1728,256]{2,1,0:T(8,128)(2,1)S(1)} pad(bf16[3,1728,192]{2,1,0:T(8,128)(2,1)S(1)} %bitcast.10, bf16[]{:T(256)} %constant.13.clone.1), padding=0_0x0_0x0_64 | pad | bytes 4644866 | tf_op jit(solution)/shard_map/jit(_pad)/pad | solution.py:114
  13.2 0.2 copy-done.3
  13.4 0.0 collective-permute-done.2.bottom
  13.4 0.0 collective-permute-done.1.top
  13.5 3.5 %collective-permute-start.3 = (bf16[4,4,16,192]{3,2,1,0:T(8,128)(2,1)S(1)}, bf16[4,4,16,192]{3,2,1,0:T(8,128)(2,1)S(1)}, u32[]{:S(2)}, u32[]{:S(2)}) collective-permute-start(bf16[4,4,16,192]{3,2,1,0:T(8,128)(2,1)S(1)} %pad_maximum_fusion), channel_id=1, source_target_pairs={{0,4},{4,8},{8,12},{1,5},{5,9},{9,13},{2,6},{6,10},{10,14},{3,7},{... | collective-permute-start | bytes 294920 | tf_op jit(solution)/shard_map/ppermute | solution.py:25
  17.0 0.1 add_convert_fusion.flags
  17.0 3.6 %collective-permute-done.3.earlier_edges = bf16[4,4,16,192]{3,2,1,0:T(8,128)(2,1)S(1)} collective-permute-done((bf16[4,4,16,192]{3,2,1,0:T(8,128)(2,1)S(1)}, bf16[4,4,16,192]{3,2,1,0:T(8,128)(2,1)S(1)}, u32[]{:S(2)}, u32[]{:S(2)}) %collective-permute-start.3) | collective-permute-done | bytes 98336 | tf_op jit(solution)/shard_map/ppermute | solution.py:25
  20.7 0.0 collective-permute-done.earlier
  20.7 0.0 copy-done
  20.7 0.0 copy-done.1
  20.7 6.3 %shard_map.55 = bf16[4,8,16,192]{3,2,1,0:T(8,128)(2,1)} custom-call(s32[3]{0:T(128)S(1)} %add_convert_fusion.flags, bf16[4,8,16,192]{3,2,1,0:T(8,128)(2,1)S(1)} %collective-permute-done.earlier, bf16[4,8,16,192]{3,2,1,0:T(8,128)(2,1)S(1)} %copy-done, bf16[4,2,16,192]{3,2,1,0:T(8,128)(2,1)S(1)} %collective-permute-done.1.top, ...), custom_call_target="tpu_custom_call" | custom-call | flops 2930245632 | bytes 7864320 | tf_op jit(solution)/shard_map/pallas_call | solution.py:119
  (2 shorter events, 0.0 us)
Async XLA Ops:
  0.9 12.5 %collective-permute-start.2 = (bf16[4,2,16,192]{3,2,1,0:T(8,128)(2,1)S(1)}, bf16[4,2,16,192]{3,2,1,0:T(8,128)(2,1)S(1)}, u32[]{:S(2)}, u32[]{:S(2)}) collective-permute-start(bf16[4,2,16,192]{3,2,1,0:T(8,128)(2,1)S(1)} %get-tuple-element.5), channel_id=1, source_target_pairs={{1,0},{2,1},{3,2},{5,4},{6,5},{7,6},{9,8},{10,9},{11,10},{13,12},{... | collective-permute-start | bytes 147464 | tf_op jit(solution)/shard_map/ppermute | solution.py:25
  2.2 11.2 %collective-permute-start.1 = (bf16[4,2,16,192]{3,2,1,0:T(8,128)(2,1)S(1)}, bf16[4,2,16,192]{3,2,1,0:T(8,128)(2,1)S(1)}, u32[]{:S(2)}, u32[]{:S(2)}) collective-permute-start(bf16[4,2,16,192]{3,2,1,0:T(8,128)(2,1)S(1)} %get-tuple-element.6), channel_id=1, source_target_pairs={{0,1},{1,2},{2,3},{4,5},{5,6},{6,7},{8,9},{9,10},{10,11},{12,13},{... | collective-permute-start | bytes 147464 | tf_op jit(solution)/shard_map/ppermute | solution.py:25
  5.2 15.5 %collective-permute-start = (bf16[4,8,16,192]{3,2,1,0:T(8,128)(2,1)}, bf16[4,8,16,192]{3,2,1,0:T(8,128)(2,1)S(1)}, u32[]{:S(2)}, u32[]{:S(2)}) collective-permute-start(bf16[4,8,16,192]{3,2,1,0:T(8,128)(2,1)} %own.1), channel_id=1, source_target_pairs={{0,4},{4,8},{8,12},{1,5},{5,9},{9,13},{2,6},{6,10},{10,14},{3,7},{... | collective-permute-start | bytes 589832 | tf_op jit(solution)/shard_map/ppermute | solution.py:25
  10.2 2.6 %copy-start.2 = (bf16[3,3,3,192,192]{4,3,2,1,0:T(8,128)(2,1)S(1)}, bf16[3,3,3,192,192]{4,3,2,1,0:T(8,128)(2,1)}, u32[]{:S(2)}) copy-start(bf16[3,3,3,192,192]{4,3,2,1,0:T(8,128)(2,1)} %param.8) | copy-start | bytes 5971972
  12.7 0.7 %copy-start.3 = (f32[192]{0:T(256)S(1)}, f32[192]{0:T(256)}, u32[]{:S(2)}) copy-start(f32[192]{0:T(256)} %param.7) | copy-start | bytes 2308
  12.7 7.9 %copy-start = (bf16[4,8,16,192]{3,2,1,0:T(8,128)(2,1)S(1)}, bf16[4,8,16,192]{3,2,1,0:T(8,128)(2,1)}, u32[]{:S(2)}) copy-start(bf16[4,8,16,192]{3,2,1,0:T(8,128)(2,1)} %own.1) | copy-start | bytes 589828
  12.7 7.9 %copy-start.1 = (f32[192]{0:T(256)S(1)}, f32[192]{0:T(256)}, u32[]{:S(2)}) copy-start(f32[192]{0:T(256)} %param.9) | copy-start | bytes 2308
  13.5 7.2 %collective-permute-start.3 = (bf16[4,4,16,192]{3,2,1,0:T(8,128)(2,1)S(1)}, bf16[4,4,16,192]{3,2,1,0:T(8,128)(2,1)S(1)}, u32[]{:S(2)}, u32[]{:S(2)}) collective-permute-start(bf16[4,4,16,192]{3,2,1,0:T(8,128)(2,1)S(1)} %pad_maximum_fusion), channel_id=1, source_target_pairs={{0,4},{4,8},{8,12},{1,5},{5,9},{9,13},{2,6},{6,10},{10,14},{3,7},{... | collective-permute-start | bytes 294920 | tf_op jit(solution)/shard_map/ppermute | solution.py:25
